TPU v7x, 32 devices: a whole 2x2x4 slice. The times are simulated.
32 devices in a mesh: dp: 2 (over x), expert: 4 (over y, core), tensor: 4 (over z).
Axes of the slice: x: 2, y: 2, z: 4, core: 2. Of those that a mesh axis runs over, the one named last changes fastest.
Arguments:
- output_grad: bfloat16 [2048, 4096], P(('dp', 'expert'), 'tensor'), may hold values from -6 to 6
- expert_ids: int32 [2048, 2], P(('dp', 'expert')), may hold values from 0 to 3, all different within a row; in each aligned block of 256 rows (0 to 255, 256 to 511, ...) at most 192 rows name the same one
- router_weights: bfloat16 [2048, 2], P(('dp', 'expert')), may hold values from 0.099609375 to 0.8984375
- gate_preact: bfloat16 [4, 1536, 14336], P('expert', 'dp', 'tensor'), may hold values from -6 to 6
- up_preact: bfloat16 [4, 1536, 14336], P('expert', 'dp', 'tensor'), may hold values from -6 to 6
- down_weight: bfloat16 [4, 14336, 4096], P('expert', 'tensor', 'dp'), may hold values from -0.046875 to 0.046875
Outputs:
- gate_preact_grad: bfloat16 [4, 1536, 14336], P('expert', 'dp', 'tensor')
- up_preact_grad: bfloat16 [4, 1536, 14336], P('expert', 'dp', 'tensor')
- down_grad: bfloat16 [4, 14336, 4096], P('expert', 'tensor', 'dp')
- router_grad: float32 [2048, 2], P(('dp', 'expert'))
Inputs may be any that keep to these rules, and one draw needn't show every extreme that they name: `expert_ids`: the ids of one token differ. Among the 256 rows of one device no expert is named by more than 192 rows, and in every draw some expert is named by exactly 192 rows of some device.
All inputs are finite; a program needn't handle non-finite values.
Results may differ from a plain program's by a relative error of at most 0.007.
Values may be sent and summed in bfloat16 or wider, within the bound.
No kernel may reach another device: no remote copies, remote signals or barrier semaphores. Data moves between devices by JAX's collectives and lax.ppermute only.
A program may use at most 192 MiB of HBM per device.

v0:
```python
import jax
import jax.numpy as jnp
from jax import lax
from jax.sharding import PartitionSpec as P


def silu_parts(values):
    sigma = jax.nn.sigmoid(values)
    return (values * sigma, sigma * (1.0 + values * (1.0 - sigma)))


def local(output_grad, expert_ids, router_weights, gate_preact, up_preact, down_weight):
    expert_count = lax.axis_size("expert")
    tokens_here = expert_ids.shape[0]
    choices_each = expert_ids.shape[1]
    capacity = gate_preact.shape[1] // expert_count
    flat_ids = expert_ids.reshape(-1)
    one_hot = (flat_ids[:, None] == jnp.arange(expert_count, dtype=jnp.int32)).astype(jnp.int32)
    earlier = jnp.cumsum(one_hot, axis=0) - one_hot
    slot_index = jnp.sum(earlier * one_hot, axis=1)
    target = (flat_ids * capacity + slot_index).reshape(tokens_here, choices_each)
    columns = jnp.arange(expert_count * capacity, dtype=jnp.int32)
    matches = [target[:, which][:, None] == columns[None, :] for which in range(choices_each)]
    selector = jnp.zeros((tokens_here, expert_count * capacity), jnp.bfloat16)
    gate_table = jnp.zeros((tokens_here, expert_count * capacity), jnp.float32)
    for which in range(choices_each):
        selector = jnp.where(matches[which], jnp.bfloat16(1.0), selector)
        gate_table = jnp.where(
            matches[which], router_weights[:, which : which + 1].astype(jnp.float32), gate_table
        )
    gate_send = jnp.sum(gate_table, axis=0).astype(jnp.bfloat16).reshape(expert_count, capacity)
    local_weight = down_weight[0]
    gate_float = gate_preact[0].astype(jnp.float32)
    up_float = up_preact[0].astype(jnp.float32)
    active, slope = silu_parts(gate_float)
    hidden = (active * up_float).astype(jnp.bfloat16)
    contract_rows = (((0,), (0,)), ((), ()))
    contract_cols = (((1,), (1,)), ((), ()))
    whole_weight = lax.all_gather(local_weight, "dp", axis=1, tiled=True)
    outgoing = lax.dot_general(
        selector, output_grad, contract_rows, preferred_element_type=jnp.float32
    )
    outgoing = outgoing.astype(jnp.bfloat16).reshape(expert_count, capacity, -1)
    received, gate_slots = (
        lax.all_to_all(outgoing, "expert", split_axis=0, concat_axis=0, tiled=True),
        lax.all_to_all(gate_send, "expert", split_axis=0, concat_axis=0, tiled=True),
    )
    narrow_rows = received.reshape(expert_count * capacity, -1)
    gate_column = gate_slots.reshape(-1).astype(jnp.float32)[:, None]
    fragment = lax.all_gather(narrow_rows, "tensor", axis=1, tiled=True)
    upstream_sum = lax.dot_general(
        fragment, whole_weight, contract_cols, preferred_element_type=jnp.float32
    )
    scaled = (gate_column * fragment.astype(jnp.float32)).astype(jnp.bfloat16)
    grad_part = lax.dot_general(hidden, scaled, contract_rows, preferred_element_type=jnp.float32)
    grad_weight = grad_part
    upstream, grad_weight = (upstream_sum, grad_weight)
    rounded = lax.optimization_barrier(grad_weight.astype(jnp.bfloat16)).astype(jnp.float32)
    down_grad = lax.psum_scatter(
        rounded.astype(jnp.bfloat16), "dp", scatter_dimension=1, tiled=True
    )
    score = jnp.sum(hidden.astype(jnp.float32) * upstream, axis=1)
    hidden_grad = gate_column * upstream
    gate_grad = (hidden_grad * up_float * slope).astype(jnp.bfloat16)
    up_grad = (hidden_grad * active).astype(jnp.bfloat16)
    summed_scores = lax.psum(score, "tensor")
    returned = lax.all_to_all(
        summed_scores.reshape(expert_count, capacity),
        "expert",
        split_axis=0,
        concat_axis=0,
        tiled=True,
    )
    flat_scores = returned.reshape(-1)
    router_grad = jnp.stack(
        [
            jnp.sum(jnp.where(matches[which], flat_scores[None, :], 0.0), axis=1)
            for which in range(choices_each)
        ],
        axis=1,
    )
    return (gate_grad[None], up_grad[None], down_grad[None], router_grad)


def solution(mesh):
    placed = (
        P(("dp", "expert"), "tensor"),
        P(("dp", "expert"), None),
        P(("dp", "expert"), None),
        P("expert", "dp", "tensor"),
        P("expert", "dp", "tensor"),
        P("expert", "tensor", "dp"),
    )
    return jax.shard_map(
        local,
        mesh=mesh,
        in_specs=placed,
        out_specs=(
            P("expert", "dp", "tensor"),
            P("expert", "dp", "tensor"),
            P("expert", "tensor", "dp"),
            P(("dp", "expert"), None),
        ),
        check_vma=False,
    )
```

profile of v0, /device:TPU:0, one launch (start us, length us, event | category | flops | bytes accessed | tf_op | source)
XLA Modules:
  0.0 914.7 jit_solution(14753980404124492061)
XLA Ops:
  7.2 0.0 copy-start
  7.2 0.0 all-gather.4.cloned.1.call-start
  7.2 0.9 copy.28
  8.1 0.1 eq.59
  8.2 0.1 eq.55
  8.4 1.2 reduce-window.6
  9.6 0.2 slice_reduce_fusion
  9.8 0.2 reduce-window.9
  10.0 0.1 add_bitcast_fusion
  10.1 0.1 reduce_sum.48
  10.3 0.1 copy.30
  10.3 0.7 multiply_add_fusion
  11.1 0.0 copy-done
  11.1 0.8 convolution_convert_fusion.1
  11.8 24.2 %all_to_all.20 = bf16[4,192,1024]{2,1,0:T(8,128)(2,1)} all-to-all(bf16[4,192,1024]{2,1,0:T(8,128)(2,1)S(1)} %bitcast.62), channel_id=1, replica_groups=mesh['dp'=2,'expert'=4,'tensor'=4] {'expert'}, dimensions={0} | all-to-all | bytes 3145728 | tf_op jit(solution)/shard_map/all_to_all | solution.py:45
  36.0 0.0 all-gather.4.cloned.1.call-update
  36.1 0.0 all-gather.6.cloned.1.call-start
  36.1 0.7 all-gather.6.cloned.1.call-update
  36.8 0.0 copy-start.2
  36.8 115.6 %all-gather.4.cloned.1.call-done = bf16[768,4096]{1,0:T(8,128)(2,1)} async-done(((bf16[768,1024]{1,0:T(8,128)(2,1)}), bf16[768,4096]{1,0:T(8,128)(2,1)}) %all-gather.4.cloned.1.call-update) | async-done | bytes 6291472 | tf_op jit(solution)/shard_map/all_gather | solution.py:50
  152.4 342.0 %all-gather.6.cloned.1.call-done = bf16[1,3584,4096]{2,1,0:T(8,128)(2,1)} async-done(((bf16[1,3584,2048]{2,1,0:T(8,128)(2,1)}), bf16[1,3584,4096]{2,1,0:T(8,128)(2,1)}) %all-gather.6.cloned.1.call-update) | async-done | bytes 29360144 | tf_op jit(solution)/shard_map/all_gather | solution.py:39
  494.4 34.1 %multiply_reduce_fusion = (f32[768]{0:T(1024)S(1)}, f32[768,3584]{1,0:T(8,128)}) fusion(bf16[1,768,3584]{2,1,0:T(8,128)(2,1)} %param.10, bf16[1,768,3584]{2,1,0:T(8,128)(2,1)} %param.9, bf16[768,4096]{1,0:T(8,128)(2,1)} %all-gather.4.cloned.1.call-done, bf16[1,3584,4096]{2,1,0:T(8,128)(2,1)} %all-gather.6.cloned.1.call-done), kind=kOutput, calls=%fused_computation.17 | convolution fusion | flops 22578855936 | bytes 57674752 | tf_op jit(solution)/shard_map/dot_general | solution.py:51
  528.4 0.1 all_to_all.15
  528.5 12.3 %psum.7 = f32[4,1,192]{2,1,0:T(1,128)} all-reduce(f32[4,1,192]{2,1,0:T(1,128)S(1)} %all_to_all.15), channel_id=1, replica_groups=mesh['dp'=2,'expert'=4,'tensor'=4] {'tensor'}, use_global_device_ids=true, to_apply=%region_6.7 | all-reduce | flops 768 | bytes 6144 | tf_op jit(solution)/shard_map/psum | solution.py:66
  540.8 3.2 all-to-all-start.2
  544.0 0.0 reduce-scatter.2.cloned.1.call-start
  544.1 0.0 copy-done.2
  544.1 3.7 all-to-all-done.2
  547.8 0.1 broadcast_in_dim.75
  547.9 0.5 select_reduce_fusion.1
  548.4 0.1 convert_element_type.92
  548.5 6.1 all_to_all.21
  554.6 0.1 reshape.73
  554.7 32.6 %convolution_convert_fusion = bf16[3584,4096]{1,0:T(8,128)(2,1)} fusion(bf16[768,4096]{1,0:T(8,128)(2,1)} %all-gather.4.cloned.1.call-done, f32[768]{0:T(1024)S(1)} %reshape.73, bf16[1,768,3584]{2,1,0:T(8,128)(2,1)} %param.10, bf16[1,768,3584]{2,1,0:T(8,128)(2,1)} %param.9), kind=kOutput, calls=%fused_computation | convolution fusion | flops 22594715648 | bytes 46664704 | tf_op jit(solution)/shard_map/dot_general | solution.py:55
  587.3 0.0 reduce-scatter.2.cloned.1.call-update
  587.3 0.6 pad_maximum_fusion
  587.9 0.0 copy-start.1
  587.9 15.9 %fusion.11 = (bf16[1,768,3584]{2,1,0:T(8,128)(2,1)}, bf16[1,768,3584]{2,1,0:T(8,128)(2,1)}) fusion(f32[768,3584]{1,0:T(8,128)} %get-tuple-element.14, f32[768]{0:T(1024)S(1)} %reshape.73, bf16[1,768,3584]{2,1,0:T(8,128)(2,1)} %param.9, bf16[1,768,3584]{2,1,0:T(8,128)(2,1)} %param.10), kind=kLoop, calls=%fused_computation.20 | loop fusion | flops 44040192 | bytes 33033216 | tf_op jit(solution)/shard_map/broadcast_in_dim | solution.py:82
  603.8 304.3 %reduce-scatter.2.cloned.1.call-done = bf16[3584,2048]{1,0:T(8,128)(2,1)} async-done(((bf16[3584,4096]{1,0:T(8,128)(2,1)}), bf16[3584,2048]{1,0:T(8,128)(2,1)}) %reduce-scatter.2.cloned.1.call-update) | async-done | bytes 14680080 | tf_op jit(solution)/shard_map/reduce_scatter | solution.py:59
  908.2 0.0 copy-done.1
  (6 shorter events, 0.1 us)
Async XLA Ops:
  7.2 3.9 copy-start
  7.2 145.2 %all-gather.4.cloned.1.call-start = ((), (), s32[]{:S(2)}) async-start(), calls=%async_computation.4 | async-start | bytes 7864320 | tf_op jit(solution)/shard_map/all_gather | solution.py:50
  36.1 458.3 %all-gather.6.cloned.1.call-start = ((), (), s32[]{:S(2)}) async-start(), calls=%async_computation.6 | async-start | bytes 44040192 | tf_op jit(solution)/shard_map/all_gather | solution.py:39
  36.8 507.3 %copy-start.2 = (bf16[256,2]{0,1:T(2,128)(2,1)S(1)}, bf16[256,2]{0,1:T(2,128)(2,1)}, u32[]{:S(2)}) copy-start(bf16[256,2]{0,1:T(2,128)(2,1)} %param.8) | copy-start | bytes 3076
  540.8 7.0 all-to-all-start.2
  544.0 364.1 %reduce-scatter.2.cloned.1.call-start = ((), (), s32[]{:S(2)}) async-start(), calls=%async_computation.5 | async-start | bytes 44040192 | tf_op jit(solution)/shard_map/reduce_scatter | solution.py:59
  587.9 320.3 %copy-start.1 = (bf16[256,1024]{1,0:T(8,128)(2,1)S(1)}, bf16[256,1024]{1,0:T(8,128)(2,1)}, u32[]{:S(2)}) copy-start(bf16[256,1024]{1,0:T(8,128)(2,1)} %param.6) | copy-start | bytes 1572868
Sparse Core Ops, SparseCore 0:
  36.2 116.1 all-gather.3
  153.9 340.3 all-gather.5
  587.4 320.6 reduce-scatter.1
where the time goes:
time: 915 us
  waiting for transfers between devices  766 us (84%)
  matrix products  67.4 us (7%)
  blocking collectives  42.6 us (5%)
  other arithmetic  19.3 us (2%)
  between operations  13.8 us (2%)
    all_gather x1, waiting for transfers between devices, local(): whole_weight = lax.all_gather(local_weight, 'dp', axis=1, tiled=True)  342 us
    reduce_scatter x1, waiting for transfers between devices, local(): lax.psum_scatter(rounded.astype(jnp.bfloat16), 'dp', scatter_dimension=1,...  304 us
    all_gather x1, waiting for transfers between devices, local(): fragment = lax.all_gather(narrow_rows, 'tensor', axis=1, tiled=True)  116 us
    dot_general x1, matrix products, local(): lax.dot_general(fragment, whole_weight, contract_cols, preferred_element_...  34.1 us
    dot_general x1, matrix products, local(): lax.dot_general(hidden, scaled, contract_rows, preferred_element_type=jnp...  32.6 us
    all_to_all x1, blocking collectives, local(): lax.all_to_all(outgoing, 'expert', split_axis=0, concat_axis=0, tiled=True)  24.2 us
  transfers between devices with their start and end apart: 4, of which 4 were waited for; matrix products, arithmetic and copies ran while one was open for 2% of the time, Pallas kernels for 0%

commit v1 on v0

--- a/solution.py
+++ b/solution.py
@@ -2,6 +2,8 @@
 import jax.numpy as jnp
 from jax import lax
 from jax.sharding import PartitionSpec as P
+
+PARTIAL_DTYPE = jnp.float32
 
 
 def silu_parts(values):
@@ -9,8 +11,15 @@
     return (values * sigma, sigma * (1.0 + values * (1.0 - sigma)))
 
 
+def swap_dp(value):
+    return lax.ppermute(value, "dp", perm=[(0, 1), (1, 0)])
+
+
 def local(output_grad, expert_ids, router_weights, gate_preact, up_preact, down_weight):
     expert_count = lax.axis_size("expert")
+    tensor_count = lax.axis_size("tensor")
+    replica = lax.axis_index("dp")
+    part = lax.axis_index("tensor")
     tokens_here = expert_ids.shape[0]
     choices_each = expert_ids.shape[1]
     capacity = gate_preact.shape[1] // expert_count
@@ -29,36 +38,65 @@
             matches[which], router_weights[:, which : which + 1].astype(jnp.float32), gate_table
         )
     gate_send = jnp.sum(gate_table, axis=0).astype(jnp.bfloat16).reshape(expert_count, capacity)
-    local_weight = down_weight[0]
+
     gate_float = gate_preact[0].astype(jnp.float32)
     up_float = up_preact[0].astype(jnp.float32)
     active, slope = silu_parts(gate_float)
     hidden = (active * up_float).astype(jnp.bfloat16)
+
     contract_rows = (((0,), (0,)), ((), ()))
     contract_cols = (((1,), (1,)), ((), ()))
-    whole_weight = lax.all_gather(local_weight, "dp", axis=1, tiled=True)
     outgoing = lax.dot_general(
         selector, output_grad, contract_rows, preferred_element_type=jnp.float32
     )
     outgoing = outgoing.astype(jnp.bfloat16).reshape(expert_count, capacity, -1)
-    received, gate_slots = (
-        lax.all_to_all(outgoing, "expert", split_axis=0, concat_axis=0, tiled=True),
-        lax.all_to_all(gate_send, "expert", split_axis=0, concat_axis=0, tiled=True),
+    hidden, outgoing = lax.optimization_barrier((hidden, outgoing))
+    hidden_other = swap_dp(hidden)
+    received = lax.all_to_all(outgoing, "expert", split_axis=0, concat_axis=0, tiled=True)
+    gate_slots = lax.all_to_all(gate_send, "expert", split_axis=0, concat_axis=0, tiled=True)
+    slots = expert_count * capacity
+    narrow_rows = received.reshape(slots, -1)
+    gate_bf16 = gate_slots.reshape(-1)
+    gate_column = gate_bf16.astype(jnp.float32)[:, None]
+    fragment = lax.all_gather(narrow_rows, "tensor", axis=1, tiled=True)
+
+    width = fragment.shape[1]
+    half = width // 2
+    piece = half // tensor_count
+    own_rows = lax.dynamic_slice_in_dim(fragment, replica * half, half, axis=1)
+    send_rows = lax.dynamic_slice_in_dim(
+        fragment, (1 - replica) * half + part * piece, piece, axis=1
     )
-    narrow_rows = received.reshape(expert_count * capacity, -1)
-    gate_column = gate_slots.reshape(-1).astype(jnp.float32)[:, None]
-    fragment = lax.all_gather(narrow_rows, "tensor", axis=1, tiled=True)
-    upstream_sum = lax.dot_general(
-        fragment, whole_weight, contract_cols, preferred_element_type=jnp.float32
+    other_piece = swap_dp(send_rows)
+    other_rows = lax.all_gather(other_piece, "tensor", axis=1, tiled=True)
+    hidden_other, other_rows = lax.optimization_barrier((hidden_other, other_rows))
+    other_gates = swap_dp(gate_bf16).astype(jnp.float32)[:, None]
+
+    local_weight = down_weight[0]
+    partial_other = lax.dot_general(
+        other_rows, local_weight, contract_cols, preferred_element_type=jnp.float32
     )
-    scaled = (gate_column * fragment.astype(jnp.float32)).astype(jnp.bfloat16)
-    grad_part = lax.dot_general(hidden, scaled, contract_rows, preferred_element_type=jnp.float32)
-    grad_weight = grad_part
-    upstream, grad_weight = (upstream_sum, grad_weight)
-    rounded = lax.optimization_barrier(grad_weight.astype(jnp.bfloat16)).astype(jnp.float32)
-    down_grad = lax.psum_scatter(
-        rounded.astype(jnp.bfloat16), "dp", scatter_dimension=1, tiled=True
+    partial_back = swap_dp(partial_other.astype(PARTIAL_DTYPE)).astype(jnp.float32)
+    partial_own = lax.dot_general(
+        own_rows, local_weight, contract_cols, preferred_element_type=jnp.float32
     )
+
+    scaled_own = (gate_column * own_rows.astype(jnp.float32)).astype(jnp.bfloat16)
+    scaled_other = (other_gates * other_rows.astype(jnp.float32)).astype(jnp.bfloat16)
+    grad_own = lax.dot_general(hidden, scaled_own, contract_rows, preferred_element_type=jnp.float32)
+    grad_other = lax.dot_general(
+        hidden_other, scaled_other, contract_rows, preferred_element_type=jnp.float32
+    )
+    rounded_own = lax.optimization_barrier(grad_own.astype(jnp.bfloat16))
+    rounded_other = lax.optimization_barrier(grad_other.astype(jnp.bfloat16))
+    partial_back, rounded_own, rounded_other = lax.optimization_barrier(
+        (partial_back, rounded_own, rounded_other)
+    )
+    upstream = partial_own + partial_back
+    down_grad = (rounded_own.astype(jnp.float32) + rounded_other.astype(jnp.float32)).astype(
+        jnp.bfloat16
+    )
+
     score = jnp.sum(hidden.astype(jnp.float32) * upstream, axis=1)
     hidden_grad = gate_column * upstream
     gate_grad = (hidden_grad * up_float * slope).astype(jnp.bfloat16)

time: 915 us -> 617 us (0.67)
  waiting for transfers between devices: 766 us -> 427 us
  other arithmetic: 19.3 us -> 48.8 us
    reduce_scatter x1 -> x0, waiting for transfers between devices: 304 us -> none  [local(): lax.psum_scatter(rounded.astype(jnp.bfloat16), 'dp', scatter_dimension=1,...]
    all_gather x1, waiting for transfers between devices: 342 us -> 64.4 us  [local(): other_rows = lax.all_gather(other_piece, 'tensor', axis=1, tiled=True)]
    ppermute x0 -> x4, waiting for transfers between devices: none -> 248 us  [swap_dp(): return lax.ppermute(value, 'dp', perm=[(0, 1), (1, 0)])]
    broadcast_in_dim x1 -> x2, other arithmetic: 15.9 us -> 36.5 us  [local(): return (gate_grad[None], up_grad[None], down_grad[None], router_grad)]
    dot_general x2 -> x4, matrix products: 66.7 us -> 72.6 us  [the longest x1 18.3 us: local(): lax.dot_general(own_rows, local_weight, contract_cols, preferred_element_...]
  transfers between devices with their start and end apart: 4 -> 7, of which waited for: 4 -> 4; matrix products, arithmetic and copies ran while one was open for 2% -> 12% of each run, Pallas kernels for 0% -> 0%
where the time goes in v1:
time: 617 us
  waiting for transfers between devices  427 us (69%)
  matrix products  73.4 us (12%)
  other arithmetic  48.8 us (8%)
  blocking collectives  40.5 us (7%)
  between operations  14.2 us (2%)
  starting transfers between devices  8.9 us (1%)
    ppermute x4, waiting for transfers between devices, swap_dp(): return lax.ppermute(value, 'dp', perm=[(0, 1), (1, 0)])  248 us
    all_gather x1, waiting for transfers between devices, local(): fragment = lax.all_gather(narrow_rows, 'tensor', axis=1, tiled=True)  114 us
    all_gather x1, waiting for transfers between devices, local(): other_rows = lax.all_gather(other_piece, 'tensor', axis=1, tiled=True)  64.4 us
    broadcast_in_dim x2, other arithmetic, local(): return (gate_grad[None], up_grad[None], down_grad[None], router_grad)  36.5 us
    all_to_all x1, blocking collectives, local(): lax.all_to_all(outgoing, 'expert', split_axis=0, concat_axis=0, tiled=True)  24.2 us
    dot_general x1, matrix products, local(): lax.dot_general(own_rows, local_weight, contract_cols, preferred_element_...  18.3 us
    dot_general x1, matrix products, local(): lax.dot_general(hidden, scaled_own, contract_rows, preferred_element_type...  18.3 us
    dot_general x1, matrix products, local(): lax.dot_general(other_rows, local_weight, contract_cols, preferred_elemen...  18.2 us
  transfers between devices with their start and end apart: 7, of which 4 were waited for; matrix products, arithmetic and copies ran while one was open for 12% of the time, Pallas kernels for 0%

profile of v1, /device:TPU:0, one launch (start us, length us, event | category | flops | bytes accessed | tf_op | source)
XLA Modules:
  0.0 616.6 jit_solution(12437453717802722302)
XLA Ops:
  7.2 0.0 copy-start
  7.2 0.0 all-gather.3.cloned.1.call-start
  7.2 0.9 copy.28
  8.1 0.1 eq.59
  8.2 0.1 eq.55
  8.4 1.2 reduce-window.6
  9.6 0.2 slice_reduce_fusion
  9.8 0.2 reduce-window.9
  10.0 0.1 add_bitcast_fusion
  10.1 0.1 reduce_sum.48
  10.3 0.1 copy.30
  10.3 0.7 multiply_add_fusion
  11.1 8.8 %fusion.5 = bf16[768,3584]{1,0:T(8,128)(2,1)} fusion(bf16[1,768,3584]{2,1,0:T(8,128)(2,1)} %param.10, bf16[1,768,3584]{2,1,0:T(8,128)(2,1)} %param.9), kind=kLoop, calls=%fused_computation.13 | loop fusion | flops 22020096 | bytes 16515072 | tf_op jit(solution)/shard_map/convert_element_type | solution.py:45
  19.9 0.0 copy-done
  19.9 0.8 convolution_convert_fusion.2
  20.7 24.2 %all_to_all.20 = bf16[4,192,1024]{2,1,0:T(8,128)(2,1)} all-to-all(bf16[4,192,1024]{2,1,0:T(8,128)(2,1)S(1)} %bitcast.61), channel_id=1, replica_groups=mesh['dp'=2,'expert'=4,'tensor'=4] {'expert'}, dimensions={0} | all-to-all | bytes 3145728 | tf_op jit(solution)/shard_map/all_to_all | solution.py:55
  44.9 0.0 all-gather.3.cloned.1.call-update
  44.9 0.0 all-gather.5.cloned.1.call-start
  45.0 2.0 collective-permute-start
  47.0 114.2 %all-gather.3.cloned.1.call-done = bf16[768,4096]{1,0:T(8,128)(2,1)} async-done(((bf16[768,1024]{1,0:T(8,128)(2,1)}), bf16[768,4096]{1,0:T(8,128)(2,1)}) %all-gather.3.cloned.1.call-update) | async-done | bytes 6291472 | tf_op jit(solution)/shard_map/all_gather | solution.py:61
  161.2 1.2 constant_dynamic-slice_fusion
  162.4 1.5 collective-permute-start.1
  163.9 18.4 %collective-permute-done.1 = bf16[768,512]{1,0:T(8,128)(2,1)S(1)} collective-permute-done((bf16[768,512]{1,0:T(8,128)(2,1)S(1)}, bf16[768,512]{1,0:T(8,128)(2,1)S(1)}, u32[]{:S(2)}, u32[]{:S(2)}) %collective-permute-start.1) | collective-permute-done | bytes 786464 | tf_op jit(solution)/shard_map/ppermute | solution.py:15
  182.4 0.0 copy-start.2
  182.4 0.9 copy-done.2
  183.2 0.0 all-gather.5.cloned.1.call-update
  183.3 0.0 copy-start.3
  183.3 0.0 collective-permute-done
  183.3 64.4 %all-gather.5.cloned.1.call-done = bf16[768,2048]{1,0:T(8,128)(2,1)} async-done(((bf16[768,512]{1,0:T(8,128)(2,1)}), bf16[768,2048]{1,0:T(8,128)(2,1)}) %all-gather.5.cloned.1.call-update) | async-done | bytes 3145744 | tf_op jit(solution)/shard_map/all_gather | solution.py:71
  247.7 18.2 %fusion.1 = f32[768,3584]{1,0:T(8,128)} fusion(bf16[768,2048]{1,0:T(8,128)(2,1)} %all-gather.5.cloned.1.call-done, bf16[1,3584,2048]{2,1,0:T(8,128)(2,1)} %param.11), kind=kOutput, calls=%fused_computation.7 | convolution fusion | flops 11274289152 | bytes 28835840 | tf_op jit(solution)/shard_map/dot_general | solution.py:76
  265.8 1.5 collective-permute-start.2
  267.3 0.0 copy-done.3
  267.3 0.2 select_reduce_fusion.2
  267.5 0.1 convert_element_type.113
  267.6 6.3 %all_to_all.21 = bf16[4,1,192]{2,1,0:T(2,128)(2,1)S(1)} all-to-all(bf16[4,1,192]{2,1,0:T(2,128)(2,1)S(1)} %convert_element_type.113), channel_id=1, replica_groups=mesh['dp'=2,'expert'=4,'tensor'=4] {'expert'}, dimensions={0} | all-to-all | bytes 3072 | tf_op jit(solution)/shard_map/all_to_all | solution.py:56
  274.0 0.1 reshape.71
  274.0 0.6 collective-permute-start.3
  274.6 229.9 %collective-permute-done.3 = bf16[768]{0:T(1024)(128)(2,1)S(1)} collective-permute-done((bf16[768]{0:T(1024)(128)(2,1)S(1)}, bf16[768]{0:T(1024)(128)(2,1)S(1)}, u32[]{:S(2)}, u32[]{:S(2)}) %collective-permute-start.3) | collective-permute-done | bytes 1568 | tf_op jit(solution)/shard_map/ppermute | solution.py:15
  504.5 0.0 slice-start
  504.5 18.3 %convolution_convert_fusion.1 = bf16[3584,2048]{1,0:T(8,128)(2,1)} fusion(bf16[768,3584]{1,0:T(8,128)(2,1)} %fusion.5, f32[768]{0:T(1024)S(1)} %convert_element_type.91, bf16[768,4096]{1,0:T(8,128)(2,1)} %all-gather.3.cloned.1.call-done, s32[]{:T(128)S(6)} %select_n.31), kind=kOutput, calls=%fused_computation.5 | convolution fusion | flops 11286347776 | bytes 23333892 | tf_op jit(solution)/shard_map/dot_general | solution.py:86
  522.8 0.0 slice-start.1
  522.8 18.3 %fusion.3 = f32[768,3584]{1,0:T(8,128)} fusion(bf16[1,3584,2048]{2,1,0:T(8,128)(2,1)} %param.11, bf16[768,4096]{1,0:T(8,128)(2,1)} %all-gather.3.cloned.1.call-done, s32[]{:T(128)S(6)} %select_n.31), kind=kOutput, calls=%fused_computation.9 | convolution fusion | flops 11274289152 | bytes 28835844 | tf_op jit(solution)/shard_map/dot_general | solution.py:80
  541.1 17.9 %convolution_convert_fusion = bf16[3584,2048]{1,0:T(8,128)(2,1)} fusion(bf16[768,3584]{1,0:T(8,128)(2,1)} %collective-permute-done, bf16[768,2048]{1,0:T(8,128)(2,1)} %all-gather.5.cloned.1.call-done, f32[768]{0:T(1024)S(1)} %convert_element_type.101), kind=kOutput, calls=%fused_computation.4 | convolution fusion | flops 11286347776 | bytes 23333888 | tf_op jit(solution)/shard_map/dot_general | solution.py:87
  559.0 0.0 collective-permute-done.2
  559.0 0.0 slice-done
  559.0 0.0 slice-done.1
  559.0 17.8 %fusion.13 = (bf16[1,768,3584]{2,1,0:T(8,128)(2,1)}, bf16[1,768,3584]{2,1,0:T(8,128)(2,1)}, f32[768]{0:T(1024)S(1)}) fusion(f32[768]{0:T(1024)S(1)} %convert_element_type.91, bf16[1,768,3584]{2,1,0:T(8,128)(2,1)S(1)} %bitcast.59, f32[768,3584]{1,0:T(8,128)} %fusion.3, f32[768,3584]{1,0:T(8,128)} %collective-permute-done.2, bf16[1,768,3584]{2,1,0:T(8,128)(2,1)} %param.10, ...), kind=kLoop, calls=%fused_computation.25 | loop fusion | flops 55049472 | bytes 49551360 | tf_op jit(solution)/shard_map/broadcast_in_dim | solution.py:120
  576.8 0.1 all_to_all.15
  576.9 9.9 %psum.7 = f32[4,1,192]{2,1,0:T(1,128)} all-reduce(f32[4,1,192]{2,1,0:T(1,128)S(1)} %all_to_all.15), channel_id=1, replica_groups=mesh['dp'=2,'expert'=4,'tensor'=4] {'tensor'}, use_global_device_ids=true, to_apply=%region_5.6 | all-reduce | flops 768 | bytes 6144 | tf_op jit(solution)/shard_map/psum | solution.py:104
  586.8 3.2 all-to-all-start.2
  590.0 0.0 copy-start.1
  590.1 18.7 %fusion = bf16[1,3584,2048]{2,1,0:T(8,128)(2,1)} fusion(bf16[3584,2048]{1,0:T(8,128)(2,1)} %convolution_convert_fusion, bf16[3584,2048]{1,0:T(8,128)(2,1)} %convolution_convert_fusion.1), kind=kLoop, calls=%fused_computation.6 | loop fusion | flops 29360128 | bytes 44040192 | tf_op jit(solution)/shard_map/broadcast_in_dim | solution.py:120
  608.7 0.0 all-to-all-done.2
  608.8 0.1 broadcast_in_dim.76
  608.8 0.3 select_reduce_fusion.1
  609.2 0.6 pad_maximum_fusion
  609.8 0.0 copy-done.1
  (9 shorter events, 0.1 us)
Async XLA Ops:
  7.2 12.7 %copy-start = (bf16[256,1024]{1,0:T(8,128)(2,1)S(1)}, bf16[256,1024]{1,0:T(8,128)(2,1)}, u32[]{:S(2)}) copy-start(bf16[256,1024]{1,0:T(8,128)(2,1)} %param.6) | copy-start | bytes 1572868
  7.2 154.0 %all-gather.3.cloned.1.call-start = ((), (), s32[]{:S(2)}) async-start(), calls=%async_computation.3 | async-start | bytes 7864320 | tf_op jit(solution)/shard_map/all_gather | solution.py:61
  44.9 202.7 %all-gather.5.cloned.1.call-start = ((), (), s32[]{:S(2)}) async-start(), calls=%async_computation.4 | async-start | bytes 3932160 | tf_op jit(solution)/shard_map/all_gather | solution.py:71
  45.0 138.3 %collective-permute-start = (bf16[768,3584]{1,0:T(8,128)(2,1)}, bf16[768,3584]{1,0:T(8,128)(2,1)}, u32[]{:S(2)}, u32[]{:S(2)}) collective-permute-start(bf16[768,3584]{1,0:T(8,128)(2,1)} %fusion.5), channel_id=1, source_target_pairs={{0,16},{16,0},{1,17},{17,1},{2,18},{18,2},{3,19},{19,3},{4,20},{20... | collective-permute-start | bytes 16515080 | tf_op jit(solution)/shard_map/ppermute | solution.py:15
  162.4 20.0 %collective-permute-start.1 = (bf16[768,512]{1,0:T(8,128)(2,1)S(1)}, bf16[768,512]{1,0:T(8,128)(2,1)S(1)}, u32[]{:S(2)}, u32[]{:S(2)}) collective-permute-start(bf16[768,512]{1,0:T(8,128)(2,1)S(1)} %constant_dynamic-slice_fusion), channel_id=1, source_target_pairs={{0,16},{16,0},{1,17},{17,1},{2,18},{18,2},{3,19},{19,3},{4,20},{20... | collective-permute-start | bytes 2359304 | tf_op jit(solution)/shard_map/ppermute | solution.py:15
  182.4 0.9 copy-start.2
  183.3 84.0 %copy-start.3 = (bf16[256,2]{0,1:T(2,128)(2,1)S(1)}, bf16[256,2]{0,1:T(2,128)(2,1)}, u32[]{:S(2)}) copy-start(bf16[256,2]{0,1:T(2,128)(2,1)} %param.8) | copy-start | bytes 3076
  265.8 293.1 %collective-permute-start.2 = (f32[768,3584]{1,0:T(8,128)}, f32[768,3584]{1,0:T(8,128)}, u32[]{:S(2)}, u32[]{:S(2)}) collective-permute-start(f32[768,3584]{1,0:T(8,128)} %fusion.1), channel_id=1, source_target_pairs={{0,16},{16,0},{1,17},{17,1},{2,18},{18,2},{3,19},{19,3},{4,20},{20... | collective-permute-start | bytes 33030152 | tf_op jit(solution)/shard_map/ppermute | solution.py:15
  274.0 230.5 %collective-permute-start.3 = (bf16[768]{0:T(1024)(128)(2,1)S(1)}, bf16[768]{0:T(1024)(128)(2,1)S(1)}, u32[]{:S(2)}, u32[]{:S(2)}) collective-permute-start(bf16[768]{0:T(1024)(128)(2,1)S(1)} %reshape.71), channel_id=1, source_target_pairs={{0,16},{16,0},{1,17},{17,1},{2,18},{18,2},{3,19},{19,3},{4,20},{20... | collective-permute-start | bytes 4616 | tf_op jit(solution)/shard_map/ppermute | solution.py:15
  504.5 54.4 %slice-start = ((s8[5505024]{0:T(1024)(128)(4,1)}), s8[4194304]{0:T(1024)(128)(4,1)S(1)}, s32[]{:S(2)}) async-start(s8[5505024]{0:T(1024)(128)(4,1)} %bitcast.58), calls=%async_computation.5 | async-start | bytes 8388608
  522.8 36.2 %slice-start.1 = ((s8[5505024]{0:T(1024)(128)(4,1)}), s8[1310720]{0:T(1024)(128)(4,1)S(1)}, s32[]{:S(2)}) async-start(s8[5505024]{0:T(1024)(128)(4,1)} %bitcast.58), calls=%async_computation.6 | async-start | bytes 2621440
  586.8 21.9 %all-to-all-start.2 = ((f32[4,1,192]{2,1,0:T(1,128)}), f32[4,1,192]{2,1,0:T(1,128)S(1)}, u32[]{:S(2)}, u32[]{:S(2)}) async-start(f32[4,1,192]{2,1,0:T(1,128)} %psum.7), calls=%async_computation.2 | async-start | bytes 8192 | tf_op jit(solution)/shard_map/all_to_all | solution.py:105
  590.0 19.7 %copy-start.1 = (bf16[256,1024]{1,0:T(8,128)(2,1)S(1)}, bf16[256,1024]{1,0:T(8,128)(2,1)}, u32[]{:S(2)}) copy-start(bf16[256,1024]{1,0:T(8,128)(2,1)} %param.6) | copy-start | bytes 1572868
Sparse Core Ops, SparseCore 0:
  45.0 116.1 all-gather.2
  183.4 64.2 all-gather.4

commit v2 on v1

--- a/solution.py
+++ b/solution.py
@@ -3,7 +3,7 @@
 from jax import lax
 from jax.sharding import PartitionSpec as P
 
-PARTIAL_DTYPE = jnp.float32
+PARTIAL_DTYPE = jnp.bfloat16
 
 
 def silu_parts(values):
@@ -50,14 +50,15 @@
         selector, output_grad, contract_rows, preferred_element_type=jnp.float32
     )
     outgoing = outgoing.astype(jnp.bfloat16).reshape(expert_count, capacity, -1)
-    hidden, outgoing = lax.optimization_barrier((hidden, outgoing))
+    hidden, outgoing, gate_send = lax.optimization_barrier((hidden, outgoing, gate_send))
     hidden_other = swap_dp(hidden)
+    gate_slots = lax.all_to_all(gate_send, "expert", split_axis=0, concat_axis=0, tiled=True)
     received = lax.all_to_all(outgoing, "expert", split_axis=0, concat_axis=0, tiled=True)
-    gate_slots = lax.all_to_all(gate_send, "expert", split_axis=0, concat_axis=0, tiled=True)
     slots = expert_count * capacity
     narrow_rows = received.reshape(slots, -1)
     gate_bf16 = gate_slots.reshape(-1)
     gate_column = gate_bf16.astype(jnp.float32)[:, None]
+    other_gates = swap_dp(gate_bf16)
     fragment = lax.all_gather(narrow_rows, "tensor", axis=1, tiled=True)
 
     width = fragment.shape[1]
@@ -69,8 +70,10 @@
     )
     other_piece = swap_dp(send_rows)
     other_rows = lax.all_gather(other_piece, "tensor", axis=1, tiled=True)
-    hidden_other, other_rows = lax.optimization_barrier((hidden_other, other_rows))
-    other_gates = swap_dp(gate_bf16).astype(jnp.float32)[:, None]
+    hidden_other, other_rows, other_gates = lax.optimization_barrier(
+        (hidden_other, other_rows, other_gates)
+    )
+    other_gates = other_gates.astype(jnp.float32)[:, None]
 
     local_weight = down_weight[0]
     partial_other = lax.dot_general(
@@ -89,13 +92,13 @@
     )
     rounded_own = lax.optimization_barrier(grad_own.astype(jnp.bfloat16))
     rounded_other = lax.optimization_barrier(grad_other.astype(jnp.bfloat16))
-    partial_back, rounded_own, rounded_other = lax.optimization_barrier(
-        (partial_back, rounded_own, rounded_other)
-    )
-    upstream = partial_own + partial_back
     down_grad = (rounded_own.astype(jnp.float32) + rounded_other.astype(jnp.float32)).astype(
         jnp.bfloat16
     )
+    partial_back, partial_own, down_grad = lax.optimization_barrier(
+        (partial_back, partial_own, down_grad)
+    )
+    upstream = partial_own + partial_back
 
     score = jnp.sum(hidden.astype(jnp.float32) * upstream, axis=1)
     hidden_grad = gate_column * upstream

time: 617 us -> 433 us (0.70)
  waiting for transfers between devices: 427 us -> 240 us
    ppermute x4, waiting for transfers between devices: 248 us -> 102 us  [swap_dp(): return lax.ppermute(value, 'dp', perm=[(0, 1), (1, 0)])]
    all_gather x1, waiting for transfers between devices: 64.4 us -> 19.9 us  [local(): other_rows = lax.all_gather(other_piece, 'tensor', axis=1, tiled=True)]
    convert_element_type x1 -> x3, other arithmetic: 0.01 us -> 22.7 us  [the longest x1 18.6 us: local(): (rounded_own.astype(jnp.float32) + rounded_other.astype(jnp.float32)).ast...]
    broadcast_in_dim x2 -> x1, other arithmetic: 36.5 us -> 16 us  [local(): return (gate_grad[None], up_grad[None], down_grad[None], router_grad)]
  transfers between devices with their start and end apart: 7 -> 7, of which waited for: 4 -> 5; matrix products, arithmetic and copies ran while one was open for 12% -> 17% of each run, Pallas kernels for 0% -> 0%
where the time goes in v2:
time: 433 us
  waiting for transfers between devices  240 us (55%)
  matrix products  72.1 us (17%)
  other arithmetic  51.7 us (12%)
  blocking collectives  40.1 us (9%)
  between operations  14.2 us (3%)
  starting transfers between devices  10.1 us (2%)
  local copies, waits for them, and re-layouts  4.71 us (1%)
    all_gather x1, waiting for transfers between devices, local(): fragment = lax.all_gather(narrow_rows, 'tensor', axis=1, tiled=True)  114 us
    ppermute x4, waiting for transfers between devices, swap_dp(): return lax.ppermute(value, 'dp', perm=[(0, 1), (1, 0)])  102 us
    all_to_all x1, blocking collectives, local(): lax.all_to_all(outgoing, 'expert', split_axis=0, concat_axis=0, tiled=True)  24.2 us
    all_gather x1, waiting for transfers between devices, local(): other_rows = lax.all_gather(other_piece, 'tensor', axis=1, tiled=True)  19.9 us
    dot_general x1, matrix products, local(): lax.dot_general(other_rows, local_weight, contract_cols, preferred_elemen...  19.4 us
    convert_element_type x1, other arithmetic, local(): (rounded_own.astype(jnp.float32) + rounded_other.astype(jnp.float32)).ast...  18.6 us
    dot_general x1, matrix products, local(): lax.dot_general(own_rows, local_weight, contract_cols, preferred_element_...  18.5 us
    dot_general x1, matrix products, local(): lax.dot_general(hidden_other, scaled_other, contract_rows, preferred_elem...  16.9 us
  transfers between devices with their start and end apart: 7, of which 5 were waited for; matrix products, arithmetic and copies ran while one was open for 17% of the time, Pallas kernels for 0%

profile of v2, /device:TPU:0, one launch (start us, length us, event | category | flops | bytes accessed | tf_op | source)
XLA Modules:
  0.0 432.8 jit_solution(11709492334514320283)
XLA Ops:
  7.2 0.0 copy-start
  7.2 0.0 all-gather.3.cloned.1.call-start
  7.2 0.9 copy.32
  8.1 0.1 eq.59
  8.2 0.1 eq.55
  8.4 1.2 reduce-window.6
  9.6 0.2 slice_reduce_fusion
  9.8 0.2 reduce-window.9
  10.0 0.1 add_bitcast_fusion
  10.1 0.1 reduce_sum.48
  10.3 0.1 copy.34
  10.3 0.7 multiply_add_fusion
  11.1 0.8 slice_convert_fusion.1
  11.8 0.2 select_reduce_fusion.2
  12.0 0.1 convert_element_type.95
  12.1 0.0 copy-done
  12.1 0.8 convolution_convert_fusion.2
  12.9 8.9 %fusion.4 = bf16[768,3584]{1,0:T(8,128)(2,1)} fusion(bf16[1,768,3584]{2,1,0:T(8,128)(2,1)} %param.10, bf16[1,768,3584]{2,1,0:T(8,128)(2,1)} %param.9), kind=kLoop, calls=%fused_computation.12 | loop fusion | flops 22020096 | bytes 16515072 | tf_op jit(solution)/shard_map/convert_element_type | solution.py:45
  21.7 24.2 %all_to_all.23 = bf16[4,192,1024]{2,1,0:T(8,128)(2,1)} all-to-all(bf16[4,192,1024]{2,1,0:T(8,128)(2,1)S(1)} %bitcast.66), channel_id=1, replica_groups=mesh['dp'=2,'expert'=4,'tensor'=4] {'expert'}, dimensions={0} | all-to-all | bytes 3145728 | tf_op jit(solution)/shard_map/all_to_all | solution.py:56
  46.0 0.0 all-gather.3.cloned.1.call-update
  46.0 0.0 all-gather.5.cloned.1.call-start
  46.0 2.0 collective-permute-start
  48.1 114.2 %all-gather.3.cloned.1.call-done = bf16[768,4096]{1,0:T(8,128)(2,1)} async-done(((bf16[768,1024]{1,0:T(8,128)(2,1)}), bf16[768,4096]{1,0:T(8,128)(2,1)}) %all-gather.3.cloned.1.call-update) | async-done | bytes 6291472 | tf_op jit(solution)/shard_map/all_gather | solution.py:62
  162.3 0.0 slice-start.2
  162.3 1.3 constant_dynamic-slice_fusion
  163.6 1.5 collective-permute-start.1
  165.1 18.3 %collective-permute-done.1 = bf16[768,512]{1,0:T(8,128)(2,1)S(1)} collective-permute-done((bf16[768,512]{1,0:T(8,128)(2,1)S(1)}, bf16[768,512]{1,0:T(8,128)(2,1)S(1)}, u32[]{:S(2)}, u32[]{:S(2)}) %collective-permute-start.1) | collective-permute-done | bytes 786464 | tf_op jit(solution)/shard_map/ppermute | solution.py:15
  183.4 0.0 copy-start.2
  183.4 0.9 copy-done.2
  184.3 0.0 all-gather.5.cloned.1.call-update
  184.3 0.6 copy.35
  184.9 3.2 all-to-all-start
  188.2 3.7 all-to-all-done
  192.0 0.1 reshape.62
  192.1 1.7 collective-permute-start.2
  193.8 0.0 slice-start.3
  193.8 18.5 %fusion = f32[768,3584]{1,0:T(8,128)} fusion(bf16[1,3584,2048]{2,1,0:T(8,128)(2,1)} %param.11, bf16[768,4096]{1,0:T(8,128)(2,1)} %all-gather.3.cloned.1.call-done, s32[]{:T(128)S(6)} %select_n.32), kind=kOutput, calls=%fused_computation.6 | convolution fusion | flops 11274289152 | bytes 28835844 | tf_op jit(solution)/shard_map/dot_general | solution.py:83
  212.3 0.0 slice-done.2
  212.3 0.0 slice-done.3
  212.3 16.6 %convolution_convert_fusion.1 = bf16[3584,2048]{1,0:T(8,128)(2,1)} fusion(bf16[768,3584]{1,0:T(8,128)(2,1)S(1)} %bitcast.63, f32[768]{0:T(1024)S(1)} %convert_element_type.96, bf16[768,4096]{1,0:T(8,128)(2,1)} %all-gather.3.cloned.1.call-done, s32[]{:T(128)S(6)} %select_n.32), kind=kOutput, calls=%fused_computation.5 | convolution fusion | flops 11286347776 | bytes 23333892 | tf_op jit(solution)/shard_map/dot_general | solution.py:89
  228.8 0.0 collective-permute-done.2
  228.9 0.0 collective-permute-done
  228.9 19.9 %all-gather.5.cloned.1.call-done = bf16[768,2048]{1,0:T(8,128)(2,1)} async-done(((bf16[768,512]{1,0:T(8,128)(2,1)}), bf16[768,2048]{1,0:T(8,128)(2,1)}) %all-gather.5.cloned.1.call-update) | async-done | bytes 3145744 | tf_op jit(solution)/shard_map/all_gather | solution.py:72
  248.7 0.0 copy-start.3
  248.7 0.0 slice-start
  248.7 19.4 %fusion.12 = bf16[768,3584]{1,0:T(8,128)(2,1)} fusion(bf16[768,2048]{1,0:T(8,128)(2,1)} %all-gather.5.cloned.1.call-done, bf16[1,3584,2048]{2,1,0:T(8,128)(2,1)} %param.11), kind=kOutput, calls=%fused_computation.22 | convolution fusion | flops 11277041664 | bytes 23330816 | tf_op jit(solution)/shard_map/dot_general | solution.py:79
  268.2 0.0 slice-start.1
  268.2 1.5 collective-permute-start.3
  269.6 0.0 copy-done.3
  269.6 16.9 %convolution_convert_fusion = bf16[3584,2048]{1,0:T(8,128)(2,1)} fusion(bf16[768,3584]{1,0:T(8,128)(2,1)} %collective-permute-done, bf16[768,2048]{1,0:T(8,128)(2,1)S(1)} %copy-done.3, f32[768]{0:T(1024)S(1)} %convert_element_type.103), kind=kOutput, calls=%fused_computation.4 | convolution fusion | flops 11286347776 | bytes 23333888 | tf_op jit(solution)/shard_map/dot_general | solution.py:90
  286.5 18.6 %add_convert_fusion = bf16[3584,2048]{1,0:T(8,128)(2,1)} fusion(bf16[3584,2048]{1,0:T(8,128)(2,1)} %convolution_convert_fusion, bf16[3584,2048]{1,0:T(8,128)(2,1)} %convolution_convert_fusion.1), kind=kLoop, calls=%fused_computation | loop fusion | flops 29360128 | bytes 44040192 | tf_op jit(solution)/shard_map/convert_element_type | solution.py:95
  305.2 83.7 %collective-permute-done.3 = bf16[768,3584]{1,0:T(8,128)(2,1)} collective-permute-done((bf16[768,3584]{1,0:T(8,128)(2,1)}, bf16[768,3584]{1,0:T(8,128)(2,1)}, u32[]{:S(2)}, u32[]{:S(2)}) %collective-permute-start.3) | collective-permute-done | bytes 5505056 | tf_op jit(solution)/shard_map/ppermute | solution.py:15
  388.9 4.1 convert_element_type.98
  393.0 0.0 slice-done
  393.0 0.0 slice-done.1
  393.0 0.0 copy-start.1
  393.0 16.0 %fusion.15 = (bf16[1,768,3584]{2,1,0:T(8,128)(2,1)}, bf16[1,768,3584]{2,1,0:T(8,128)(2,1)}, f32[768]{0:T(1024)S(1)}) fusion(f32[768]{0:T(1024)S(1)} %convert_element_type.96, bf16[1,768,3584]{2,1,0:T(8,128)(2,1)S(1)} %bitcast.61, f32[768,3584]{1,0:T(8,128)} %fusion, f32[768,3584]{1,0:T(8,128)S(1)} %convert_element_type.98, bf16[1,768,3584]{2,1,0:T(8,128)(2,1)} %param.10, ...), kind=kLoop, calls=%fused_computation.25 | loop fusion | flops 55049472 | bytes 49551360 | tf_op jit(solution)/shard_map/broadcast_in_dim | solution.py:123
  409.0 0.1 all_to_all.18
  409.1 9.3 %psum.7 = f32[4,1,192]{2,1,0:T(1,128)S(1)} all-reduce(f32[4,1,192]{2,1,0:T(1,128)S(1)} %all_to_all.18), channel_id=1, replica_groups=mesh['dp'=2,'expert'=4,'tensor'=4] {'tensor'}, use_global_device_ids=true, to_apply=%region_5.6 | all-reduce | flops 768 | bytes 6144 | tf_op jit(solution)/shard_map/psum | solution.py:107
  418.4 6.5 %all_to_all.24 = f32[4,1,192]{2,1,0:T(1,128)S(1)} all-to-all(f32[4,1,192]{2,1,0:T(1,128)S(1)} %psum.7), channel_id=1, replica_groups=mesh['dp'=2,'expert'=4,'tensor'=4] {'expert'}, dimensions={0} | all-to-all | bytes 6144 | tf_op jit(solution)/shard_map/all_to_all | solution.py:108
  425.0 0.1 broadcast_in_dim.76
  425.1 0.3 select_reduce_fusion.1
  425.4 0.6 pad_maximum_fusion
  426.0 0.0 copy-done.1
  (9 shorter events, 0.1 us)
Async XLA Ops:
  7.2 5.0 %copy-start = (bf16[256,1024]{1,0:T(8,128)(2,1)S(1)}, bf16[256,1024]{1,0:T(8,128)(2,1)}, u32[]{:S(2)}) copy-start(bf16[256,1024]{1,0:T(8,128)(2,1)} %param.6) | copy-start | bytes 1572868
  7.2 155.1 %all-gather.3.cloned.1.call-start = ((), (), s32[]{:S(2)}) async-start(), calls=%async_computation.3 | async-start | bytes 7864320 | tf_op jit(solution)/shard_map/all_gather | solution.py:62
  46.0 202.7 %all-gather.5.cloned.1.call-start = ((), (), s32[]{:S(2)}) async-start(), calls=%async_computation.4 | async-start | bytes 3932160 | tf_op jit(solution)/shard_map/all_gather | solution.py:72
  46.0 182.8 %collective-permute-start = (bf16[768,3584]{1,0:T(8,128)(2,1)}, bf16[768,3584]{1,0:T(8,128)(2,1)}, u32[]{:S(2)}, u32[]{:S(2)}) collective-permute-start(bf16[768,3584]{1,0:T(8,128)(2,1)} %fusion.4), channel_id=1, source_target_pairs={{0,16},{16,0},{1,17},{17,1},{2,18},{18,2},{3,19},{19,3},{4,20},{20... | collective-permute-start | bytes 16515080 | tf_op jit(solution)/shard_map/ppermute | solution.py:15
  162.3 50.0 %slice-start.2 = ((s8[5505024]{0:T(1024)(128)(4,1)}), s8[1310720]{0:T(1024)(128)(4,1)S(1)}, s32[]{:S(2)}) async-start(s8[5505024]{0:T(1024)(128)(4,1)} %bitcast.62), calls=%async_computation.7 | async-start | bytes 2621440
  163.6 19.9 %collective-permute-start.1 = (bf16[768,512]{1,0:T(8,128)(2,1)S(1)}, bf16[768,512]{1,0:T(8,128)(2,1)S(1)}, u32[]{:S(2)}, u32[]{:S(2)}) collective-permute-start(bf16[768,512]{1,0:T(8,128)(2,1)S(1)} %constant_dynamic-slice_fusion), channel_id=1, source_target_pairs={{0,16},{16,0},{1,17},{17,1},{2,18},{18,2},{3,19},{19,3},{4,20},{20... | collective-permute-start | bytes 2359304 | tf_op jit(solution)/shard_map/ppermute | solution.py:15
  183.4 0.9 copy-start.2
  184.9 7.0 %all-to-all-start = ((bf16[4,1,192]{2,1,0:T(2,128)(2,1)}), bf16[4,1,192]{2,1,0:T(2,128)(2,1)S(1)}, u32[]{:S(2)}, u32[]{:S(2)}) async-start(bf16[4,1,192]{2,1,0:T(2,128)(2,1)} %copy.35), calls=%async_computation | async-start | bytes 8192 | tf_op jit(solution)/shard_map/all_to_all | solution.py:55
  192.1 36.8 %collective-permute-start.2 = (bf16[768]{0:T(1024)(128)(2,1)S(1)}, bf16[768]{0:T(1024)(128)(2,1)S(1)}, u32[]{:S(2)}, u32[]{:S(2)}) collective-permute-start(bf16[768]{0:T(1024)(128)(2,1)S(1)} %reshape.62), channel_id=1, source_target_pairs={{0,16},{16,0},{1,17},{17,1},{2,18},{18,2},{3,19},{19,3},{4,20},{20... | collective-permute-start | bytes 4616 | tf_op jit(solution)/shard_map/ppermute | solution.py:15
  193.8 18.5 %slice-start.3 = ((s8[5505024]{0:T(1024)(128)(4,1)}), s8[4194304]{0:T(1024)(128)(4,1)S(1)}, s32[]{:S(2)}) async-start(s8[5505024]{0:T(1024)(128)(4,1)} %bitcast.62), calls=%async_computation.8 | async-start | bytes 8388608
  248.7 20.9 %copy-start.3 = (bf16[768,2048]{1,0:T(8,128)(2,1)S(1)}, bf16[768,2048]{1,0:T(8,128)(2,1)}, u32[]{:S(2)}) copy-start(bf16[768,2048]{1,0:T(8,128)(2,1)} %all-gather.5.cloned.1.call-done) | copy-start | bytes 9437188
  248.7 144.2 %slice-start = ((s8[5505024]{0:T(1024)(128)(4,1)}), s8[4194304]{0:T(1024)(128)(4,1)S(1)}, s32[]{:S(2)}) async-start(s8[5505024]{0:T(1024)(128)(4,1)} %bitcast.60), calls=%async_computation.5 | async-start | bytes 8388608
  268.2 124.8 %slice-start.1 = ((s8[5505024]{0:T(1024)(128)(4,1)}), s8[1310720]{0:T(1024)(128)(4,1)S(1)}, s32[]{:S(2)}) async-start(s8[5505024]{0:T(1024)(128)(4,1)} %bitcast.60), calls=%async_computation.6 | async-start | bytes 2621440
  268.2 120.7 %collective-permute-start.3 = (bf16[768,3584]{1,0:T(8,128)(2,1)}, bf16[768,3584]{1,0:T(8,128)(2,1)}, u32[]{:S(2)}, u32[]{:S(2)}) collective-permute-start(bf16[768,3584]{1,0:T(8,128)(2,1)} %fusion.12), channel_id=1, source_target_pairs={{0,16},{16,0},{1,17},{17,1},{2,18},{18,2},{3,19},{19,3},{4,20},{20... | collective-permute-start | bytes 16515080 | tf_op jit(solution)/shard_map/ppermute | solution.py:15
  393.0 33.0 %copy-start.1 = (bf16[256,1024]{1,0:T(8,128)(2,1)S(1)}, bf16[256,1024]{1,0:T(8,128)(2,1)}, u32[]{:S(2)}) copy-start(bf16[256,1024]{1,0:T(8,128)(2,1)} %param.6) | copy-start | bytes 1572868
Sparse Core Ops, SparseCore 0:
  46.1 116.1 all-gather.2
  184.5 64.2 all-gather.4

commit v3 on v2

--- a/solution.py
+++ b/solution.py
@@ -4,6 +4,7 @@
 from jax.sharding import PartitionSpec as P
 
 PARTIAL_DTYPE = jnp.bfloat16
+CHUNKS = 2
 
 
 def silu_parts(values):
@@ -51,7 +52,6 @@
     )
     outgoing = outgoing.astype(jnp.bfloat16).reshape(expert_count, capacity, -1)
     hidden, outgoing, gate_send = lax.optimization_barrier((hidden, outgoing, gate_send))
-    hidden_other = swap_dp(hidden)
     gate_slots = lax.all_to_all(gate_send, "expert", split_axis=0, concat_axis=0, tiled=True)
     received = lax.all_to_all(outgoing, "expert", split_axis=0, concat_axis=0, tiled=True)
     slots = expert_count * capacity
@@ -59,30 +59,55 @@
     gate_bf16 = gate_slots.reshape(-1)
     gate_column = gate_bf16.astype(jnp.float32)[:, None]
     other_gates = swap_dp(gate_bf16)
-    fragment = lax.all_gather(narrow_rows, "tensor", axis=1, tiled=True)
-
-    width = fragment.shape[1]
+    width = narrow_rows.shape[1] * tensor_count
     half = width // 2
     piece = half // tensor_count
-    own_rows = lax.dynamic_slice_in_dim(fragment, replica * half, half, axis=1)
-    send_rows = lax.dynamic_slice_in_dim(
-        fragment, (1 - replica) * half + part * piece, piece, axis=1
-    )
-    other_piece = swap_dp(send_rows)
-    other_rows = lax.all_gather(other_piece, "tensor", axis=1, tiled=True)
+    local_weight = down_weight[0]
+    chunk = slots // CHUNKS
+    hidden_parts = [swap_dp(hidden[:chunk])]
+    fragments = [
+        lax.all_gather(narrow_rows[index * chunk : (index + 1) * chunk], "tensor", axis=1, tiled=True)
+        for index in range(CHUNKS)
+    ]
+    own_parts = [
+        lax.dynamic_slice_in_dim(fragment, replica * half, half, axis=1) for fragment in fragments
+    ]
+    pieces = []
+    for index in range(CHUNKS):
+        send_rows = lax.dynamic_slice_in_dim(
+            fragments[index], (1 - replica) * half + part * piece, piece, axis=1
+        )
+        send_rows, hidden_parts[-1] = lax.optimization_barrier((send_rows, hidden_parts[-1]))
+        pieces.append(swap_dp(send_rows))
+        if index + 1 < CHUNKS:
+            next_hidden, pieces[-1] = lax.optimization_barrier(
+                (hidden[(index + 1) * chunk : (index + 2) * chunk], pieces[-1])
+            )
+            hidden_parts.append(swap_dp(next_hidden))
+    other_parts, partial_own_parts, partial_back_parts = [], [], []
+    for index in range(CHUNKS):
+        other_part = lax.all_gather(pieces[index], "tensor", axis=1, tiled=True)
+        if index == 0:
+            other_part, pieces[-1] = lax.optimization_barrier((other_part, pieces[-1]))
+        other_parts.append(other_part)
+        partial_other = lax.dot_general(
+            other_part, local_weight, contract_cols, preferred_element_type=jnp.float32
+        )
+        partial_back_parts.append(swap_dp(partial_other.astype(PARTIAL_DTYPE)))
+        partial_own_parts.append(
+            lax.dot_general(
+                own_parts[index], local_weight, contract_cols, preferred_element_type=jnp.float32
+            )
+        )
+    hidden_other = jnp.concatenate(hidden_parts, axis=0)
+    own_rows = jnp.concatenate(own_parts, axis=0)
+    other_rows = jnp.concatenate(other_parts, axis=0)
+    partial_own = jnp.concatenate(partial_own_parts, axis=0)
+    partial_back = jnp.concatenate(partial_back_parts, axis=0).astype(jnp.float32)
     hidden_other, other_rows, other_gates = lax.optimization_barrier(
         (hidden_other, other_rows, other_gates)
     )
     other_gates = other_gates.astype(jnp.float32)[:, None]
-
-    local_weight = down_weight[0]
-    partial_other = lax.dot_general(
-        other_rows, local_weight, contract_cols, preferred_element_type=jnp.float32
-    )
-    partial_back = swap_dp(partial_other.astype(PARTIAL_DTYPE)).astype(jnp.float32)
-    partial_own = lax.dot_general(
-        own_rows, local_weight, contract_cols, preferred_element_type=jnp.float32
-    )
 
     scaled_own = (gate_column * own_rows.astype(jnp.float32)).astype(jnp.bfloat16)
     scaled_other = (other_gates * other_rows.astype(jnp.float32)).astype(jnp.bfloat16)

time: 433 us -> 451 us (1.042)
  waiting for transfers between devices: 240 us -> 215 us
  other arithmetic: 51.7 us -> 71.6 us
  local copies, waits for them, and re-layouts: 4.71 us -> 20.2 us
  matrix products: 72.1 us -> 77.3 us
    all_gather x2 -> x4, waiting for transfers between devices: 134 us -> 118 us  [the longest x2 107 us: local(): lax.all_gather(narrow_rows[index * chunk:(index + 1) * chunk], 'tensor',...]
    concatenate x0 -> x3, other arithmetic: none -> 15.6 us  [the longest x1 8.99 us: local(): partial_own = jnp.concatenate(partial_own_parts, axis=0)]
    ppermute x4 -> x7, waiting for transfers between devices: 102 us -> 93 us  [swap_dp(): return lax.ppermute(value, 'dp', perm=[(0, 1), (1, 0)])]
    dynamic_slice x1 -> x4, local copies, waits for them, and re-layouts: 1.29 us -> 9.07 us  [the longest x2 5.48 us: local(): lax.dynamic_slice_in_dim(fragment, replica * half, half, axis=1)]
    slice x1 -> x3, local copies, waits for them, and re-layouts: 0.22 us -> 6.93 us  [the longest x1 5.41 us: local(): hidden_parts = [swap_dp(hidden[:chunk])]]
    dot_general x2 -> x4, matrix products: 37.9 us -> 44.1 us  [the longest x2 22.9 us: local(): lax.dot_general(own_parts[index], local_weight, contract_cols, preferred_...]
  transfers between devices with their start and end apart: 7 -> 12, of which waited for: 5 -> 8; matrix products, arithmetic and copies ran while one was open for 17% -> 28% of each run, Pallas kernels for 0% -> 0%
where the time goes in v3:
time: 451 us; the launch traced here: 450 us
  waiting for transfers between devices  215 us (48%)
  matrix products  77.3 us (17%)
  other arithmetic  71.6 us (16%)
  blocking collectives  40.4 us (9%)
  local copies, waits for them, and re-layouts  20.2 us (4%)
  between operations  14 us (3%)
  starting transfers between devices  12 us (3%)
    all_gather x2, waiting for transfers between devices, local(): lax.all_gather(narrow_rows[index * chunk:(index + 1) * chunk], 'tensor',...  107 us
    ppermute x7, waiting for transfers between devices, swap_dp(): return lax.ppermute(value, 'dp', perm=[(0, 1), (1, 0)])  93 us
    all_to_all x1, blocking collectives, local(): lax.all_to_all(outgoing, 'expert', split_axis=0, concat_axis=0, tiled=True)  24.1 us
    dot_general x2, matrix products, local(): lax.dot_general(own_parts[index], local_weight, contract_cols, preferred_...  22.9 us
    dot_general x2, matrix products, local(): lax.dot_general(other_part, local_weight, contract_cols, preferred_elemen...  21.2 us
    convert_element_type x1, other arithmetic, local(): (rounded_own.astype(jnp.float32) + rounded_other.astype(jnp.float32)).ast...  18.6 us
    dot_general x1, matrix products, local(): lax.dot_general(hidden, scaled_own, contract_rows, preferred_element_type...  18.1 us
    broadcast_in_dim x1, other arithmetic, local(): return (gate_grad[None], up_grad[None], down_grad[None], router_grad)  16 us
  transfers between devices with their start and end apart: 12, of which 8 were waited for; matrix products, arithmetic and copies ran while one was open for 28% of the time, Pallas kernels for 0%

profile of v3, /device:TPU:0, one launch (start us, length us, event | category | flops | bytes accessed | tf_op | source)
XLA Modules:
  0.0 450.5 jit_solution(10268415616874670514)
XLA Ops:
  7.2 0.9 copy.32
  8.1 0.1 eq.59
  8.2 0.1 eq.55
  8.4 1.2 reduce-window.6
  9.6 0.2 slice_reduce_fusion
  9.8 0.2 reduce-window.9
  10.0 0.1 add_bitcast_fusion
  10.1 0.1 reduce_sum.48
  10.3 0.1 copy.34
  10.3 0.7 multiply_add_fusion
  11.1 0.8 slice_convert_fusion.1
  11.8 0.2 select_reduce_fusion.2
  12.0 0.1 convert_element_type.98
  12.1 0.8 convolution_convert_fusion.2
  12.9 8.9 %fusion.8 = bf16[768,3584]{1,0:T(8,128)(2,1)} fusion(bf16[1,768,3584]{2,1,0:T(8,128)(2,1)} %param.10, bf16[1,768,3584]{2,1,0:T(8,128)(2,1)} %param.9), kind=kLoop, calls=%fused_computation.16 | loop fusion | flops 22020096 | bytes 16515072 | tf_op jit(solution)/shard_map/convert_element_type | solution.py:46
  21.8 24.1 %all_to_all.23 = bf16[4,192,1024]{2,1,0:T(8,128)(2,1)S(1)} all-to-all(bf16[4,192,1024]{2,1,0:T(8,128)(2,1)S(1)} %bitcast.77), channel_id=1, replica_groups=mesh['dp'=2,'expert'=4,'tensor'=4] {'expert'}, dimensions={0} | all-to-all | bytes 3145728 | tf_op jit(solution)/shard_map/all_to_all | solution.py:56
  45.9 1.3 fusion.45
  47.2 0.0 all-gather.9.cloned.1.call-start
  47.3 0.7 all-gather.9.cloned.1.call-update
  48.0 5.4 %fusion.44 = (bf16[384,3584]{1,0:T(8,128)(2,1)}, bf16[384,3584]{1,0:T(8,128)(2,1)}) fusion(bf16[768,3584]{1,0:T(8,128)(2,1)} %fusion.8), kind=kLoop, calls=%fused_computation.73 | loop fusion | bytes 11010048 | tf_op jit(solution)/shard_map/slice | solution.py:67
  53.4 1.5 collective-permute-start
  54.9 0.6 copy.35
  55.5 3.2 all-to-all-start
  58.7 0.0 all-gather.7.cloned.1.call-start
  58.8 3.7 all-to-all-done
  62.5 0.1 reshape.62
  62.6 0.5 collective-permute-start.6
  63.1 48.0 %all-gather.5.cloned.1.call-done = bf16[384,4096]{1,0:T(8,128)(2,1)} async-done(((bf16[384,1024]{1,0:T(8,128)(2,1)}), bf16[384,4096]{1,0:T(8,128)(2,1)}) %all-gather.5.cloned.1.call-update) | async-done | bytes 3145744 | tf_op jit(solution)/shard_map/all_gather | solution.py:69
  111.1 1.8 constant_dynamic-slice_fusion.3
  112.9 1.7 collective-permute-done
  114.7 1.5 collective-permute-start.1
  116.2 59.3 %all-gather.9.cloned.1.call-done = bf16[384,4096]{1,0:T(8,128)(2,1)} async-done(((bf16[384,1024]{1,0:T(8,128)(2,1)}), bf16[384,4096]{1,0:T(8,128)(2,1)}) %all-gather.9.cloned.1.call-update) | async-done | bytes 3145744 | tf_op jit(solution)/shard_map/all_gather | solution.py:69
  175.5 2.7 constant_dynamic-slice_fusion
  178.2 1.8 constant_dynamic-slice_fusion.2
  180.0 2.8 constant_dynamic-slice_fusion.1
  182.8 1.5 collective-permute-start.2
  184.2 18.1 %convolution_convert_fusion.1 = bf16[3584,2048]{1,0:T(8,128)(2,1)} fusion(bf16[768,3584]{1,0:T(8,128)(2,1)} %fusion.8, bf16[384,2048]{1,0:T(8,128)(2,1)} %constant_dynamic-slice_fusion, bf16[384,2048]{1,0:T(8,128)(2,1)} %constant_dynamic-slice_fusion.1, f32[768]{0:T(1024)S(1)} %convert_element_type.99), kind=kOutput, calls=%fused_computation.5 | convolution fusion | flops 11291066368 | bytes 23333888 | tf_op jit(solution)/shard_map/dot_general | solution.py:114
  202.4 0.2 all-gather.11.cloned.1.call-start
  202.6 11.3 %fusion = f32[384,3584]{1,0:T(8,128)} fusion(bf16[384,2048]{1,0:T(8,128)(2,1)} %constant_dynamic-slice_fusion, bf16[1,3584,2048]{2,1,0:T(8,128)(2,1)} %param.11), kind=kOutput, calls=%fused_computation.6 | convolution fusion | flops 5637144576 | bytes 21757952 | tf_op jit(solution)/shard_map/dot_general | solution.py:98
  213.9 30.6 %collective-permute-done.2 = bf16[384,3584]{1,0:T(8,128)(2,1)} collective-permute-done((bf16[384,3584]{1,0:T(8,128)(2,1)}, bf16[384,3584]{1,0:T(8,128)(2,1)}, u32[]{:S(2)}, u32[]{:S(2)}) %collective-permute-start.2) | collective-permute-done | bytes 2752544 | tf_op jit(solution)/shard_map/ppermute | solution.py:16
  244.5 1.5 collective-permute-start.3
  246.0 11.6 %fusion.2 = f32[384,3584]{1,0:T(8,128)} fusion(bf16[384,2048]{1,0:T(8,128)(2,1)S(1)} %copy-done.5, bf16[1,3584,2048]{2,1,0:T(8,128)(2,1)} %param.11), kind=kOutput, calls=%fused_computation.8 | convolution fusion | flops 5637144576 | bytes 21757952 | tf_op jit(solution)/shard_map/dot_general | solution.py:98
  257.6 0.7 copy-done.8
  258.4 9.0 %pad_maximum_fusion = f32[768,3584]{1,0:T(8,128)} fusion(f32[384,3584]{1,0:T(8,128)} %fusion, f32[384,3584]{1,0:T(8,128)} %fusion.2), kind=kLoop, calls=%fused_computation.24 | loop fusion | flops 2752512 | bytes 22020096 | tf_op jit(solution)/shard_map/concatenate | solution.py:105
  267.4 4.7 %pad_maximum_fusion.1 = bf16[768,3584]{1,0:T(8,128)(2,1)} fusion(bf16[384,3584]{1,0:T(8,128)(2,1)} %collective-permute-done.2, bf16[384,3584]{1,0:T(8,128)(2,1)S(1)} %collective-permute-done), kind=kLoop, calls=%fused_computation.33 | loop fusion | flops 11010048 | bytes 11010048 | tf_op jit(solution)/shard_map/concatenate | solution.py:102
  272.1 10.6 %fusion.16 = bf16[384,3584]{1,0:T(8,128)(2,1)} fusion(bf16[384,2048]{1,0:T(8,128)(2,1)S(1)} %copy-done.3, bf16[1,3584,2048]{2,1,0:T(8,128)(2,1)} %param.11), kind=kOutput, calls=%fused_computation.29 | convolution fusion | flops 5638520832 | bytes 19005440 | tf_op jit(solution)/shard_map/dot_general | solution.py:93
  282.7 0.6 collective-permute-start.4
  283.2 10.3 %all-gather.11.cloned.1.call-done = bf16[384,2048]{1,0:T(8,128)(2,1)} async-done(((bf16[384,512]{1,0:T(8,128)(2,1)}), bf16[384,2048]{1,0:T(8,128)(2,1)}) %all-gather.11.cloned.1.call-update) | async-done | bytes 1572880 | tf_op jit(solution)/shard_map/all_gather | solution.py:89
  293.5 1.9 pad_maximum_fusion.2
  295.4 1.1 copy-done.2
  296.5 14.3 %convolution_convert_fusion = bf16[3584,2048]{1,0:T(8,128)(2,1)} fusion(bf16[768,3584]{1,0:T(8,128)(2,1)S(1)} %copy-done.2, bf16[768,2048]{1,0:T(8,128)(2,1)S(1)} %pad_maximum_fusion.2, f32[768]{0:T(1024)S(1)} %convert_element_type.107), kind=kOutput, calls=%fused_computation.4 | convolution fusion | flops 11286347776 | bytes 23333888 | tf_op jit(solution)/shard_map/dot_general | solution.py:115
  310.9 10.6 %fusion.19 = bf16[384,3584]{1,0:T(8,128)(2,1)} fusion(bf16[384,2048]{1,0:T(8,128)(2,1)S(1)} %copy-done.6, bf16[1,3584,2048]{2,1,0:T(8,128)(2,1)} %param.11), kind=kOutput, calls=%fused_computation.30 | convolution fusion | flops 5638520832 | bytes 19005440 | tf_op jit(solution)/shard_map/dot_general | solution.py:93
  321.5 1.5 collective-permute-start.5
  323.0 18.6 %add_convert_fusion = bf16[3584,2048]{1,0:T(8,128)(2,1)} fusion(bf16[3584,2048]{1,0:T(8,128)(2,1)} %convolution_convert_fusion, bf16[3584,2048]{1,0:T(8,128)(2,1)} %convolution_convert_fusion.1), kind=kLoop, calls=%fused_computation | loop fusion | flops 29360128 | bytes 44040192 | tf_op jit(solution)/shard_map/convert_element_type | solution.py:120
  341.6 4.0 collective-permute-done.4
  345.6 56.6 %collective-permute-done.5 = bf16[384,3584]{1,0:T(8,128)(2,1)} collective-permute-done((bf16[384,3584]{1,0:T(8,128)(2,1)}, bf16[384,3584]{1,0:T(8,128)(2,1)}, u32[]{:S(2)}, u32[]{:S(2)}) %collective-permute-start.5) | collective-permute-done | bytes 2752544 | tf_op jit(solution)/shard_map/ppermute | solution.py:16
  402.2 8.3 %maximum_convert_fusion = f32[768,3584]{1,0:T(8,128)} fusion(bf16[384,3584]{1,0:T(8,128)(2,1)} %collective-permute-done.5, bf16[384,3584]{1,0:T(8,128)(2,1)} %collective-permute-done.4), kind=kLoop, calls=%fused_computation.32 | loop fusion | flops 11010048 | bytes 16515072 | tf_op jit(solution)/shard_map/convert_element_type | solution.py:106
  410.6 16.0 %fusion.22 = (bf16[1,768,3584]{2,1,0:T(8,128)(2,1)}, bf16[1,768,3584]{2,1,0:T(8,128)(2,1)}, f32[768]{0:T(1024)S(1)}) fusion(f32[768]{0:T(1024)S(1)} %convert_element_type.99, bf16[1,768,3584]{2,1,0:T(8,128)(2,1)} %param.9, f32[768,3584]{1,0:T(8,128)S(1)} %bitcast.73, f32[768,3584]{1,0:T(8,128)} %maximum_convert_fusion, bf16[1,768,3584]{2,1,0:T(8,128)(2,1)} %param.10, ...), kind=kLoop, calls=%fused_computation.31 | loop fusion | flops 55049472 | bytes 49551360 | tf_op jit(solution)/shard_map/broadcast_in_dim | solution.py:148
  426.6 0.1 all_to_all.18
  426.7 9.9 %psum.7 = f32[4,1,192]{2,1,0:T(1,128)S(1)} all-reduce(f32[4,1,192]{2,1,0:T(1,128)S(1)} %all_to_all.18), channel_id=1, replica_groups=mesh['dp'=2,'expert'=4,'tensor'=4] {'tensor'}, use_global_device_ids=true, to_apply=%region_5.6 | all-reduce | flops 768 | bytes 6144 | tf_op jit(solution)/shard_map/psum | solution.py:132
  436.6 6.3 %all_to_all.24 = f32[4,1,192]{2,1,0:T(1,128)S(1)} all-to-all(f32[4,1,192]{2,1,0:T(1,128)S(1)} %psum.7), channel_id=1, replica_groups=mesh['dp'=2,'expert'=4,'tensor'=4] {'expert'}, dimensions={0} | all-to-all | bytes 6144 | tf_op jit(solution)/shard_map/all_to_all | solution.py:133
  442.9 0.1 broadcast_in_dim.76
  443.0 0.3 select_reduce_fusion.1
  443.4 0.6 pad_maximum_fusion.3
  (51 shorter events, 0.3 us)
Async XLA Ops:
  7.2 5.0 %copy-start = (bf16[256,1024]{1,0:T(8,128)(2,1)S(1)}, bf16[256,1024]{1,0:T(8,128)(2,1)}, u32[]{:S(2)}) copy-start(bf16[256,1024]{1,0:T(8,128)(2,1)} %param.6) | copy-start | bytes 1572868
  7.2 104.0 %all-gather.5.cloned.1.call-start = ((), (), s32[]{:S(2)}) async-start(), calls=%async_computation.3 | async-start | bytes 3932160 | tf_op jit(solution)/shard_map/all_gather | solution.py:69
  11.1 10.7 %copy-start.9 = (s32[256,1]{0,1:T(1,128)}, s32[256,1]{0,1:T(1,128)S(1)}, u32[]{:S(2)}) copy-start(s32[256,1]{0,1:T(1,128)S(1)} %get-tuple-element.47) | copy-start | bytes 3076
  11.1 10.7 %copy-start.11 = (s32[256,1]{0,1:T(1,128)}, s32[256,1]{0,1:T(1,128)S(1)}, u32[]{:S(2)}) copy-start(s32[256,1]{0,1:T(1,128)S(1)} %get-tuple-element.48) | copy-start | bytes 3076
  47.2 128.2 %all-gather.9.cloned.1.call-start = ((), (), s32[]{:S(2)}) async-start(), calls=%async_computation.5 | async-start | bytes 3932160 | tf_op jit(solution)/shard_map/all_gather | solution.py:69
  53.4 61.3 %collective-permute-start = (bf16[384,3584]{1,0:T(8,128)(2,1)}, bf16[384,3584]{1,0:T(8,128)(2,1)S(1)}, u32[]{:S(2)}, u32[]{:S(2)}) collective-permute-start(bf16[384,3584]{1,0:T(8,128)(2,1)} %get-tuple-element.43), channel_id=1, source_target_pairs={{0,16},{16,0},{1,17},{17,1},{2,18},{18,2},{3,19},{19,3},{4,20},{20... | collective-permute-start | bytes 8257544 | tf_op jit(solution)/shard_map/ppermute | solution.py:16
  55.5 7.0 %all-to-all-start = ((bf16[4,1,192]{2,1,0:T(2,128)(2,1)}), bf16[4,1,192]{2,1,0:T(2,128)(2,1)S(1)}, u32[]{:S(2)}, u32[]{:S(2)}) async-start(bf16[4,1,192]{2,1,0:T(2,128)(2,1)} %copy.35), calls=%async_computation | async-start | bytes 8192 | tf_op jit(solution)/shard_map/all_to_all | solution.py:55
  58.7 198.9 %all-gather.7.cloned.1.call-start = ((), (), s32[]{:S(2)}) async-start(), calls=%async_computation.4 | async-start | bytes 1966080 | tf_op jit(solution)/shard_map/all_gather | solution.py:89
  62.6 232.8 %collective-permute-start.6 = (bf16[768]{0:T(1024)(128)(2,1)S(1)}, bf16[768]{0:T(1024)(128)(2,1)S(1)}, u32[]{:S(2)}, u32[]{:S(2)}) collective-permute-start(bf16[768]{0:T(1024)(128)(2,1)S(1)} %reshape.62), channel_id=1, source_target_pairs={{0,16},{16,0},{1,17},{17,1},{2,18},{18,2},{3,19},{19,3},{4,20},{20... | collective-permute-start | bytes 4616 | tf_op jit(solution)/shard_map/ppermute | solution.py:16
  114.7 68.1 %collective-permute-start.1 = (bf16[384,512]{1,0:T(8,128)(2,1)}, bf16[384,512]{1,0:T(8,128)(2,1)S(1)}, u32[]{:S(2)}, u32[]{:S(2)}) collective-permute-start(bf16[384,512]{1,0:T(8,128)(2,1)} %constant_dynamic-slice_fusion.3), channel_id=1, source_target_pairs={{0,16},{16,0},{1,17},{17,1},{2,18},{18,2},{3,19},{19,3},{4,20},{20... | collective-permute-start | bytes 1179656 | tf_op jit(solution)/shard_map/ppermute | solution.py:16
  182.7 19.6 %copy-start.7 = (bf16[384,512]{1,0:T(8,128)(2,1)}, bf16[384,512]{1,0:T(8,128)(2,1)S(1)}, u32[]{:S(2)}) copy-start(bf16[384,512]{1,0:T(8,128)(2,1)S(1)} %collective-permute-done.1) | copy-start | bytes 1179652
  182.8 61.7 %collective-permute-start.2 = (bf16[384,3584]{1,0:T(8,128)(2,1)}, bf16[384,3584]{1,0:T(8,128)(2,1)}, u32[]{:S(2)}, u32[]{:S(2)}) collective-permute-start(bf16[384,3584]{1,0:T(8,128)(2,1)} %get-tuple-element.26), channel_id=1, source_target_pairs={{0,16},{16,0},{1,17},{17,1},{2,18},{18,2},{3,19},{19,3},{4,20},{20... | collective-permute-start | bytes 8257544 | tf_op jit(solution)/shard_map/ppermute | solution.py:16
  202.4 91.1 %all-gather.11.cloned.1.call-start = ((), (), s32[]{:S(2)}) async-start(), calls=%async_computation.6 | async-start | bytes 1966080 | tf_op jit(solution)/shard_map/all_gather | solution.py:89
  202.6 43.4 %copy-start.5 = (bf16[384,2048]{1,0:T(8,128)(2,1)S(1)}, bf16[384,2048]{1,0:T(8,128)(2,1)}, u32[]{:S(2)}) copy-start(bf16[384,2048]{1,0:T(8,128)(2,1)} %constant_dynamic-slice_fusion.1) | copy-start | bytes 4718596
  244.5 13.1 %collective-permute-start.3 = (bf16[384,512]{1,0:T(8,128)(2,1)}, bf16[384,512]{1,0:T(8,128)(2,1)S(1)}, u32[]{:S(2)}, u32[]{:S(2)}) collective-permute-start(bf16[384,512]{1,0:T(8,128)(2,1)} %constant_dynamic-slice_fusion.2), channel_id=1, source_target_pairs={{0,16},{16,0},{1,17},{17,1},{2,18},{18,2},{3,19},{19,3},{4,20},{20... | collective-permute-start | bytes 1179656 | tf_op jit(solution)/shard_map/ppermute | solution.py:16
  257.6 0.7 copy-start.8
  267.4 4.7 %copy-start.3 = (bf16[384,2048]{1,0:T(8,128)(2,1)S(1)}, bf16[384,2048]{1,0:T(8,128)(2,1)}, u32[]{:S(2)}) copy-start(bf16[384,2048]{1,0:T(8,128)(2,1)} %all-gather.7.cloned.1.call-done) | copy-start | bytes 4718596
  272.1 21.4 %copy-start.4 = (bf16[384,2048]{1,0:T(8,128)(2,1)S(1)}, bf16[384,2048]{1,0:T(8,128)(2,1)}, u32[]{:S(2)}) copy-start(bf16[384,2048]{1,0:T(8,128)(2,1)} %all-gather.7.cloned.1.call-done) | copy-start | bytes 4718596
  282.7 62.9 %collective-permute-start.4 = (bf16[384,3584]{1,0:T(8,128)(2,1)}, bf16[384,3584]{1,0:T(8,128)(2,1)}, u32[]{:S(2)}, u32[]{:S(2)}) collective-permute-start(bf16[384,3584]{1,0:T(8,128)(2,1)} %fusion.16), channel_id=1, source_target_pairs={{0,16},{16,0},{1,17},{17,1},{2,18},{18,2},{3,19},{19,3},{4,20},{20... | collective-permute-start | bytes 8257544 | tf_op jit(solution)/shard_map/ppermute | solution.py:16
  293.5 3.0 copy-start.2
  296.5 14.3 %copy-start.6 = (bf16[384,2048]{1,0:T(8,128)(2,1)S(1)}, bf16[384,2048]{1,0:T(8,128)(2,1)}, u32[]{:S(2)}) copy-start(bf16[384,2048]{1,0:T(8,128)(2,1)} %all-gather.11.cloned.1.call-done) | copy-start | bytes 4718596
  310.9 99.6 %slice-start = ((s8[5505024]{0:T(1024)(128)(4,1)}), s8[4194304]{0:T(1024)(128)(4,1)S(1)}, s32[]{:S(2)}) async-start(s8[5505024]{0:T(1024)(128)(4,1)} %bitcast.70), calls=%async_computation.7 | async-start | bytes 8388608
  310.9 99.6 %slice-start.2 = ((s8[11010048]{0:T(1024)(128)(4,1)}), s8[4194304]{0:T(1024)(128)(4,1)S(1)}, s32[]{:S(2)}) async-start(s8[11010048]{0:T(1024)(128)(4,1)} %bitcast.72), calls=%async_computation.9 | async-start | bytes 8388608
  310.9 99.6 %slice-start.3 = ((s8[11010048]{0:T(1024)(128)(4,1)}), s8[4194304]{0:T(1024)(128)(4,1)S(1)}, s32[]{:S(2)}) async-start(s8[11010048]{0:T(1024)(128)(4,1)} %bitcast.72), calls=%async_computation.10 | async-start | bytes 8388608
  321.5 89.0 %slice-start.1 = ((s8[5505024]{0:T(1024)(128)(4,1)}), s8[1310720]{0:T(1024)(128)(4,1)S(1)}, s32[]{:S(2)}) async-start(s8[5505024]{0:T(1024)(128)(4,1)} %bitcast.70), calls=%async_computation.8 | async-start | bytes 2621440
  321.5 89.0 %slice-start.4 = ((s8[11010048]{0:T(1024)(128)(4,1)}), s8[2621440]{0:T(1024)(128)(4,1)S(1)}, s32[]{:S(2)}) async-start(s8[11010048]{0:T(1024)(128)(4,1)} %bitcast.72), calls=%async_computation.11 | async-start | bytes 5242880
  321.5 80.7 %collective-permute-start.5 = (bf16[384,3584]{1,0:T(8,128)(2,1)}, bf16[384,3584]{1,0:T(8,128)(2,1)}, u32[]{:S(2)}, u32[]{:S(2)}) collective-permute-start(bf16[384,3584]{1,0:T(8,128)(2,1)} %fusion.19), channel_id=1, source_target_pairs={{0,16},{16,0},{1,17},{17,1},{2,18},{18,2},{3,19},{19,3},{4,20},{20... | collective-permute-start | bytes 8257544 | tf_op jit(solution)/shard_map/ppermute | solution.py:16
  410.6 32.5 %copy-start.10 = (s32[256,1]{0,1:T(1,128)S(1)}, s32[256,1]{0,1:T(1,128)}, u32[]{:S(2)}) copy-start(s32[256,1]{0,1:T(1,128)} %copy-done.9) | copy-start | bytes 3076
  410.6 32.5 %copy-start.12 = (s32[256,1]{0,1:T(1,128)S(1)}, s32[256,1]{0,1:T(1,128)}, u32[]{:S(2)}) copy-start(s32[256,1]{0,1:T(1,128)} %copy-done.11) | copy-start | bytes 3076
  410.6 33.4 %copy-start.1 = (bf16[256,1024]{1,0:T(8,128)(2,1)S(1)}, bf16[256,1024]{1,0:T(8,128)(2,1)}, u32[]{:S(2)}) copy-start(bf16[256,1024]{1,0:T(8,128)(2,1)} %param.6) | copy-start | bytes 1572868
Sparse Core Ops, SparseCore 0:
  47.4 63.7 all-gather.4
  113.3 62.1 all-gather.8
  202.5 34.8 all-gather.6
  258.5 34.9 all-gather.10

commit v4 on v2

--- a/solution.py
+++ b/solution.py
@@ -39,6 +39,10 @@
         )
     gate_send = jnp.sum(gate_table, axis=0).astype(jnp.bfloat16).reshape(expert_count, capacity)
 
+    local_weight = down_weight[0]
+    units = local_weight.shape[0]
+    moved = units // 4 // 16 * 16
+
     gate_float = gate_preact[0].astype(jnp.float32)
     up_float = up_preact[0].astype(jnp.float32)
     active, slope = silu_parts(gate_float)
@@ -60,6 +64,7 @@
     gate_column = gate_bf16.astype(jnp.float32)[:, None]
     other_gates = swap_dp(gate_bf16)
     fragment = lax.all_gather(narrow_rows, "tensor", axis=1, tiled=True)
+    fragment, hidden_other = lax.optimization_barrier((fragment, hidden_other))
 
     width = fragment.shape[1]
     half = width // 2
@@ -69,20 +74,26 @@
         fragment, (1 - replica) * half + part * piece, piece, axis=1
     )
     other_piece = swap_dp(send_rows)
+    weight_rest, other_piece = lax.optimization_barrier((local_weight[:moved], other_piece))
+    weight_moved = swap_dp(weight_rest)
     other_rows = lax.all_gather(other_piece, "tensor", axis=1, tiled=True)
     hidden_other, other_rows, other_gates = lax.optimization_barrier(
         (hidden_other, other_rows, other_gates)
     )
     other_gates = other_gates.astype(jnp.float32)[:, None]
 
-    local_weight = down_weight[0]
     partial_other = lax.dot_general(
-        other_rows, local_weight, contract_cols, preferred_element_type=jnp.float32
+        other_rows, local_weight[moved:], contract_cols, preferred_element_type=jnp.float32
     )
-    partial_back = swap_dp(partial_other.astype(PARTIAL_DTYPE)).astype(jnp.float32)
+    weight_moved, partial_send = lax.optimization_barrier(
+        (weight_moved, partial_other.astype(PARTIAL_DTYPE))
+    )
+    partial_back = swap_dp(partial_send).astype(jnp.float32)
     partial_own = lax.dot_general(
         own_rows, local_weight, contract_cols, preferred_element_type=jnp.float32
     )
+    far_rows = lax.dynamic_slice_in_dim(fragment, (1 - replica) * half, half, axis=1)
+    near = lax.dot_general(far_rows, weight_moved, contract_cols, preferred_element_type=jnp.float32)
 
     scaled_own = (gate_column * own_rows.astype(jnp.float32)).astype(jnp.bfloat16)
     scaled_other = (other_gates * other_rows.astype(jnp.float32)).astype(jnp.bfloat16)
@@ -95,10 +106,10 @@
     down_grad = (rounded_own.astype(jnp.float32) + rounded_other.astype(jnp.float32)).astype(
         jnp.bfloat16
     )
-    partial_back, partial_own, down_grad = lax.optimization_barrier(
-        (partial_back, partial_own, down_grad)
+    partial_back, partial_own, near, down_grad = lax.optimization_barrier(
+        (partial_back, partial_own, near, down_grad)
     )
-    upstream = partial_own + partial_back
+    upstream = partial_own + jnp.concatenate((near, partial_back), axis=1)
 
     score = jnp.sum(hidden.astype(jnp.float32) * upstream, axis=1)
     hidden_grad = gate_column * upstream

time: 433 us -> 432 us (level)
  waiting for transfers between devices: 240 us -> 233 us
  local copies, waits for them, and re-layouts: 4.71 us -> 9.64 us
    all_gather x1, waiting for transfers between devices: 114 us -> 0.01 us  [local(): fragment = lax.all_gather(narrow_rows, 'tensor', axis=1, tiled=True)]
    ppermute x4 -> x5, waiting for transfers between devices: 102 us -> 210 us  [swap_dp(): return lax.ppermute(value, 'dp', perm=[(0, 1), (1, 0)])]
    slice x1 -> x2, local copies, waits for them, and re-layouts: 0.22 us -> 4.69 us  [the longest x1 4.48 us: local(): local_weight[:moved]]
    dot_general x1 -> x2, matrix products: 19.4 us -> 21.1 us  [the longest x1 15.4 us: local(): lax.dot_general(other_rows, local_weight[moved:], contract_cols, preferre...]
  transfers between devices with their start and end apart: 7 -> 8, of which waited for: 5 -> 6; matrix products, arithmetic and copies ran while one was open for 17% -> 22% of each run, Pallas kernels for 0% -> 0%
where the time goes in v4:
time: 432 us; the launch traced here: 431 us
  waiting for transfers between devices  233 us (54%)
  matrix products  73.9 us (17%)
  other arithmetic  47.5 us (11%)
  blocking collectives  42.2 us (10%)
  between operations  14.2 us (3%)
  starting transfers between devices  10.4 us (2%)
  local copies, waits for them, and re-layouts  9.64 us (2%)
    ppermute x5, waiting for transfers between devices, swap_dp(): return lax.ppermute(value, 'dp', perm=[(0, 1), (1, 0)])  210 us
    all_to_all x1, blocking collectives, local(): lax.all_to_all(outgoing, 'expert', split_axis=0, concat_axis=0, tiled=True)  24.2 us
    all_gather x1, waiting for transfers between devices, local(): other_rows = lax.all_gather(other_piece, 'tensor', axis=1, tiled=True)  19.5 us
    dot_general x1, matrix products, local(): lax.dot_general(own_rows, local_weight, contract_cols, preferred_element_...  18.6 us
    dot_general x1, matrix products, local(): lax.dot_general(hidden_other, scaled_other, contract_rows, preferred_elem...  16.9 us
    dot_general x1, matrix products, local(): lax.dot_general(hidden, scaled_own, contract_rows, preferred_element_type...  16.5 us
    broadcast_in_dim x1, other arithmetic, local(): return (gate_grad[None], up_grad[None], down_grad[None], router_grad)  16.2 us
    convert_element_type x1, other arithmetic, local(): (rounded_own.astype(jnp.float32) + rounded_other.astype(jnp.float32)).ast...  15.6 us
  transfers between devices with their start and end apart: 8, of which 6 were waited for; matrix products, arithmetic and copies ran while one was open for 22% of the time, Pallas kernels for 0%

profile of v4, /device:TPU:0, one launch (start us, length us, event | category | flops | bytes accessed | tf_op | source)
XLA Modules:
  0.0 431.1 jit_solution(2947618288941008345)
XLA Ops:
  7.2 0.0 copy-start
  7.2 0.0 all-gather.3.cloned.1.call-start
  7.2 0.9 copy.32
  8.1 0.1 eq.59
  8.2 0.1 eq.55
  8.4 1.2 reduce-window.6
  9.6 0.2 slice_reduce_fusion
  9.8 0.2 reduce-window.9
  10.0 0.1 add_bitcast_fusion
  10.1 0.1 reduce_sum.48
  10.3 0.1 copy.34
  10.3 0.7 multiply_add_fusion
  11.1 0.8 slice_convert_fusion.1
  11.8 0.2 select_reduce_fusion.2
  12.0 0.1 convert_element_type.95
  12.1 0.0 copy-done
  12.1 0.8 convolution_convert_fusion.2
  12.9 8.9 %fusion.2 = bf16[768,3584]{1,0:T(8,128)(2,1)} fusion(bf16[1,768,3584]{2,1,0:T(8,128)(2,1)} %param.10, bf16[1,768,3584]{2,1,0:T(8,128)(2,1)} %param.9), kind=kLoop, calls=%fused_computation.10 | loop fusion | flops 22020096 | bytes 16515072 | tf_op jit(solution)/shard_map/convert_element_type | solution.py:49
  21.7 24.2 %all_to_all.23 = bf16[4,192,1024]{2,1,0:T(8,128)(2,1)} all-to-all(bf16[4,192,1024]{2,1,0:T(8,128)(2,1)S(1)} %bitcast.70), channel_id=1, replica_groups=mesh['dp'=2,'expert'=4,'tensor'=4] {'expert'}, dimensions={0} | all-to-all | bytes 3145728 | tf_op jit(solution)/shard_map/all_to_all | solution.py:60
  46.0 0.0 all-gather.3.cloned.1.call-update
  46.0 0.0 all-gather.5.cloned.1.call-start
  46.0 2.0 collective-permute-start
  48.1 118.6 %collective-permute-done = bf16[768,3584]{1,0:T(8,128)(2,1)} collective-permute-done((bf16[768,3584]{1,0:T(8,128)(2,1)}, bf16[768,3584]{1,0:T(8,128)(2,1)}, u32[]{:S(2)}, u32[]{:S(2)}) %collective-permute-start) | collective-permute-done | bytes 5505056 | tf_op jit(solution)/shard_map/ppermute | solution.py:15
  166.7 1.2 constant_dynamic-slice_fusion
  167.9 1.8 collective-permute-start.1
  169.7 4.5 %slice_bitcast_fusion = bf16[896,2048]{1,0:T(8,128)(2,1)} fusion(bf16[1,3584,2048]{2,1,0:T(8,128)(2,1)} %param.11), kind=kLoop, calls=%fused_computation.29 | loop fusion | bytes 7340032 | tf_op jit(solution)/shard_map/slice | solution.py:77
  174.2 12.0 %collective-permute-done.1 = bf16[768,512]{1,0:T(8,128)(2,1)S(1)} collective-permute-done((bf16[768,512]{1,0:T(8,128)(2,1)S(1)}, bf16[768,512]{1,0:T(8,128)(2,1)S(1)}, u32[]{:S(2)}, u32[]{:S(2)}) %collective-permute-start.1) | collective-permute-done | bytes 786464 | tf_op jit(solution)/shard_map/ppermute | solution.py:15
  186.2 0.9 copy-done.3
  187.1 0.0 all-gather.5.cloned.1.call-update
  187.1 0.6 copy.35
  187.7 3.4 all-to-all-start
  191.1 3.6 all-to-all-done
  194.7 0.1 reshape.64
  194.8 1.5 collective-permute-start.3
  196.3 18.6 %fusion = f32[768,3584]{1,0:T(8,128)} fusion(bf16[1,3584,2048]{2,1,0:T(8,128)(2,1)} %param.11, bf16[768,4096]{1,0:T(8,128)(2,1)} %all-gather.3.cloned.1.call-done, s32[]{:T(128)S(6)} %select_n.35), kind=kOutput, calls=%fused_computation.6 | convolution fusion | flops 11274289152 | bytes 28835844 | tf_op jit(solution)/shard_map/dot_general | solution.py:92
  214.9 0.8 collective-permute-start.2
  215.7 0.0 slice-done.2
  215.7 0.0 slice-done.3
  215.7 16.5 %convolution_convert_fusion.1 = bf16[3584,2048]{1,0:T(8,128)(2,1)} fusion(bf16[768,3584]{1,0:T(8,128)(2,1)S(1)} %bitcast.67, f32[768]{0:T(1024)S(1)} %convert_element_type.96, bf16[768,4096]{1,0:T(8,128)(2,1)} %all-gather.3.cloned.1.call-done, s32[]{:T(128)S(6)} %select_n.35), kind=kOutput, calls=%fused_computation.5 | convolution fusion | flops 11286347776 | bytes 23333892 | tf_op jit(solution)/shard_map/dot_general | solution.py:100
  232.2 0.0 collective-permute-done.3
  232.2 19.5 %all-gather.5.cloned.1.call-done = bf16[768,2048]{1,0:T(8,128)(2,1)} async-done(((bf16[768,512]{1,0:T(8,128)(2,1)}), bf16[768,2048]{1,0:T(8,128)(2,1)}) %all-gather.5.cloned.1.call-update) | async-done | bytes 3145744 | tf_op jit(solution)/shard_map/all_gather | solution.py:79
  251.7 15.4 %fusion.15 = bf16[768,2688]{1,0:T(8,128)(2,1)} fusion(bf16[768,2048]{1,0:T(8,128)(2,1)} %all-gather.5.cloned.1.call-done, bf16[1,3584,2048]{2,1,0:T(8,128)(2,1)} %param.11), kind=kOutput, calls=%fused_computation.28 | convolution fusion | flops 8457781248 | bytes 18284544 | tf_op jit(solution)/shard_map/dot_general | solution.py:85
  267.1 28.9 %collective-permute-done.2 = bf16[896,2048]{1,0:T(8,128)(2,1)} collective-permute-done((bf16[896,2048]{1,0:T(8,128)(2,1)}, bf16[896,2048]{1,0:T(8,128)(2,1)}, u32[]{:S(2)}, u32[]{:S(2)}) %collective-permute-start.2) | collective-permute-done | bytes 3670048 | tf_op jit(solution)/shard_map/ppermute | solution.py:15
  296.1 0.8 collective-permute-start.4
  296.9 0.0 copy-done.4
  296.9 16.9 %convolution_convert_fusion = bf16[3584,2048]{1,0:T(8,128)(2,1)} fusion(bf16[768,3584]{1,0:T(8,128)(2,1)} %collective-permute-done, bf16[768,2048]{1,0:T(8,128)(2,1)S(1)} %copy-done.4, f32[768]{0:T(1024)S(1)} %convert_element_type.103), kind=kOutput, calls=%fused_computation.4 | convolution fusion | flops 11286347776 | bytes 23333888 | tf_op jit(solution)/shard_map/dot_general | solution.py:101
  313.8 0.0 slice-done.4
  313.8 0.0 slice-done.5
  313.8 0.0 slice-start
  313.9 5.7 %fusion.20 = f32[768,896]{1,0:T(8,128)S(1)} fusion(bf16[896,2048]{1,0:T(8,128)(2,1)} %collective-permute-done.2, bf16[768,4096]{1,0:T(8,128)(2,1)S(1)} %bitcast.72, s32[]{:T(128)S(6)} %select_n.36), kind=kOutput, calls=%fused_computation.32 | convolution fusion | flops 2818572288 | bytes 9568260 | tf_op jit(solution)/shard_map/dot_general | solution.py:96
  319.6 0.5 copy-done.2
  320.1 15.6 %add_convert_fusion = bf16[3584,2048]{1,0:T(8,128)(2,1)} fusion(bf16[3584,2048]{1,0:T(8,128)(2,1)} %convolution_convert_fusion, bf16[3584,2048]{1,0:T(8,128)(2,1)S(1)} %copy-done.2), kind=kLoop, calls=%fused_computation | loop fusion | flops 29360128 | bytes 44040192 | tf_op jit(solution)/shard_map/convert_element_type | solution.py:106
  335.7 50.5 %collective-permute-done.4 = bf16[768,2688]{1,0:T(8,128)(2,1)} collective-permute-done((bf16[768,2688]{1,0:T(8,128)(2,1)}, bf16[768,2688]{1,0:T(8,128)(2,1)}, u32[]{:S(2)}, u32[]{:S(2)}) %collective-permute-start.4) | collective-permute-done | bytes 4128800 | tf_op jit(solution)/shard_map/ppermute | solution.py:15
  386.2 2.7 convert_element_type.98
  388.9 0.0 slice-done
  388.9 0.0 slice-done.1
  388.9 0.0 copy-start.1
  388.9 16.2 %fusion.13 = (bf16[1,768,3584]{2,1,0:T(8,128)(2,1)}, bf16[1,768,3584]{2,1,0:T(8,128)(2,1)}, f32[768]{0:T(1024)S(1)}) fusion(f32[768]{0:T(1024)S(1)} %convert_element_type.96, bf16[1,768,3584]{2,1,0:T(8,128)(2,1)S(1)} %bitcast.65, f32[768,3584]{1,0:T(8,128)} %fusion, f32[768,2688]{1,0:T(8,128)S(1)} %convert_element_type.98, f32[768,896]{1,0:T(8,128)S(1)} %fusion.20, ...), kind=kLoop, calls=%fused_computation.26 | loop fusion | flops 57801984 | bytes 49551360 | tf_op jit(solution)/shard_map/broadcast_in_dim | solution.py:134
  405.1 0.1 all_to_all.18
  405.2 11.9 %psum.7 = f32[4,1,192]{2,1,0:T(1,128)S(1)} all-reduce(f32[4,1,192]{2,1,0:T(1,128)S(1)} %all_to_all.18), channel_id=1, replica_groups=mesh['dp'=2,'expert'=4,'tensor'=4] {'tensor'}, use_global_device_ids=true, to_apply=%region_5.6 | all-reduce | flops 768 | bytes 6144 | tf_op jit(solution)/shard_map/psum | solution.py:118
  417.1 6.1 %all_to_all.24 = f32[4,1,192]{2,1,0:T(1,128)S(1)} all-to-all(f32[4,1,192]{2,1,0:T(1,128)S(1)} %psum.7), channel_id=1, replica_groups=mesh['dp'=2,'expert'=4,'tensor'=4] {'expert'}, dimensions={0} | all-to-all | bytes 6144 | tf_op jit(solution)/shard_map/all_to_all | solution.py:119
  423.2 0.1 broadcast_in_dim.76
  423.3 0.3 select_reduce_fusion.1
  423.6 0.6 pad_maximum_fusion
  (20 shorter events, 0.1 us)
Async XLA Ops:
  7.2 5.0 %copy-start = (bf16[256,1024]{1,0:T(8,128)(2,1)S(1)}, bf16[256,1024]{1,0:T(8,128)(2,1)}, u32[]{:S(2)}) copy-start(bf16[256,1024]{1,0:T(8,128)(2,1)} %param.6) | copy-start | bytes 1572868
  7.2 159.5 %all-gather.3.cloned.1.call-start = ((), (), s32[]{:S(2)}) async-start(), calls=%async_computation.3 | async-start | bytes 7864320 | tf_op jit(solution)/shard_map/all_gather | solution.py:66
  46.0 205.7 %all-gather.5.cloned.1.call-start = ((), (), s32[]{:S(2)}) async-start(), calls=%async_computation.4 | async-start | bytes 3932160 | tf_op jit(solution)/shard_map/all_gather | solution.py:79
  46.0 120.7 %collective-permute-start = (bf16[768,3584]{1,0:T(8,128)(2,1)}, bf16[768,3584]{1,0:T(8,128)(2,1)}, u32[]{:S(2)}, u32[]{:S(2)}) collective-permute-start(bf16[768,3584]{1,0:T(8,128)(2,1)} %fusion.2), channel_id=1, source_target_pairs={{0,16},{16,0},{1,17},{17,1},{2,18},{18,2},{3,19},{19,3},{4,20},{20... | collective-permute-start | bytes 16515080 | tf_op jit(solution)/shard_map/ppermute | solution.py:15
  167.9 18.3 %collective-permute-start.1 = (bf16[768,512]{1,0:T(8,128)(2,1)S(1)}, bf16[768,512]{1,0:T(8,128)(2,1)S(1)}, u32[]{:S(2)}, u32[]{:S(2)}) collective-permute-start(bf16[768,512]{1,0:T(8,128)(2,1)S(1)} %constant_dynamic-slice_fusion), channel_id=1, source_target_pairs={{0,16},{16,0},{1,17},{17,1},{2,18},{18,2},{3,19},{19,3},{4,20},{20... | collective-permute-start | bytes 2359304 | tf_op jit(solution)/shard_map/ppermute | solution.py:15
  169.7 46.0 %slice-start.2 = ((s8[5505024]{0:T(1024)(128)(4,1)}), s8[1310720]{0:T(1024)(128)(4,1)S(1)}, s32[]{:S(2)}) async-start(s8[5505024]{0:T(1024)(128)(4,1)} %bitcast.66), calls=%async_computation.7 | async-start | bytes 2621440
  186.2 0.9 copy-start.3
  187.7 7.0 %all-to-all-start = ((bf16[4,1,192]{2,1,0:T(2,128)(2,1)}), bf16[4,1,192]{2,1,0:T(2,128)(2,1)S(1)}, u32[]{:S(2)}, u32[]{:S(2)}) async-start(bf16[4,1,192]{2,1,0:T(2,128)(2,1)} %copy.35), calls=%async_computation | async-start | bytes 8192 | tf_op jit(solution)/shard_map/all_to_all | solution.py:59
  194.8 37.4 %collective-permute-start.3 = (bf16[768]{0:T(1024)(128)(2,1)S(1)}, bf16[768]{0:T(1024)(128)(2,1)S(1)}, u32[]{:S(2)}, u32[]{:S(2)}) collective-permute-start(bf16[768]{0:T(1024)(128)(2,1)S(1)} %reshape.64), channel_id=1, source_target_pairs={{0,16},{16,0},{1,17},{17,1},{2,18},{18,2},{3,19},{19,3},{4,20},{20... | collective-permute-start | bytes 4616 | tf_op jit(solution)/shard_map/ppermute | solution.py:15
  196.3 19.4 %slice-start.3 = ((s8[5505024]{0:T(1024)(128)(4,1)}), s8[4194304]{0:T(1024)(128)(4,1)S(1)}, s32[]{:S(2)}) async-start(s8[5505024]{0:T(1024)(128)(4,1)} %bitcast.66), calls=%async_computation.8 | async-start | bytes 8388608
  214.9 81.2 %collective-permute-start.2 = (bf16[896,2048]{1,0:T(8,128)(2,1)}, bf16[896,2048]{1,0:T(8,128)(2,1)}, u32[]{:S(2)}, u32[]{:S(2)}) collective-permute-start(bf16[896,2048]{1,0:T(8,128)(2,1)} %slice_bitcast_fusion), channel_id=1, source_target_pairs={{0,16},{16,0},{1,17},{17,1},{2,18},{18,2},{3,19},{19,3},{4,20},{20... | collective-permute-start | bytes 11010056 | tf_op jit(solution)/shard_map/ppermute | solution.py:15
  251.7 45.2 %copy-start.4 = (bf16[768,2048]{1,0:T(8,128)(2,1)S(1)}, bf16[768,2048]{1,0:T(8,128)(2,1)}, u32[]{:S(2)}) copy-start(bf16[768,2048]{1,0:T(8,128)(2,1)} %all-gather.5.cloned.1.call-done) | copy-start | bytes 9437188
  251.7 62.1 %slice-start.4 = ((s8[6291456]{0:T(1024)(128)(4,1)}), s8[2097152]{0:T(1024)(128)(4,1)S(1)}, s32[]{:S(2)}) async-start(s8[6291456]{0:T(1024)(128)(4,1)} %bitcast.71), calls=%async_computation.9 | async-start | bytes 4194304
  267.1 46.7 %slice-start.5 = ((s8[6291456]{0:T(1024)(128)(4,1)}), s8[4194304]{0:T(1024)(128)(4,1)S(1)}, s32[]{:S(2)}) async-start(s8[6291456]{0:T(1024)(128)(4,1)} %bitcast.71), calls=%async_computation.10 | async-start | bytes 8388608
  296.1 90.1 %collective-permute-start.4 = (bf16[768,2688]{1,0:T(8,128)(2,1)}, bf16[768,2688]{1,0:T(8,128)(2,1)}, u32[]{:S(2)}, u32[]{:S(2)}) collective-permute-start(bf16[768,2688]{1,0:T(8,128)(2,1)} %fusion.15), channel_id=1, source_target_pairs={{0,16},{16,0},{1,17},{17,1},{2,18},{18,2},{3,19},{19,3},{4,20},{20... | collective-permute-start | bytes 12386312 | tf_op jit(solution)/shard_map/ppermute | solution.py:15
  313.8 6.3 %copy-start.2 = (bf16[3584,2048]{1,0:T(8,128)(2,1)S(1)}, bf16[3584,2048]{1,0:T(8,128)(2,1)}, u32[]{:S(2)}) copy-start(bf16[3584,2048]{1,0:T(8,128)(2,1)} %convolution_convert_fusion.1) | copy-start | bytes 44040196
  313.8 75.1 %slice-start = ((s8[5505024]{0:T(1024)(128)(4,1)}), s8[4194304]{0:T(1024)(128)(4,1)S(1)}, s32[]{:S(2)}) async-start(s8[5505024]{0:T(1024)(128)(4,1)} %bitcast.64), calls=%async_computation.5 | async-start | bytes 8388608
  320.1 68.8 %slice-start.1 = ((s8[5505024]{0:T(1024)(128)(4,1)}), s8[1310720]{0:T(1024)(128)(4,1)S(1)}, s32[]{:S(2)}) async-start(s8[5505024]{0:T(1024)(128)(4,1)} %bitcast.64), calls=%async_computation.6 | async-start | bytes 2621440
  388.9 35.3 %copy-start.1 = (bf16[256,1024]{1,0:T(8,128)(2,1)S(1)}, bf16[256,1024]{1,0:T(8,128)(2,1)}, u32[]{:S(2)}) copy-start(bf16[256,1024]{1,0:T(8,128)(2,1)} %param.6) | copy-start | bytes 1572868
Sparse Core Ops, SparseCore 0:
  46.1 116.1 all-gather.2
  187.2 64.4 all-gather.4

commit v5 on v4

--- a/solution.py
+++ b/solution.py
@@ -64,7 +64,9 @@
     gate_column = gate_bf16.astype(jnp.float32)[:, None]
     other_gates = swap_dp(gate_bf16)
     fragment = lax.all_gather(narrow_rows, "tensor", axis=1, tiled=True)
-    fragment, hidden_other = lax.optimization_barrier((fragment, hidden_other))
+    fragment, hidden_other, other_gates = lax.optimization_barrier(
+        (fragment, hidden_other, other_gates)
+    )
 
     width = fragment.shape[1]
     half = width // 2
@@ -77,16 +79,14 @@
     weight_rest, other_piece = lax.optimization_barrier((local_weight[:moved], other_piece))
     weight_moved = swap_dp(weight_rest)
     other_rows = lax.all_gather(other_piece, "tensor", axis=1, tiled=True)
-    hidden_other, other_rows, other_gates = lax.optimization_barrier(
-        (hidden_other, other_rows, other_gates)
-    )
+    hidden_other, other_rows = lax.optimization_barrier((hidden_other, other_rows))
     other_gates = other_gates.astype(jnp.float32)[:, None]
 
     partial_other = lax.dot_general(
         other_rows, local_weight[moved:], contract_cols, preferred_element_type=jnp.float32
     )
-    weight_moved, partial_send = lax.optimization_barrier(
-        (weight_moved, partial_other.astype(PARTIAL_DTYPE))
+    weight_moved, partial_send, own_rows = lax.optimization_barrier(
+        (weight_moved, partial_other.astype(PARTIAL_DTYPE), own_rows)
     )
     partial_back = swap_dp(partial_send).astype(jnp.float32)
     partial_own = lax.dot_general(

time: 432 us -> 402 us (0.931)
  waiting for transfers between devices: 233 us -> 201 us
    ppermute x5, waiting for transfers between devices: 210 us -> 142 us  [swap_dp(): return lax.ppermute(value, 'dp', perm=[(0, 1), (1, 0)])]
    all_gather x1, waiting for transfers between devices: 19.5 us -> 59 us  [local(): other_rows = lax.all_gather(other_piece, 'tensor', axis=1, tiled=True)]
    all_to_all x0 -> x1, blocking collectives: none -> 6.11 us  [local(): lax.all_to_all(gate_send, 'expert', split_axis=0, concat_axis=0, tiled=True)]
  transfers between devices with their start and end apart: 8 -> 7, of which waited for: 6 -> 4; matrix products, arithmetic and copies ran while one was open for 22% -> 24% of each run, Pallas kernels for 0% -> 0%
where the time goes in v5:
time: 402 us; the launch traced here: 401 us
  waiting for transfers between devices  201 us (50%)
  matrix products  71.9 us (18%)
  other arithmetic  47.4 us (12%)
  blocking collectives  46.2 us (11%)
  between operations  14.2 us (4%)
  local copies, waits for them, and re-layouts  13 us (3%)
  starting transfers between devices  7.02 us (2%)
    ppermute x5, waiting for transfers between devices, swap_dp(): return lax.ppermute(value, 'dp', perm=[(0, 1), (1, 0)])  142 us
    all_gather x1, waiting for transfers between devices, local(): other_rows = lax.all_gather(other_piece, 'tensor', axis=1, tiled=True)  59 us
    all_to_all x1, blocking collectives, local(): lax.all_to_all(outgoing, 'expert', split_axis=0, concat_axis=0, tiled=True)  24.2 us
    dot_general x1, matrix products, local(): lax.dot_general(hidden_other, scaled_other, contract_rows, preferred_elem...  17.5 us
    dot_general x1, matrix products, local(): lax.dot_general(own_rows, local_weight, contract_cols, preferred_element_...  17.3 us
    broadcast_in_dim x1, other arithmetic, local(): return (gate_grad[None], up_grad[None], down_grad[None], router_grad)  16.2 us
    convert_element_type x1, other arithmetic, local(): (rounded_own.astype(jnp.float32) + rounded_other.astype(jnp.float32)).ast...  15.6 us
    dot_general x1, matrix products, local(): lax.dot_general(other_rows, local_weight[moved:], contract_cols, preferre...  15.4 us
  transfers between devices with their start and end apart: 7, of which 4 were waited for; matrix products, arithmetic and copies ran while one was open for 24% of the time, Pallas kernels for 0%

profile of v5, /device:TPU:0, one launch (start us, length us, event | category | flops | bytes accessed | tf_op | source)
XLA Modules:
  0.0 401.2 jit_solution(2342481063395187698)
XLA Ops:
  7.2 0.0 copy-start
  7.2 0.0 all-gather.3.cloned.1.call-start
  7.2 0.9 copy.32
  8.1 0.1 eq.59
  8.2 0.1 eq.55
  8.4 1.2 reduce-window.6
  9.6 0.2 slice_reduce_fusion
  9.8 0.2 reduce-window.9
  10.0 0.1 add_bitcast_fusion
  10.1 0.1 reduce_sum.48
  10.3 0.1 copy.34
  10.3 0.7 multiply_add_fusion
  11.1 0.8 slice_convert_fusion.1
  11.8 0.2 select_reduce_fusion.2
  12.0 0.1 convert_element_type.95
  12.1 0.0 copy-done
  12.1 0.8 convolution_convert_fusion.2
  12.9 8.9 %fusion.2 = bf16[768,3584]{1,0:T(8,128)(2,1)} fusion(bf16[1,768,3584]{2,1,0:T(8,128)(2,1)} %param.10, bf16[1,768,3584]{2,1,0:T(8,128)(2,1)} %param.9), kind=kLoop, calls=%fused_computation.10 | loop fusion | flops 22020096 | bytes 16515072 | tf_op jit(solution)/shard_map/convert_element_type | solution.py:49
  21.7 24.2 %all_to_all.23 = bf16[4,192,1024]{2,1,0:T(8,128)(2,1)} all-to-all(bf16[4,192,1024]{2,1,0:T(8,128)(2,1)S(1)} %bitcast.71), channel_id=1, replica_groups=mesh['dp'=2,'expert'=4,'tensor'=4] {'expert'}, dimensions={0} | all-to-all | bytes 3145728 | tf_op jit(solution)/shard_map/all_to_all | solution.py:60
  46.0 0.0 all-gather.3.cloned.1.call-update
  46.0 0.0 all-gather.5.cloned.1.call-start
  46.0 2.1 collective-permute-start
  48.1 6.1 %all_to_all.24 = bf16[4,1,192]{2,1,0:T(2,128)(2,1)S(1)} all-to-all(bf16[4,1,192]{2,1,0:T(2,128)(2,1)S(1)} %copy.35), channel_id=1, replica_groups=mesh['dp'=2,'expert'=4,'tensor'=4] {'expert'}, dimensions={0} | all-to-all | bytes 3072 | tf_op jit(solution)/shard_map/all_to_all | solution.py:59
  54.3 0.1 reshape.64
  54.3 0.0 collective-permute-start.1
  54.4 112.4 %collective-permute-done.1 = bf16[768]{0:T(1024)(128)(2,1)S(1)} collective-permute-done((bf16[768]{0:T(1024)(128)(2,1)S(1)}, bf16[768]{0:T(1024)(128)(2,1)S(1)}, u32[]{:S(2)}, u32[]{:S(2)}) %collective-permute-start.1) | collective-permute-done | bytes 1568 | tf_op jit(solution)/shard_map/ppermute | solution.py:15
  166.7 0.0 collective-permute-done
  166.7 0.0 all-gather.3.cloned.1.call-done
  166.7 1.2 constant_dynamic-slice_fusion.1
  167.9 1.8 collective-permute-start.2
  169.7 4.4 %slice_bitcast_fusion = bf16[896,2048]{1,0:T(8,128)(2,1)} fusion(bf16[1,3584,2048]{2,1,0:T(8,128)(2,1)} %param.11), kind=kLoop, calls=%fused_computation.29 | loop fusion | bytes 7340032 | tf_op jit(solution)/shard_map/slice | solution.py:79
  174.1 12.2 %collective-permute-done.2 = bf16[768,512]{1,0:T(8,128)(2,1)S(1)} collective-permute-done((bf16[768,512]{1,0:T(8,128)(2,1)S(1)}, bf16[768,512]{1,0:T(8,128)(2,1)S(1)}, u32[]{:S(2)}, u32[]{:S(2)}) %collective-permute-start.2) | collective-permute-done | bytes 786464 | tf_op jit(solution)/shard_map/ppermute | solution.py:15
  186.3 0.0 copy-start.4
  186.3 0.9 copy-done.4
  187.2 0.0 all-gather.5.cloned.1.call-update
  187.2 1.5 collective-permute-start.3
  188.7 4.0 %constant_dynamic-slice_fusion = bf16[768,2048]{1,0:T(8,128)(2,1)} fusion(bf16[768,4096]{1,0:T(8,128)(2,1)} %all-gather.3.cloned.1.call-done, s32[]{:T(128)S(6)} %select_n.35), kind=kLoop, calls=%fused_computation.60 | loop fusion | bytes 6291460 | tf_op jit(solution)/shard_map/dynamic_slice | solution.py:74
  192.8 59.0 %all-gather.5.cloned.1.call-done = bf16[768,2048]{1,0:T(8,128)(2,1)} async-done(((bf16[768,512]{1,0:T(8,128)(2,1)}), bf16[768,2048]{1,0:T(8,128)(2,1)}) %all-gather.5.cloned.1.call-update) | async-done | bytes 3145744 | tf_op jit(solution)/shard_map/all_gather | solution.py:81
  251.8 15.4 %fusion.15 = bf16[768,2688]{1,0:T(8,128)(2,1)} fusion(bf16[768,2048]{1,0:T(8,128)(2,1)} %all-gather.5.cloned.1.call-done, bf16[1,3584,2048]{2,1,0:T(8,128)(2,1)} %param.11), kind=kOutput, calls=%fused_computation.28 | convolution fusion | flops 8457781248 | bytes 18284544 | tf_op jit(solution)/shard_map/dot_general | solution.py:85
  267.2 0.0 collective-permute-done.3
  267.2 1.5 collective-permute-start.4
  268.7 0.0 copy-done.5
  268.7 17.5 %convolution_convert_fusion = bf16[3584,2048]{1,0:T(8,128)(2,1)} fusion(bf16[768,3584]{1,0:T(8,128)(2,1)} %collective-permute-done, bf16[768,2048]{1,0:T(8,128)(2,1)S(1)} %copy-done.5, f32[768]{0:T(1024)S(1)} %convert_element_type.103), kind=kOutput, calls=%fused_computation.4 | convolution fusion | flops 11286347776 | bytes 23333888 | tf_op jit(solution)/shard_map/dot_general | solution.py:101
  286.3 0.0 slice-done.2
  286.3 0.0 slice-done.3
  286.3 0.0 copy-done.3
  286.3 14.4 %convolution_convert_fusion.1 = bf16[3584,2048]{1,0:T(8,128)(2,1)} fusion(bf16[768,3584]{1,0:T(8,128)(2,1)S(1)} %bitcast.68, bf16[768,2048]{1,0:T(8,128)(2,1)S(1)} %copy-done.3, f32[768]{0:T(1024)S(1)} %convert_element_type.96), kind=kOutput, calls=%fused_computation.5 | convolution fusion | flops 11286347776 | bytes 23333888 | tf_op jit(solution)/shard_map/dot_general | solution.py:100
  300.7 17.3 %fusion = f32[768,3584]{1,0:T(8,128)} fusion(bf16[768,2048]{1,0:T(8,128)(2,1)S(1)} %copy-done.3, bf16[1,3584,2048]{2,1,0:T(8,128)(2,1)} %param.11), kind=kOutput, calls=%fused_computation.6 | convolution fusion | flops 11274289152 | bytes 28835840 | tf_op jit(solution)/shard_map/dot_general | solution.py:92
  317.9 6.6 %fusion.20 = f32[768,896]{1,0:T(8,128)S(1)} fusion(bf16[896,2048]{1,0:T(8,128)(2,1)} %collective-permute-done.3, bf16[768,4096]{1,0:T(8,128)(2,1)} %all-gather.3.cloned.1.call-done, s32[]{:T(128)S(6)} %select_n.36), kind=kOutput, calls=%fused_computation.32 | convolution fusion | flops 2818572288 | bytes 9568260 | tf_op jit(solution)/shard_map/dot_general | solution.py:96
  324.5 0.6 copy-done.2
  325.1 15.6 %add_convert_fusion = bf16[3584,2048]{1,0:T(8,128)(2,1)} fusion(bf16[3584,2048]{1,0:T(8,128)(2,1)S(1)} %copy-done.2, bf16[3584,2048]{1,0:T(8,128)(2,1)} %convolution_convert_fusion.1), kind=kLoop, calls=%fused_computation | loop fusion | flops 29360128 | bytes 44040192 | tf_op jit(solution)/shard_map/convert_element_type | solution.py:106
  340.7 17.8 %collective-permute-done.4 = bf16[768,2688]{1,0:T(8,128)(2,1)} collective-permute-done((bf16[768,2688]{1,0:T(8,128)(2,1)}, bf16[768,2688]{1,0:T(8,128)(2,1)}, u32[]{:S(2)}, u32[]{:S(2)}) %collective-permute-start.4) | collective-permute-done | bytes 4128800 | tf_op jit(solution)/shard_map/ppermute | solution.py:15
  358.5 2.7 convert_element_type.98
  361.2 0.0 slice-done
  361.2 0.0 slice-done.1
  361.2 0.0 copy-start.1
  361.2 16.2 %fusion.13 = (bf16[1,768,3584]{2,1,0:T(8,128)(2,1)}, bf16[1,768,3584]{2,1,0:T(8,128)(2,1)}, f32[768]{0:T(1024)S(1)}) fusion(f32[768]{0:T(1024)S(1)} %convert_element_type.96, bf16[1,768,3584]{2,1,0:T(8,128)(2,1)S(1)} %bitcast.66, f32[768,3584]{1,0:T(8,128)} %fusion, f32[768,2688]{1,0:T(8,128)S(1)} %convert_element_type.98, f32[768,896]{1,0:T(8,128)S(1)} %fusion.20, ...), kind=kLoop, calls=%fused_computation.26 | loop fusion | flops 57801984 | bytes 49551360 | tf_op jit(solution)/shard_map/broadcast_in_dim | solution.py:134
  377.4 0.1 all_to_all.18
  377.5 9.3 %psum.7 = f32[4,1,192]{2,1,0:T(1,128)S(1)} all-reduce(f32[4,1,192]{2,1,0:T(1,128)S(1)} %all_to_all.18), channel_id=1, replica_groups=mesh['dp'=2,'expert'=4,'tensor'=4] {'tensor'}, use_global_device_ids=true, to_apply=%region_5.6 | all-reduce | flops 768 | bytes 6144 | tf_op jit(solution)/shard_map/psum | solution.py:118
  386.8 6.5 %all_to_all.25 = f32[4,1,192]{2,1,0:T(1,128)S(1)} all-to-all(f32[4,1,192]{2,1,0:T(1,128)S(1)} %psum.7), channel_id=1, replica_groups=mesh['dp'=2,'expert'=4,'tensor'=4] {'expert'}, dimensions={0} | all-to-all | bytes 6144 | tf_op jit(solution)/shard_map/all_to_all | solution.py:119
  393.4 0.1 broadcast_in_dim.76
  393.4 0.3 select_reduce_fusion.1
  393.8 0.6 pad_maximum_fusion
  394.4 0.0 copy-done.1
  (17 shorter events, 0.1 us)
Async XLA Ops:
  7.2 5.0 %copy-start = (bf16[256,1024]{1,0:T(8,128)(2,1)S(1)}, bf16[256,1024]{1,0:T(8,128)(2,1)}, u32[]{:S(2)}) copy-start(bf16[256,1024]{1,0:T(8,128)(2,1)} %param.6) | copy-start | bytes 1572868
  7.2 159.6 %all-gather.3.cloned.1.call-start = ((), (), s32[]{:S(2)}) async-start(), calls=%async_computation.3 | async-start | bytes 7864320 | tf_op jit(solution)/shard_map/all_gather | solution.py:66
  46.0 205.8 %all-gather.5.cloned.1.call-start = ((), (), s32[]{:S(2)}) async-start(), calls=%async_computation.4 | async-start | bytes 3932160 | tf_op jit(solution)/shard_map/all_gather | solution.py:81
  46.0 120.7 %collective-permute-start = (bf16[768,3584]{1,0:T(8,128)(2,1)}, bf16[768,3584]{1,0:T(8,128)(2,1)}, u32[]{:S(2)}, u32[]{:S(2)}) collective-permute-start(bf16[768,3584]{1,0:T(8,128)(2,1)} %fusion.2), channel_id=1, source_target_pairs={{0,16},{16,0},{1,17},{17,1},{2,18},{18,2},{3,19},{19,3},{4,20},{20... | collective-permute-start | bytes 16515080 | tf_op jit(solution)/shard_map/ppermute | solution.py:15
  54.3 112.4 %collective-permute-start.1 = (bf16[768]{0:T(1024)(128)(2,1)S(1)}, bf16[768]{0:T(1024)(128)(2,1)S(1)}, u32[]{:S(2)}, u32[]{:S(2)}) collective-permute-start(bf16[768]{0:T(1024)(128)(2,1)S(1)} %reshape.64), channel_id=1, source_target_pairs={{0,16},{16,0},{1,17},{17,1},{2,18},{18,2},{3,19},{19,3},{4,20},{20... | collective-permute-start | bytes 4616 | tf_op jit(solution)/shard_map/ppermute | solution.py:15
  167.9 18.4 %collective-permute-start.2 = (bf16[768,512]{1,0:T(8,128)(2,1)S(1)}, bf16[768,512]{1,0:T(8,128)(2,1)S(1)}, u32[]{:S(2)}, u32[]{:S(2)}) collective-permute-start(bf16[768,512]{1,0:T(8,128)(2,1)S(1)} %constant_dynamic-slice_fusion.1), channel_id=1, source_target_pairs={{0,16},{16,0},{1,17},{17,1},{2,18},{18,2},{3,19},{19,3},{4,20},{20... | collective-permute-start | bytes 2359304 | tf_op jit(solution)/shard_map/ppermute | solution.py:15
  186.3 0.9 copy-start.4
  187.2 80.0 %collective-permute-start.3 = (bf16[896,2048]{1,0:T(8,128)(2,1)}, bf16[896,2048]{1,0:T(8,128)(2,1)}, u32[]{:S(2)}, u32[]{:S(2)}) collective-permute-start(bf16[896,2048]{1,0:T(8,128)(2,1)} %slice_bitcast_fusion), channel_id=1, source_target_pairs={{0,16},{16,0},{1,17},{17,1},{2,18},{18,2},{3,19},{19,3},{4,20},{20... | collective-permute-start | bytes 11010056 | tf_op jit(solution)/shard_map/ppermute | solution.py:15
  251.8 17.0 %copy-start.5 = (bf16[768,2048]{1,0:T(8,128)(2,1)S(1)}, bf16[768,2048]{1,0:T(8,128)(2,1)}, u32[]{:S(2)}) copy-start(bf16[768,2048]{1,0:T(8,128)(2,1)} %all-gather.5.cloned.1.call-done) | copy-start | bytes 9437188
  251.8 34.5 %slice-start.2 = ((s8[5505024]{0:T(1024)(128)(4,1)}), s8[1310720]{0:T(1024)(128)(4,1)S(1)}, s32[]{:S(2)}) async-start(s8[5505024]{0:T(1024)(128)(4,1)} %bitcast.67), calls=%async_computation.7 | async-start | bytes 2621440
  267.2 19.1 %slice-start.3 = ((s8[5505024]{0:T(1024)(128)(4,1)}), s8[4194304]{0:T(1024)(128)(4,1)S(1)}, s32[]{:S(2)}) async-start(s8[5505024]{0:T(1024)(128)(4,1)} %bitcast.67), calls=%async_computation.8 | async-start | bytes 8388608
  267.2 19.1 %copy-start.3 = (bf16[768,2048]{1,0:T(8,128)(2,1)S(1)}, bf16[768,2048]{1,0:T(8,128)(2,1)}, u32[]{:S(2)}) copy-start(bf16[768,2048]{1,0:T(8,128)(2,1)} %constant_dynamic-slice_fusion) | copy-start | bytes 9437188
  267.2 91.3 %collective-permute-start.4 = (bf16[768,2688]{1,0:T(8,128)(2,1)}, bf16[768,2688]{1,0:T(8,128)(2,1)}, u32[]{:S(2)}, u32[]{:S(2)}) collective-permute-start(bf16[768,2688]{1,0:T(8,128)(2,1)} %fusion.15), channel_id=1, source_target_pairs={{0,16},{16,0},{1,17},{17,1},{2,18},{18,2},{3,19},{19,3},{4,20},{20... | collective-permute-start | bytes 12386312 | tf_op jit(solution)/shard_map/ppermute | solution.py:15
  317.9 7.2 %copy-start.2 = (bf16[3584,2048]{1,0:T(8,128)(2,1)S(1)}, bf16[3584,2048]{1,0:T(8,128)(2,1)}, u32[]{:S(2)}) copy-start(bf16[3584,2048]{1,0:T(8,128)(2,1)} %convolution_convert_fusion) | copy-start | bytes 44040196
  317.9 43.3 %slice-start = ((s8[5505024]{0:T(1024)(128)(4,1)}), s8[4194304]{0:T(1024)(128)(4,1)S(1)}, s32[]{:S(2)}) async-start(s8[5505024]{0:T(1024)(128)(4,1)} %bitcast.65), calls=%async_computation.5 | async-start | bytes 8388608
  325.1 36.1 %slice-start.1 = ((s8[5505024]{0:T(1024)(128)(4,1)}), s8[1310720]{0:T(1024)(128)(4,1)S(1)}, s32[]{:S(2)}) async-start(s8[5505024]{0:T(1024)(128)(4,1)} %bitcast.65), calls=%async_computation.6 | async-start | bytes 2621440
  361.2 33.1 %copy-start.1 = (bf16[256,1024]{1,0:T(8,128)(2,1)S(1)}, bf16[256,1024]{1,0:T(8,128)(2,1)}, u32[]{:S(2)}) copy-start(bf16[256,1024]{1,0:T(8,128)(2,1)} %param.6) | copy-start | bytes 1572868
Sparse Core Ops, SparseCore 0:
  46.1 116.1 all-gather.2
  187.4 64.3 all-gather.4

commit v6 on v5

--- a/solution.py
+++ b/solution.py
@@ -106,22 +106,22 @@
     down_grad = (rounded_own.astype(jnp.float32) + rounded_other.astype(jnp.float32)).astype(
         jnp.bfloat16
     )
-    partial_back, partial_own, near, down_grad = lax.optimization_barrier(
-        (partial_back, partial_own, near, down_grad)
+    hidden_float = hidden.astype(jnp.float32)
+    score_head = jnp.sum(hidden_float[:, :moved] * (partial_own[:, :moved] + near), axis=1)
+    score_head = score_head + jnp.sum(hidden_float[:, moved:] * partial_own[:, moved:], axis=1)
+    partial_back, partial_own, near, down_grad, score_head = lax.optimization_barrier(
+        (partial_back, partial_own, near, down_grad, score_head)
     )
+    score = score_head + jnp.sum(hidden_float[:, moved:] * partial_back, axis=1)
+    every_score = lax.all_gather(score, ("expert", "tensor"))
     upstream = partial_own + jnp.concatenate((near, partial_back), axis=1)
-
-    score = jnp.sum(hidden.astype(jnp.float32) * upstream, axis=1)
     hidden_grad = gate_column * upstream
     gate_grad = (hidden_grad * up_float * slope).astype(jnp.bfloat16)
     up_grad = (hidden_grad * active).astype(jnp.bfloat16)
-    summed_scores = lax.psum(score, "tensor")
-    returned = lax.all_to_all(
-        summed_scores.reshape(expert_count, capacity),
-        "expert",
-        split_axis=0,
-        concat_axis=0,
-        tiled=True,
+    expert_here = lax.axis_index("expert")
+    summed_scores = jnp.sum(every_score.reshape(expert_count, tensor_count, slots), axis=1)
+    returned = lax.dynamic_slice_in_dim(
+        summed_scores.reshape(expert_count, expert_count, capacity), expert_here, 1, axis=1
     )
     flat_scores = returned.reshape(-1)
     router_grad = jnp.stack(

time: 402 us -> 457 us (1.14)
  other arithmetic: 47.4 us -> 67.6 us
  waiting for transfers between devices: 201 us -> 220 us
  blocking collectives: 46.2 us -> 59.1 us
    all_gather x0 -> x1, blocking collectives: none -> 28.8 us  [local(): every_score = lax.all_gather(score, ('expert', 'tensor'))]
    ppermute x5, waiting for transfers between devices: 142 us -> 169 us  [swap_dp(): return lax.ppermute(value, 'dp', perm=[(0, 1), (1, 0)])]
    reduce_sum x0 -> x3, other arithmetic: none -> 11.3 us  [the longest x1 7.12 us: local(): score = score_head + jnp.sum(hidden_float[:, moved:] * partial_back, axis=1)]
    psum x1 -> x0, blocking collectives: 9.31 us -> none  [local(): summed_scores = lax.psum(score, 'tensor')]
    all_gather x1, waiting for transfers between devices: 59 us -> 50.6 us  [local(): other_rows = lax.all_gather(other_piece, 'tensor', axis=1, tiled=True)]
    convert_element_type x0 -> x1, other arithmetic: none -> 8.39 us  [local(): hidden_float = hidden.astype(jnp.float32)]
    all_to_all x1 -> x0, blocking collectives: 6.55 us -> none  [local(): lax.all_to_all(summed_scores.reshape(expert_count, capacity), 'expert', s...]
  transfers between devices with their start and end apart: 7 -> 7, of which waited for: 4 -> 4; matrix products, arithmetic and copies ran while one was open for 24% -> 17% of each run, Pallas kernels for 0% -> 0%
where the time goes in v6:
time: 457 us; the launch traced here: 456 us
  waiting for transfers between devices  220 us (48%)
  matrix products  75.9 us (17%)
  other arithmetic  67.6 us (15%)
  blocking collectives  59.1 us (13%)
  between operations  14.2 us (3%)
  local copies, waits for them, and re-layouts  13 us (3%)
  starting transfers between devices  7.01 us (2%)
    ppermute x5, waiting for transfers between devices, swap_dp(): return lax.ppermute(value, 'dp', perm=[(0, 1), (1, 0)])  169 us
    all_gather x1, waiting for transfers between devices, local(): other_rows = lax.all_gather(other_piece, 'tensor', axis=1, tiled=True)  50.6 us
    all_gather x1, blocking collectives, local(): every_score = lax.all_gather(score, ('expert', 'tensor'))  28.8 us
    all_to_all x1, blocking collectives, local(): lax.all_to_all(outgoing, 'expert', split_axis=0, concat_axis=0, tiled=True)  24.2 us
    dot_general x1, matrix products, local(): lax.dot_general(hidden_other, scaled_other, contract_rows, preferred_elem...  17.9 us
    dot_general x1, matrix products, local(): lax.dot_general(own_rows, local_weight, contract_cols, preferred_element_...  17.3 us
    dot_general x1, matrix products, local(): lax.dot_general(hidden, scaled_own, contract_rows, preferred_element_type...  17.1 us
    broadcast_in_dim x1, other arithmetic, local(): return (gate_grad[None], up_grad[None], down_grad[None], router_grad)  16.7 us
  transfers between devices with their start and end apart: 7, of which 4 were waited for; matrix products, arithmetic and copies ran while one was open for 17% of the time, Pallas kernels for 0%

profile of v6, /device:TPU:0, one launch (start us, length us, event | category | flops | bytes accessed | tf_op | source)
XLA Modules:
  0.0 456.3 jit_solution(13458965661788614969)
XLA Ops:
  7.2 0.0 copy-start
  7.2 0.0 all-gather.5.cloned.1.call-start
  7.2 0.9 copy.32
  8.1 0.1 eq.59
  8.2 0.1 eq.55
  8.4 1.2 reduce-window.6
  9.6 0.2 slice_reduce_fusion
  9.8 0.2 reduce-window.9
  10.0 0.1 add_bitcast_fusion
  10.1 0.1 reduce_sum.75
  10.3 0.1 copy.34
  10.3 0.7 multiply_add_fusion
  11.1 0.8 slice_convert_fusion.1
  11.8 0.2 select_reduce_fusion.2
  12.0 0.1 convert_element_type.95
  12.1 0.0 copy-done
  12.1 0.8 convolution_convert_fusion.2
  12.9 8.9 %fusion.2 = bf16[768,3584]{1,0:T(8,128)(2,1)} fusion(bf16[1,768,3584]{2,1,0:T(8,128)(2,1)} %param.10, bf16[1,768,3584]{2,1,0:T(8,128)(2,1)} %param.9), kind=kLoop, calls=%fused_computation.10 | loop fusion | flops 22020096 | bytes 16515072 | tf_op jit(solution)/shard_map/convert_element_type | solution.py:49
  21.7 24.2 %all_to_all.14 = bf16[4,192,1024]{2,1,0:T(8,128)(2,1)} all-to-all(bf16[4,192,1024]{2,1,0:T(8,128)(2,1)S(1)} %bitcast.69), channel_id=1, replica_groups=mesh['dp'=2,'expert'=4,'tensor'=4] {'expert'}, dimensions={0} | all-to-all | bytes 3145728 | tf_op jit(solution)/shard_map/all_to_all | solution.py:60
  46.0 0.0 all-gather.5.cloned.1.call-update
  46.0 0.0 all-gather.7.cloned.1.call-start
  46.0 2.0 collective-permute-start
  48.1 6.1 %all_to_all.15 = bf16[4,1,192]{2,1,0:T(2,128)(2,1)S(1)} all-to-all(bf16[4,1,192]{2,1,0:T(2,128)(2,1)S(1)} %copy.35), channel_id=1, replica_groups=mesh['dp'=2,'expert'=4,'tensor'=4] {'expert'}, dimensions={0} | all-to-all | bytes 3072 | tf_op jit(solution)/shard_map/all_to_all | solution.py:59
  54.2 0.1 reshape.65
  54.3 0.1 collective-permute-start.1
  54.4 112.3 %collective-permute-done.1 = bf16[768]{0:T(1024)(128)(2,1)S(1)} collective-permute-done((bf16[768]{0:T(1024)(128)(2,1)S(1)}, bf16[768]{0:T(1024)(128)(2,1)S(1)}, u32[]{:S(2)}, u32[]{:S(2)}) %collective-permute-start.1) | collective-permute-done | bytes 1568 | tf_op jit(solution)/shard_map/ppermute | solution.py:15
  166.7 0.0 collective-permute-done
  166.7 1.2 constant_dynamic-slice_fusion.1
  167.9 1.8 collective-permute-start.2
  169.7 4.4 slice_bitcast_fusion
  174.1 12.2 %collective-permute-done.2 = bf16[768,512]{1,0:T(8,128)(2,1)S(1)} collective-permute-done((bf16[768,512]{1,0:T(8,128)(2,1)S(1)}, bf16[768,512]{1,0:T(8,128)(2,1)S(1)}, u32[]{:S(2)}, u32[]{:S(2)}) %collective-permute-start.2) | collective-permute-done | bytes 786464 | tf_op jit(solution)/shard_map/ppermute | solution.py:15
  186.3 0.9 copy-done.5
  187.1 0.0 all-gather.7.cloned.1.call-update
  187.2 1.5 collective-permute-start.3
  188.7 8.4 %convert_element_type.109 = f32[768,3584]{1,0:T(8,128)} convert(bf16[768,3584]{1,0:T(8,128)(2,1)} %fusion.2) | non-fusion elementwise | flops 2752512 | bytes 16515072 | tf_op jit(solution)/shard_map/convert_element_type | solution.py:109
  197.1 4.1 constant_dynamic-slice_fusion
  201.1 50.6 %all-gather.7.cloned.1.call-done = bf16[768,2048]{1,0:T(8,128)(2,1)} async-done(((bf16[768,512]{1,0:T(8,128)(2,1)}), bf16[768,2048]{1,0:T(8,128)(2,1)}) %all-gather.7.cloned.1.call-update) | async-done | bytes 3145744 | tf_op jit(solution)/shard_map/all_gather | solution.py:81
  251.8 15.4 %fusion.17 = bf16[768,2688]{1,0:T(8,128)(2,1)} fusion(bf16[768,2048]{1,0:T(8,128)(2,1)} %all-gather.7.cloned.1.call-done, bf16[1,3584,2048]{2,1,0:T(8,128)(2,1)} %param.11), kind=kOutput, calls=%fused_computation.31 | convolution fusion | flops 8457781248 | bytes 18284544 | tf_op jit(solution)/shard_map/dot_general | solution.py:85
  267.1 0.0 collective-permute-done.3
  267.1 0.0 copy-done.4
  267.1 17.3 %fusion = f32[768,3584]{1,0:T(8,128)} fusion(bf16[768,2048]{1,0:T(8,128)(2,1)S(1)} %copy-done.4, bf16[1,3584,2048]{2,1,0:T(8,128)(2,1)} %param.11), kind=kOutput, calls=%fused_computation.6 | convolution fusion | flops 11274289152 | bytes 28835840 | tf_op jit(solution)/shard_map/dot_general | solution.py:92
  284.5 17.1 %convolution_convert_fusion.1 = bf16[3584,2048]{1,0:T(8,128)(2,1)} fusion(bf16[768,3584]{1,0:T(8,128)(2,1)} %fusion.2, bf16[768,2048]{1,0:T(8,128)(2,1)S(1)} %copy-done.4, f32[768]{0:T(1024)S(1)} %convert_element_type.96), kind=kOutput, calls=%fused_computation.5 | convolution fusion | flops 11286347776 | bytes 23333888 | tf_op jit(solution)/shard_map/dot_general | solution.py:100
  301.6 1.5 collective-permute-start.4
  303.1 17.9 %convolution_convert_fusion = bf16[3584,2048]{1,0:T(8,128)(2,1)} fusion(bf16[768,3584]{1,0:T(8,128)(2,1)} %collective-permute-done, bf16[768,2048]{1,0:T(8,128)(2,1)} %all-gather.7.cloned.1.call-done, f32[768]{0:T(1024)S(1)} %convert_element_type.103), kind=kOutput, calls=%fused_computation.4 | convolution fusion | flops 11286347776 | bytes 23333888 | tf_op jit(solution)/shard_map/dot_general | solution.py:101
  320.9 0.0 slice-done
  320.9 0.0 slice-done.1
  320.9 0.0 slice-done.2
  320.9 4.1 fusion.14
  325.1 0.0 copy-start.3
  325.1 7.5 %fusion.25 = (f32[768]{0:T(1024)S(1)}, f32[768,896]{1,0:T(8,128)S(1)}) fusion(f32[768,3584]{1,0:T(8,128)} %fusion, f32[768,3584]{1,0:T(8,128)S(1)} %bitcast.66, bf16[896,2048]{1,0:T(8,128)(2,1)} %collective-permute-done.3, bf16[768,4096]{1,0:T(8,128)(2,1)} %all-gather.5.cloned.1.call-done, s32[]{:T(128)S(6)} %select_n.39), kind=kOutput, calls=%fused_computation.39 | convolution fusion | flops 2820635904 | bytes 15076356 | tf_op jit(solution)/shard_map/dot_general | solution.py:96
  332.6 0.5 copy-done.3
  333.0 15.4 %add_convert_fusion = bf16[3584,2048]{1,0:T(8,128)(2,1)} fusion(bf16[3584,2048]{1,0:T(8,128)(2,1)S(1)} %copy-done.3, bf16[3584,2048]{1,0:T(8,128)(2,1)} %convolution_convert_fusion.1), kind=kLoop, calls=%fused_computation | loop fusion | flops 29360128 | bytes 44040192 | tf_op jit(solution)/shard_map/convert_element_type | solution.py:106
  348.4 44.4 %collective-permute-done.4 = bf16[768,2688]{1,0:T(8,128)(2,1)} collective-permute-done((bf16[768,2688]{1,0:T(8,128)(2,1)}, bf16[768,2688]{1,0:T(8,128)(2,1)}, u32[]{:S(2)}, u32[]{:S(2)}) %collective-permute-start.4) | collective-permute-done | bytes 4128800 | tf_op jit(solution)/shard_map/ppermute | solution.py:15
  392.8 2.7 convert_element_type.98
  395.5 0.0 copy-start.2
  395.5 7.1 %multiply_reduce_fusion = f32[768]{0:T(1024)S(1)} fusion(f32[768,2688]{1,0:T(8,128)S(1)} %convert_element_type.98, f32[768,3584]{1,0:T(8,128)} %convert_element_type.109), kind=kLoop, calls=%fused_computation.26 | loop fusion | flops 4128000 | bytes 16518144 | tf_op jit(solution)/shard_map/reduce_sum | solution.py:115
  402.7 28.8 %all-gather.1 = f32[16,1,768]{2,1,0:T(1,128)S(1)} all-gather(f32[1,1,768]{2,1,0:T(1,128)S(1)} %reshape.75), channel_id=2, replica_groups=mesh['dp'=2,'expert'=4,'tensor'=4] {'expert','tensor'}, dimensions={0}, use_global_device_ids=true | all-gather | bytes 52224 | tf_op jit(solution)/shard_map/all_gather | solution.py:116
  431.5 0.1 reduce.2
  431.7 0.1 reshape.68
  431.8 0.1 broadcast_in_dim.76
  431.9 0.3 select_reduce_fusion.1
  432.2 0.6 pad_maximum_fusion
  432.8 16.7 %fusion.15 = (bf16[1,768,3584]{2,1,0:T(8,128)(2,1)}, bf16[1,768,3584]{2,1,0:T(8,128)(2,1)}) fusion(bf16[1,768,3584]{2,1,0:T(8,128)(2,1)} %param.9, f32[768,3584]{1,0:T(8,128)} %fusion, f32[768,2688]{1,0:T(8,128)} %copy-done.2, f32[768,896]{1,0:T(8,128)S(1)} %get-tuple-element.36, f32[768]{0:T(1024)S(1)} %convert_element_type.96, bf16[1,768,3584]{2,1,0:T(8,128)(2,1)} %param.10), kind=kLoop, calls=%fused_computation.29 | loop fusion | flops 49545216 | bytes 44043264 | tf_op jit(solution)/shard_map/broadcast_in_dim | solution.py:134
  449.5 0.0 copy-done.1
  (22 shorter events, 0.2 us)
Async XLA Ops:
  7.2 5.0 %copy-start = (bf16[256,1024]{1,0:T(8,128)(2,1)S(1)}, bf16[256,1024]{1,0:T(8,128)(2,1)}, u32[]{:S(2)}) copy-start(bf16[256,1024]{1,0:T(8,128)(2,1)} %param.6) | copy-start | bytes 1572868
  7.2 159.5 %all-gather.5.cloned.1.call-start = ((), (), s32[]{:S(2)}) async-start(), calls=%async_computation.2 | async-start | bytes 7864320 | tf_op jit(solution)/shard_map/all_gather | solution.py:66
  46.0 205.8 %all-gather.7.cloned.1.call-start = ((), (), s32[]{:S(2)}) async-start(), calls=%async_computation.3 | async-start | bytes 3932160 | tf_op jit(solution)/shard_map/all_gather | solution.py:81
  46.0 120.7 %collective-permute-start = (bf16[768,3584]{1,0:T(8,128)(2,1)}, bf16[768,3584]{1,0:T(8,128)(2,1)}, u32[]{:S(2)}, u32[]{:S(2)}) collective-permute-start(bf16[768,3584]{1,0:T(8,128)(2,1)} %fusion.2), channel_id=1, source_target_pairs={{0,16},{16,0},{1,17},{17,1},{2,18},{18,2},{3,19},{19,3},{4,20},{20... | collective-permute-start | bytes 16515080 | tf_op jit(solution)/shard_map/ppermute | solution.py:15
  54.3 112.4 %collective-permute-start.1 = (bf16[768]{0:T(1024)(128)(2,1)S(1)}, bf16[768]{0:T(1024)(128)(2,1)S(1)}, u32[]{:S(2)}, u32[]{:S(2)}) collective-permute-start(bf16[768]{0:T(1024)(128)(2,1)S(1)} %reshape.65), channel_id=1, source_target_pairs={{0,16},{16,0},{1,17},{17,1},{2,18},{18,2},{3,19},{19,3},{4,20},{20... | collective-permute-start | bytes 4616 | tf_op jit(solution)/shard_map/ppermute | solution.py:15
  167.9 18.3 %collective-permute-start.2 = (bf16[768,512]{1,0:T(8,128)(2,1)S(1)}, bf16[768,512]{1,0:T(8,128)(2,1)S(1)}, u32[]{:S(2)}, u32[]{:S(2)}) collective-permute-start(bf16[768,512]{1,0:T(8,128)(2,1)S(1)} %constant_dynamic-slice_fusion.1), channel_id=1, source_target_pairs={{0,16},{16,0},{1,17},{17,1},{2,18},{18,2},{3,19},{19,3},{4,20},{20... | collective-permute-start | bytes 2359304 | tf_op jit(solution)/shard_map/ppermute | solution.py:15
  186.2 0.9 copy-start.5
  187.2 80.0 %collective-permute-start.3 = (bf16[896,2048]{1,0:T(8,128)(2,1)}, bf16[896,2048]{1,0:T(8,128)(2,1)}, u32[]{:S(2)}, u32[]{:S(2)}) collective-permute-start(bf16[896,2048]{1,0:T(8,128)(2,1)} %slice_bitcast_fusion), channel_id=1, source_target_pairs={{0,16},{16,0},{1,17},{17,1},{2,18},{18,2},{3,19},{19,3},{4,20},{20... | collective-permute-start | bytes 11010056 | tf_op jit(solution)/shard_map/ppermute | solution.py:15
  251.8 15.4 %copy-start.4 = (bf16[768,2048]{1,0:T(8,128)(2,1)S(1)}, bf16[768,2048]{1,0:T(8,128)(2,1)}, u32[]{:S(2)}) copy-start(bf16[768,2048]{1,0:T(8,128)(2,1)} %constant_dynamic-slice_fusion) | copy-start | bytes 9437188
  284.5 36.5 %slice-start = ((s8[11010048]{0:T(1024)(128)(4,1)}), s8[4194304]{0:T(1024)(128)(4,1)S(1)}, s32[]{:S(2)}) async-start(s8[11010048]{0:T(1024)(128)(4,1)} %bitcast.65), calls=%async_computation.4 | async-start | bytes 8388608
  284.5 36.5 %slice-start.1 = ((s8[11010048]{0:T(1024)(128)(4,1)}), s8[4194304]{0:T(1024)(128)(4,1)S(1)}, s32[]{:S(2)}) async-start(s8[11010048]{0:T(1024)(128)(4,1)} %bitcast.65), calls=%async_computation.5 | async-start | bytes 8388608
  301.6 19.4 %slice-start.2 = ((s8[11010048]{0:T(1024)(128)(4,1)}), s8[2621440]{0:T(1024)(128)(4,1)S(1)}, s32[]{:S(2)}) async-start(s8[11010048]{0:T(1024)(128)(4,1)} %bitcast.65), calls=%async_computation.6 | async-start | bytes 5242880
  301.6 91.2 %collective-permute-start.4 = (bf16[768,2688]{1,0:T(8,128)(2,1)}, bf16[768,2688]{1,0:T(8,128)(2,1)}, u32[]{:S(2)}, u32[]{:S(2)}) collective-permute-start(bf16[768,2688]{1,0:T(8,128)(2,1)} %fusion.17), channel_id=1, source_target_pairs={{0,16},{16,0},{1,17},{17,1},{2,18},{18,2},{3,19},{19,3},{4,20},{20... | collective-permute-start | bytes 12386312 | tf_op jit(solution)/shard_map/ppermute | solution.py:15
  325.1 8.0 %copy-start.3 = (bf16[3584,2048]{1,0:T(8,128)(2,1)S(1)}, bf16[3584,2048]{1,0:T(8,128)(2,1)}, u32[]{:S(2)}) copy-start(bf16[3584,2048]{1,0:T(8,128)(2,1)} %convolution_convert_fusion) | copy-start | bytes 44040196
  395.5 7.1 %copy-start.2 = (f32[768,2688]{1,0:T(8,128)}, f32[768,2688]{1,0:T(8,128)S(1)}, u32[]{:S(2)}) copy-start(f32[768,2688]{1,0:T(8,128)S(1)} %convert_element_type.98) | copy-start | bytes 24772612
  432.8 16.7 %copy-start.1 = (bf16[256,1024]{1,0:T(8,128)(2,1)S(1)}, bf16[256,1024]{1,0:T(8,128)(2,1)}, u32[]{:S(2)}) copy-start(bf16[256,1024]{1,0:T(8,128)(2,1)} %param.6) | copy-start | bytes 1572868
Sparse Core Ops, SparseCore 0:
  46.1 116.1 all-gather.4
  187.3 64.4 all-gather.6

commit v7 on v5

--- a/solution.py
+++ b/solution.py
@@ -41,7 +41,7 @@
 
     local_weight = down_weight[0]
     units = local_weight.shape[0]
-    moved = units // 4 // 16 * 16
+    moved = units * 3 // 16 // 128 * 128
 
     gate_float = gate_preact[0].astype(jnp.float32)
     up_float = up_preact[0].astype(jnp.float32)
@@ -55,7 +55,8 @@
     )
     outgoing = outgoing.astype(jnp.bfloat16).reshape(expert_count, capacity, -1)
     hidden, outgoing, gate_send = lax.optimization_barrier((hidden, outgoing, gate_send))
-    hidden_other = swap_dp(hidden)
+    split = hidden.shape[0] // 2
+    hidden_first = swap_dp(hidden[:split])
     gate_slots = lax.all_to_all(gate_send, "expert", split_axis=0, concat_axis=0, tiled=True)
     received = lax.all_to_all(outgoing, "expert", split_axis=0, concat_axis=0, tiled=True)
     slots = expert_count * capacity
@@ -63,41 +64,70 @@
     gate_bf16 = gate_slots.reshape(-1)
     gate_column = gate_bf16.astype(jnp.float32)[:, None]
     other_gates = swap_dp(gate_bf16)
-    fragment = lax.all_gather(narrow_rows, "tensor", axis=1, tiled=True)
-    fragment, hidden_other, other_gates = lax.optimization_barrier(
-        (fragment, hidden_other, other_gates)
+    narrow = narrow_rows.shape[1]
+    cut = narrow // 2
+    front = lax.all_gather(narrow_rows[:, :cut], "tensor", axis=1, tiled=True)
+    back = lax.all_gather(narrow_rows[:, cut:], "tensor", axis=1, tiled=True)
+    front, hidden_first, other_gates = lax.optimization_barrier(
+        (front, hidden_first, other_gates)
     )
 
-    width = fragment.shape[1]
+    width = narrow * tensor_count
     half = width // 2
-    piece = half // tensor_count
-    own_rows = lax.dynamic_slice_in_dim(fragment, replica * half, half, axis=1)
-    send_rows = lax.dynamic_slice_in_dim(
-        fragment, (1 - replica) * half + part * piece, piece, axis=1
+    half_part = half // 2
+    piece = half_part // tensor_count
+    quarters = tensor_count // 2
+
+    def in_order(front_part, back_part):
+        blocks = []
+        for quarter in range(quarters):
+            blocks.append(front_part[:, quarter * cut : (quarter + 1) * cut])
+            blocks.append(back_part[:, quarter * cut : (quarter + 1) * cut])
+        return jnp.concatenate(blocks, axis=1)
+
+    def half_of(rows, which):
+        return lax.dynamic_slice_in_dim(rows, which * half_part, half_part, axis=1)
+
+    send_front = lax.dynamic_slice_in_dim(
+        front, (1 - replica) * half_part + part * piece, piece, axis=1
     )
-    other_piece = swap_dp(send_rows)
-    weight_rest, other_piece = lax.optimization_barrier((local_weight[:moved], other_piece))
+    piece_front = swap_dp(send_front)
+    hidden_rest, piece_front = lax.optimization_barrier((hidden[split:], piece_front))
+    hidden_second = swap_dp(hidden_rest)
+    send_back = lax.dynamic_slice_in_dim(
+        back, (1 - replica) * half_part + part * piece, piece, axis=1
+    )
+    send_back, hidden_second = lax.optimization_barrier((send_back, hidden_second))
+    piece_back = swap_dp(send_back)
+    weight_rest, piece_back = lax.optimization_barrier((local_weight[:moved], piece_back))
     weight_moved = swap_dp(weight_rest)
-    other_rows = lax.all_gather(other_piece, "tensor", axis=1, tiled=True)
-    hidden_other, other_rows = lax.optimization_barrier((hidden_other, other_rows))
+    other_front = lax.all_gather(piece_front, "tensor", axis=1, tiled=True)
+    other_front, front, back = lax.optimization_barrier((other_front, front, back))
+    other_back = lax.all_gather(piece_back, "tensor", axis=1, tiled=True)
+    other_rows = in_order(other_front, other_back)
+    own_rows = in_order(half_of(front, replica), half_of(back, replica))
+    far_rows = in_order(half_of(front, 1 - replica), half_of(back, 1 - replica))
+    hidden_first, hidden_second, other_rows = lax.optimization_barrier(
+        (hidden_first, hidden_second, other_rows)
+    )
     other_gates = other_gates.astype(jnp.float32)[:, None]
 
     partial_other = lax.dot_general(
         other_rows, local_weight[moved:], contract_cols, preferred_element_type=jnp.float32
     )
-    weight_moved, partial_send, own_rows = lax.optimization_barrier(
-        (weight_moved, partial_other.astype(PARTIAL_DTYPE), own_rows)
+    weight_moved, partial_send, hidden_first, hidden_second = lax.optimization_barrier(
+        (weight_moved, partial_other.astype(PARTIAL_DTYPE), hidden_first, hidden_second)
     )
     partial_back = swap_dp(partial_send).astype(jnp.float32)
     partial_own = lax.dot_general(
         own_rows, local_weight, contract_cols, preferred_element_type=jnp.float32
     )
-    far_rows = lax.dynamic_slice_in_dim(fragment, (1 - replica) * half, half, axis=1)
     near = lax.dot_general(far_rows, weight_moved, contract_cols, preferred_element_type=jnp.float32)
 
     scaled_own = (gate_column * own_rows.astype(jnp.float32)).astype(jnp.bfloat16)
     scaled_other = (other_gates * other_rows.astype(jnp.float32)).astype(jnp.bfloat16)
     grad_own = lax.dot_general(hidden, scaled_own, contract_rows, preferred_element_type=jnp.float32)
+    hidden_other = jnp.concatenate((hidden_first, hidden_second), axis=0)
     grad_other = lax.dot_general(
         hidden_other, scaled_other, contract_rows, preferred_element_type=jnp.float32
     )

time: 402 us -> 459 us (1.14)
  waiting for transfers between devices: 201 us -> 244 us
  local copies, waits for them, and re-layouts: 13 us -> 23.9 us
    all_gather x2 -> x4, waiting for transfers between devices: 59 us -> 96.7 us  [the longest x1 45 us: local(): back = lax.all_gather(narrow_rows[:, cut:], 'tensor', axis=1, tiled=True)]
    slice x1 -> x6, local copies, waits for them, and re-layouts: 0.22 us -> 13.6 us  [the longest x2 6.17 us: in_order(): blocks.append(front_part[:, quarter * cut:(quarter + 1) * cut])]
    ppermute x5 -> x7, waiting for transfers between devices: 142 us -> 146 us  [swap_dp(): return lax.ppermute(value, 'dp', perm=[(0, 1), (1, 0)])]
  transfers between devices with their start and end apart: 7 -> 11, of which waited for: 4 -> 7; matrix products, arithmetic and copies ran while one was open for 24% -> 23% of each run, Pallas kernels for 0% -> 0%
where the time goes in v7:
time: 459 us; the launch traced here: 458 us
  waiting for transfers between devices  244 us (53%)
  matrix products  73.3 us (16%)
  other arithmetic  48.1 us (10%)
  blocking collectives  45.8 us (10%)
  local copies, waits for them, and re-layouts  23.9 us (5%)
  between operations  14 us (3%)
  starting transfers between devices  9.1 us (2%)
    ppermute x7, waiting for transfers between devices, swap_dp(): return lax.ppermute(value, 'dp', perm=[(0, 1), (1, 0)])  146 us
    all_gather x1, waiting for transfers between devices, local(): back = lax.all_gather(narrow_rows[:, cut:], 'tensor', axis=1, tiled=True)  45 us
    all_gather x1, waiting for transfers between devices, local(): other_front = lax.all_gather(piece_front, 'tensor', axis=1, tiled=True)  36.8 us
    all_to_all x1, blocking collectives, local(): lax.all_to_all(outgoing, 'expert', split_axis=0, concat_axis=0, tiled=True)  24.1 us
    dot_general x1, matrix products, local(): lax.dot_general(own_rows, local_weight, contract_cols, preferred_element_...  18.4 us
    dot_general x1, matrix products, local(): lax.dot_general(hidden, scaled_own, contract_rows, preferred_element_type...  17.9 us
    dot_general x1, matrix products, local(): lax.dot_general(hidden_other, scaled_other, contract_rows, preferred_elem...  17 us
    broadcast_in_dim x1, other arithmetic, local(): return (gate_grad[None], up_grad[None], down_grad[None], router_grad)  16.2 us
  transfers between devices with their start and end apart: 11, of which 7 were waited for; matrix products, arithmetic and copies ran while one was open for 23% of the time, Pallas kernels for 0%

profile of v7, /device:TPU:0, one launch (start us, length us, event | category | flops | bytes accessed | tf_op | source)
XLA Modules:
  0.0 458.0 jit_solution(17940032286841163684)
XLA Ops:
  7.2 0.0 all-gather.7.cloned.1.call-start
  7.2 0.9 copy.32
  8.1 0.1 eq.59
  8.2 0.1 eq.55
  8.4 1.2 reduce-window.6
  9.6 0.2 slice_reduce_fusion
  9.8 0.2 reduce-window.9
  10.0 0.1 add_bitcast_fusion
  10.1 0.1 reduce_sum.48
  10.3 0.1 copy.34
  10.3 0.7 multiply_add_fusion
  11.1 0.8 slice_convert_fusion.1
  11.8 0.2 select_reduce_fusion.2
  12.0 0.1 convert_element_type.95
  12.1 0.8 convolution_convert_fusion.2
  12.9 8.9 %fusion.5 = bf16[768,3584]{1,0:T(8,128)(2,1)} fusion(bf16[1,768,3584]{2,1,0:T(8,128)(2,1)} %param.10, bf16[1,768,3584]{2,1,0:T(8,128)(2,1)} %param.9), kind=kLoop, calls=%fused_computation.13 | loop fusion | flops 22020096 | bytes 16515072 | tf_op jit(solution)/shard_map/convert_element_type | solution.py:49
  21.7 24.1 %all_to_all.23 = bf16[4,192,1024]{2,1,0:T(8,128)(2,1)S(1)} all-to-all(bf16[4,192,1024]{2,1,0:T(8,128)(2,1)S(1)} %bitcast.67), channel_id=1, replica_groups=mesh['dp'=2,'expert'=4,'tensor'=4] {'expert'}, dimensions={0} | all-to-all | bytes 3145728 | tf_op jit(solution)/shard_map/all_to_all | solution.py:61
  45.9 1.3 fusion.52
  47.1 0.0 all-gather.7.cloned.1.call-update
  47.1 0.0 all-gather.5.cloned.1.call-start
  47.2 0.7 all-gather.5.cloned.1.call-update
  47.9 0.0 all-gather.9.cloned.1.call-start
  47.9 4.5 fusion.49
  52.4 1.5 collective-permute-start
  53.9 6.1 %all_to_all.24 = bf16[4,1,192]{2,1,0:T(2,128)(2,1)S(1)} all-to-all(bf16[4,1,192]{2,1,0:T(2,128)(2,1)S(1)} %copy.35), channel_id=1, replica_groups=mesh['dp'=2,'expert'=4,'tensor'=4] {'expert'}, dimensions={0} | all-to-all | bytes 3072 | tf_op jit(solution)/shard_map/all_to_all | solution.py:60
  60.1 0.1 reshape.64
  60.2 0.5 collective-permute-start.1
  60.7 53.1 %collective-permute-done.1 = bf16[768]{0:T(1024)(128)(2,1)S(1)} collective-permute-done((bf16[768]{0:T(1024)(128)(2,1)S(1)}, bf16[768]{0:T(1024)(128)(2,1)S(1)}, u32[]{:S(2)}, u32[]{:S(2)}) %collective-permute-start.1) | collective-permute-done | bytes 1568 | tf_op jit(solution)/shard_map/ppermute | solution.py:15
  113.8 1.0 constant_dynamic-slice_fusion.7
  114.9 1.6 collective-permute-start.2
  116.4 8.1 %collective-permute-done.2 = bf16[768,256]{1,0:T(8,128)(2,1)S(1)} collective-permute-done((bf16[768,256]{1,0:T(8,128)(2,1)S(1)}, bf16[768,256]{1,0:T(8,128)(2,1)S(1)}, u32[]{:S(2)}, u32[]{:S(2)}) %collective-permute-start.2) | collective-permute-done | bytes 393248 | tf_op jit(solution)/shard_map/ppermute | solution.py:15
  124.5 1.5 collective-permute-start.3
  126.0 0.0 all-gather.9.cloned.1.call-update
  126.0 0.2 all-gather.11.cloned.1.call-start
  126.3 3.6 slice_bitcast_fusion
  129.8 45.0 %all-gather.5.cloned.1.call-done = bf16[768,2048]{1,0:T(8,128)(2,1)} async-done(((bf16[768,512]{1,0:T(8,128)(2,1)}), bf16[768,2048]{1,0:T(8,128)(2,1)}) %all-gather.5.cloned.1.call-update) | async-done | bytes 3145744 | tf_op jit(solution)/shard_map/all_gather | solution.py:70
  174.8 1.8 constant_dynamic-slice_fusion.8
  176.6 36.8 %all-gather.9.cloned.1.call-done = bf16[768,1024]{1,0:T(8,128)(2,1)} async-done(((bf16[768,256]{1,0:T(8,128)(2,1)}), bf16[768,1024]{1,0:T(8,128)(2,1)}) %all-gather.9.cloned.1.call-update) | async-done | bytes 1572880 | tf_op jit(solution)/shard_map/all_gather | solution.py:104
  213.4 4.7 %constant_dynamic-slice_fusion = (bf16[768,512]{1,0:T(8,128)(2,1)}, bf16[768,512]{1,0:T(8,128)(2,1)S(1)}, bf16[768,512]{1,0:T(8,128)(2,1)}, bf16[768,512]{1,0:T(...) fusion(bf16[768,2048]{1,0:T(8,128)(2,1)} %all-gather.7.cloned.1, ...), kind=kLoop, calls=%fused_computation.66 | loop fusion | bytes 12582928 | tf_op jit(solution)/shard_map/slice | solution.py:84
  218.1 1.6 collective-permute-start.4
  219.7 17.9 %convolution_convert_fusion.1 = bf16[3584,2048]{1,0:T(8,128)(2,1)} fusion(bf16[768,3584]{1,0:T(8,128)(2,1)} %fusion.5, f32[768]{0:T(1024)S(1)} %convert_element_type.96, bf16[768,512]{1,0:T(8,128)(2,1)S(1)} %get-tuple-element.81, bf16[768,512]{1,0:T(8,128)(2,1)S(1)} %get-tuple-element.66, bf16[768,512]{1,0:T(8,128)(2,1)S(1)} %get-tuple-element.83, ...), kind=kOutput, calls=%fused_computation.5 | convolution fusion | flops 11297357824 | bytes 23333888 | tf_op jit(solution)/shard_map/dot_general | solution.py:129
  237.7 0.8 copy-done.11
  238.4 1.5 fusion.50
  239.9 18.4 %fusion = f32[768,3584]{1,0:T(8,128)} fusion(bf16[1,3584,2048]{2,1,0:T(8,128)(2,1)} %param.11, bf16[768,512]{1,0:T(8,128)(2,1)} %copy-done.8, bf16[768,512]{1,0:T(8,128)(2,1)} %copy-done.7, bf16[768,512]{1,0:T(8,128)(2,1)} %copy-done.9, bf16[768,512]{1,0:T(8,128)(2,1)} %copy-done.6), kind=kOutput, calls=%fused_computation.6 | convolution fusion | flops 11286872064 | bytes 28835840 | tf_op jit(solution)/shard_map/dot_general | solution.py:122
  258.3 0.8 collective-permute-start.5
  259.1 14.9 %all-gather.11.cloned.1.call-done = bf16[768,1024]{1,0:T(8,128)(2,1)} async-done(((bf16[768,256]{1,0:T(8,128)(2,1)}), bf16[768,1024]{1,0:T(8,128)(2,1)}) %all-gather.11.cloned.1.call-update) | async-done | bytes 1572880 | tf_op jit(solution)/shard_map/all_gather | solution.py:106
  274.0 1.5 fusion.51
  275.5 0.5 pad_maximum_fusion
  276.0 14.5 %fusion.18 = bf16[768,2944]{1,0:T(8,128)(2,1)} fusion(bf16[768,2048]{1,0:T(8,128)(2,1)S(1)} %pad_maximum_fusion, bf16[1,3584,2048]{2,1,0:T(8,128)(2,1)} %param.11), kind=kOutput, calls=%fused_computation.31 | convolution fusion | flops 9263284224 | bytes 19726336 | tf_op jit(solution)/shard_map/dot_general | solution.py:115
  290.5 26.6 %collective-permute-done.5 = bf16[640,2048]{1,0:T(8,128)(2,1)} collective-permute-done((bf16[640,2048]{1,0:T(8,128)(2,1)}, bf16[640,2048]{1,0:T(8,128)(2,1)}, u32[]{:S(2)}, u32[]{:S(2)}) %collective-permute-start.5) | collective-permute-done | bytes 2621472 | tf_op jit(solution)/shard_map/ppermute | solution.py:15
  317.0 1.3 collective-permute-start.6
  318.3 17.0 %convolution_convert_fusion = bf16[3584,2048]{1,0:T(8,128)(2,1)} fusion(bf16[384,3584]{1,0:T(8,128)(2,1)} %collective-permute-done.3, bf16[384,3584]{1,0:T(8,128)(2,1)} %collective-permute-done, bf16[768,2048]{1,0:T(8,128)(2,1)S(1)} %pad_maximum_fusion, f32[768]{0:T(1024)S(1)} %convert_element_type.103), kind=kOutput, calls=%fused_computation.4 | convolution fusion | flops 11297357824 | bytes 23333888 | tf_op jit(solution)/shard_map/dot_general | solution.py:131
  335.3 4.8 %fusion.21 = f32[768,640]{1,0:T(8,128)S(1)} fusion(bf16[640,2048]{1,0:T(8,128)(2,1)} %collective-permute-done.5, bf16[768,512]{1,0:T(8,128)(2,1)S(1)} %copy-done.5, bf16[768,512]{1,0:T(8,128)(2,1)S(1)} %copy-done.4, bf16[768,512]{1,0:T(8,128)(2,1)} %get-tuple-element.84, bf16[768,512]{1,0:T(8,128)(2,1)S(1)} %copy-done.3), kind=kOutput, calls=%fused_computation.34 | convolution fusion | flops 2025848832 | bytes 7733248 | tf_op jit(solution)/shard_map/dot_general | solution.py:125
  340.1 1.4 copy-done.2
  341.5 15.6 %add_convert_fusion = bf16[3584,2048]{1,0:T(8,128)(2,1)} fusion(bf16[3584,2048]{1,0:T(8,128)(2,1)S(1)} %copy-done.2, bf16[3584,2048]{1,0:T(8,128)(2,1)} %convolution_convert_fusion.1), kind=kLoop, calls=%fused_computation | loop fusion | flops 29360128 | bytes 44040192 | tf_op jit(solution)/shard_map/convert_element_type | solution.py:136
  357.0 58.6 %collective-permute-done.6 = bf16[768,2944]{1,0:T(8,128)(2,1)} collective-permute-done((bf16[768,2944]{1,0:T(8,128)(2,1)}, bf16[768,2944]{1,0:T(8,128)(2,1)}, u32[]{:S(2)}, u32[]{:S(2)}) %collective-permute-start.6) | collective-permute-done | bytes 4522016 | tf_op jit(solution)/shard_map/ppermute | solution.py:15
  415.6 2.9 convert_element_type.98
  418.5 16.2 %fusion.13 = (bf16[1,768,3584]{2,1,0:T(8,128)(2,1)}, bf16[1,768,3584]{2,1,0:T(8,128)(2,1)}, f32[768]{0:T(1024)S(1)}) fusion(f32[768]{0:T(1024)S(1)} %convert_element_type.96, bf16[1,768,3584]{2,1,0:T(8,128)(2,1)} %param.9, f32[768,3584]{1,0:T(8,128)} %fusion, f32[768,2944]{1,0:T(8,128)S(1)} %convert_element_type.98, f32[768,640]{1,0:T(8,128)S(1)} %fusion.21, ...), kind=kLoop, calls=%fused_computation.26 | loop fusion | flops 57801984 | bytes 49551360 | tf_op jit(solution)/shard_map/broadcast_in_dim | solution.py:164
  434.7 0.1 all_to_all.18
  434.8 9.5 %psum.7 = f32[4,1,192]{2,1,0:T(1,128)S(1)} all-reduce(f32[4,1,192]{2,1,0:T(1,128)S(1)} %all_to_all.18), channel_id=1, replica_groups=mesh['dp'=2,'expert'=4,'tensor'=4] {'tensor'}, use_global_device_ids=true, to_apply=%region_5.6 | all-reduce | flops 768 | bytes 6144 | tf_op jit(solution)/shard_map/psum | solution.py:148
  444.3 6.1 %all_to_all.25 = f32[4,1,192]{2,1,0:T(1,128)S(1)} all-to-all(f32[4,1,192]{2,1,0:T(1,128)S(1)} %psum.7), channel_id=1, replica_groups=mesh['dp'=2,'expert'=4,'tensor'=4] {'expert'}, dimensions={0} | all-to-all | bytes 6144 | tf_op jit(solution)/shard_map/all_to_all | solution.py:149
  450.4 0.1 broadcast_in_dim.76
  450.5 0.3 select_reduce_fusion.1
  450.8 0.6 pad_maximum_fusion.4
  (42 shorter events, 0.2 us)
Async XLA Ops:
  7.2 5.0 %copy-start = (bf16[256,1024]{1,0:T(8,128)(2,1)S(1)}, bf16[256,1024]{1,0:T(8,128)(2,1)}, u32[]{:S(2)}) copy-start(bf16[256,1024]{1,0:T(8,128)(2,1)} %param.6) | copy-start | bytes 1572868
  7.2 106.7 %all-gather.7.cloned.1.call-start = ((), (), s32[]{:S(2)}) async-start(), calls=%async_computation.4 | async-start | bytes 3932160 | tf_op jit(solution)/shard_map/all_gather | solution.py:69
  47.1 127.7 %all-gather.5.cloned.1.call-start = ((), (), s32[]{:S(2)}) async-start(), calls=%async_computation.3 | async-start | bytes 3932160 | tf_op jit(solution)/shard_map/all_gather | solution.py:70
  47.9 165.5 %all-gather.9.cloned.1.call-start = ((), (), s32[]{:S(2)}) async-start(), calls=%async_computation.5 | async-start | bytes 1966080 | tf_op jit(solution)/shard_map/all_gather | solution.py:104
  52.4 61.4 %collective-permute-start = (bf16[384,3584]{1,0:T(8,128)(2,1)}, bf16[384,3584]{1,0:T(8,128)(2,1)}, u32[]{:S(2)}, u32[]{:S(2)}) collective-permute-start(bf16[384,3584]{1,0:T(8,128)(2,1)} %get-tuple-element.61), channel_id=1, source_target_pairs={{0,16},{16,0},{1,17},{17,1},{2,18},{18,2},{3,19},{19,3},{4,20},{20... | collective-permute-start | bytes 8257544 | tf_op jit(solution)/shard_map/ppermute | solution.py:15
  60.2 53.7 %collective-permute-start.1 = (bf16[768]{0:T(1024)(128)(2,1)S(1)}, bf16[768]{0:T(1024)(128)(2,1)S(1)}, u32[]{:S(2)}, u32[]{:S(2)}) collective-permute-start(bf16[768]{0:T(1024)(128)(2,1)S(1)} %reshape.64), channel_id=1, source_target_pairs={{0,16},{16,0},{1,17},{17,1},{2,18},{18,2},{3,19},{19,3},{4,20},{20... | collective-permute-start | bytes 4616 | tf_op jit(solution)/shard_map/ppermute | solution.py:15
  114.9 9.7 %collective-permute-start.2 = (bf16[768,256]{1,0:T(8,128)(2,1)S(1)}, bf16[768,256]{1,0:T(8,128)(2,1)S(1)}, u32[]{:S(2)}, u32[]{:S(2)}) collective-permute-start(bf16[768,256]{1,0:T(8,128)(2,1)S(1)} %constant_dynamic-slice_fusion.7), channel_id=1, source_target_pairs={{0,16},{16,0},{1,17},{17,1},{2,18},{18,2},{3,19},{19,3},{4,20},{20... | collective-permute-start | bytes 1179656 | tf_op jit(solution)/shard_map/ppermute | solution.py:15
  124.5 1.5 copy-start.10
  124.5 93.6 %collective-permute-start.3 = (bf16[384,3584]{1,0:T(8,128)(2,1)S(1)}, bf16[384,3584]{1,0:T(8,128)(2,1)}, u32[]{:S(2)}, u32[]{:S(2)}) collective-permute-start(bf16[384,3584]{1,0:T(8,128)(2,1)S(1)} %get-tuple-element.34), channel_id=1, source_target_pairs={{0,16},{16,0},{1,17},{17,1},{2,18},{18,2},{3,19},{19,3},{4,20},{20... | collective-permute-start | bytes 8257544 | tf_op jit(solution)/shard_map/ppermute | solution.py:15
  126.0 148.0 %all-gather.11.cloned.1.call-start = ((), (), s32[]{:S(2)}) async-start(), calls=%async_computation.6 | async-start | bytes 1966080 | tf_op jit(solution)/shard_map/all_gather | solution.py:106
  213.4 4.7 %copy-start.12 = (bf16[768,256]{1,0:T(8,128)(2,1)S(1)}, bf16[768,256]{1,0:T(8,128)(2,1)}, u32[]{:S(2)}) copy-start(bf16[768,256]{1,0:T(8,128)(2,1)} %constant_dynamic-slice_fusion.8) | copy-start | bytes 1179652
  218.1 19.5 %copy-start.6 = (bf16[768,512]{1,0:T(8,128)(2,1)}, bf16[768,512]{1,0:T(8,128)(2,1)S(1)}, u32[]{:S(2)}) copy-start(bf16[768,512]{1,0:T(8,128)(2,1)S(1)} %get-tuple-element.64) | copy-start | bytes 2359300
  218.1 19.5 %copy-start.7 = (bf16[768,512]{1,0:T(8,128)(2,1)}, bf16[768,512]{1,0:T(8,128)(2,1)S(1)}, u32[]{:S(2)}) copy-start(bf16[768,512]{1,0:T(8,128)(2,1)S(1)} %get-tuple-element.66) | copy-start | bytes 2359300
  218.1 19.5 %copy-start.8 = (bf16[768,512]{1,0:T(8,128)(2,1)}, bf16[768,512]{1,0:T(8,128)(2,1)S(1)}, u32[]{:S(2)}) copy-start(bf16[768,512]{1,0:T(8,128)(2,1)S(1)} %get-tuple-element.81) | copy-start | bytes 2359300
  218.1 19.5 %copy-start.9 = (bf16[768,512]{1,0:T(8,128)(2,1)}, bf16[768,512]{1,0:T(8,128)(2,1)S(1)}, u32[]{:S(2)}) copy-start(bf16[768,512]{1,0:T(8,128)(2,1)S(1)} %get-tuple-element.83) | copy-start | bytes 2359300
  218.1 19.5 %collective-permute-start.4 = (bf16[768,256]{1,0:T(8,128)(2,1)S(1)}, bf16[768,256]{1,0:T(8,128)(2,1)S(1)}, u32[]{:S(2)}, u32[]{:S(2)}) collective-permute-start(bf16[768,256]{1,0:T(8,128)(2,1)S(1)} %copy-done.12), channel_id=1, source_target_pairs={{0,16},{16,0},{1,17},{17,1},{2,18},{18,2},{3,19},{19,3},{4,20},{20... | collective-permute-start | bytes 1179656 | tf_op jit(solution)/shard_map/ppermute | solution.py:15
  237.7 0.8 copy-start.11
  258.3 58.8 %collective-permute-start.5 = (bf16[640,2048]{1,0:T(8,128)(2,1)}, bf16[640,2048]{1,0:T(8,128)(2,1)}, u32[]{:S(2)}, u32[]{:S(2)}) collective-permute-start(bf16[640,2048]{1,0:T(8,128)(2,1)} %slice_bitcast_fusion), channel_id=1, source_target_pairs={{0,16},{16,0},{1,17},{17,1},{2,18},{18,2},{3,19},{19,3},{4,20},{20... | collective-permute-start | bytes 7864328 | tf_op jit(solution)/shard_map/ppermute | solution.py:15
  290.5 44.8 %copy-start.3 = (bf16[768,512]{1,0:T(8,128)(2,1)S(1)}, bf16[768,512]{1,0:T(8,128)(2,1)}, u32[]{:S(2)}) copy-start(bf16[768,512]{1,0:T(8,128)(2,1)} %get-tuple-element.63) | copy-start | bytes 2359300
  290.5 44.8 %copy-start.4 = (bf16[768,512]{1,0:T(8,128)(2,1)S(1)}, bf16[768,512]{1,0:T(8,128)(2,1)}, u32[]{:S(2)}) copy-start(bf16[768,512]{1,0:T(8,128)(2,1)} %get-tuple-element.65) | copy-start | bytes 2359300
  290.5 44.8 %copy-start.5 = (bf16[768,512]{1,0:T(8,128)(2,1)S(1)}, bf16[768,512]{1,0:T(8,128)(2,1)}, u32[]{:S(2)}) copy-start(bf16[768,512]{1,0:T(8,128)(2,1)} %get-tuple-element.82) | copy-start | bytes 2359300
  317.0 98.6 %collective-permute-start.6 = (bf16[768,2944]{1,0:T(8,128)(2,1)}, bf16[768,2944]{1,0:T(8,128)(2,1)}, u32[]{:S(2)}, u32[]{:S(2)}) collective-permute-start(bf16[768,2944]{1,0:T(8,128)(2,1)} %fusion.18), channel_id=1, source_target_pairs={{0,16},{16,0},{1,17},{17,1},{2,18},{18,2},{3,19},{19,3},{4,20},{20... | collective-permute-start | bytes 13565960 | tf_op jit(solution)/shard_map/ppermute | solution.py:15
  335.3 6.2 %copy-start.2 = (bf16[3584,2048]{1,0:T(8,128)(2,1)S(1)}, bf16[3584,2048]{1,0:T(8,128)(2,1)}, u32[]{:S(2)}) copy-start(bf16[3584,2048]{1,0:T(8,128)(2,1)} %convolution_convert_fusion) | copy-start | bytes 44040196
  335.3 83.2 %slice-start = ((s8[5505024]{0:T(1024)(128)(4,1)}), s8[4194304]{0:T(1024)(128)(4,1)S(1)}, s32[]{:S(2)}) async-start(s8[5505024]{0:T(1024)(128)(4,1)} %bitcast.63), calls=%async_computation.7 | async-start | bytes 8388608
  341.5 77.0 %slice-start.1 = ((s8[5505024]{0:T(1024)(128)(4,1)}), s8[1310720]{0:T(1024)(128)(4,1)S(1)}, s32[]{:S(2)}) async-start(s8[5505024]{0:T(1024)(128)(4,1)} %bitcast.63), calls=%async_computation.8 | async-start | bytes 2621440
  418.5 32.9 %copy-start.1 = (bf16[256,1024]{1,0:T(8,128)(2,1)S(1)}, bf16[256,1024]{1,0:T(8,128)(2,1)}, u32[]{:S(2)}) copy-start(bf16[256,1024]{1,0:T(8,128)(2,1)} %param.6) | copy-start | bytes 1572868
Sparse Core Ops, SparseCore 0:
  47.3 63.7 all-gather.6
  112.6 62.1 all-gather.4
  176.9 36.3 all-gather.8
  238.6 35.4 all-gather.10

commit v8 on v5

--- a/solution.py
+++ b/solution.py
@@ -110,12 +110,14 @@
         (partial_back, partial_own, near, down_grad)
     )
     upstream = partial_own + jnp.concatenate((near, partial_back), axis=1)
-
     score = jnp.sum(hidden.astype(jnp.float32) * upstream, axis=1)
+    score, partial_back = lax.optimization_barrier((score, partial_back))
+    every_score = lax.all_gather(score, "tensor")
+    upstream = partial_own + jnp.concatenate((near, partial_back), axis=1)
     hidden_grad = gate_column * upstream
     gate_grad = (hidden_grad * up_float * slope).astype(jnp.bfloat16)
     up_grad = (hidden_grad * active).astype(jnp.bfloat16)
-    summed_scores = lax.psum(score, "tensor")
+    summed_scores = jnp.sum(every_score, axis=0)
     returned = lax.all_to_all(
         summed_scores.reshape(expert_count, capacity),
         "expert",

time: 402 us -> 407 us (1.012)
  other arithmetic: 47.4 us -> 55.1 us
  waiting for transfers between devices: 201 us -> 196 us
    all_gather x0 -> x1, blocking collectives: none -> 13 us  [local(): every_score = lax.all_gather(score, 'tensor')]
    psum x1 -> x0, blocking collectives: 9.31 us -> none  [local(): summed_scores = lax.psum(score, 'tensor')]
    all_to_all x1 -> x0, blocking collectives: 6.55 us -> none  [local(): lax.all_to_all(summed_scores.reshape(expert_count, capacity), 'expert', s...]
    ppermute x5, waiting for transfers between devices: 142 us -> 137 us  [swap_dp(): return lax.ppermute(value, 'dp', perm=[(0, 1), (1, 0)])]
    convert_element_type x1, other arithmetic: 15.6 us -> 19.6 us  [local(): (rounded_own.astype(jnp.float32) + rounded_other.astype(jnp.float32)).ast...]
  transfers between devices with their start and end apart: 7 -> 8, of which waited for: 4 -> 4; matrix products, arithmetic and copies ran while one was open for 24% -> 29% of each run, Pallas kernels for 0% -> 0%
where the time goes in v8:
time: 407 us
  waiting for transfers between devices  196 us (48%)
  matrix products  74.3 us (18%)
  other arithmetic  55.1 us (14%)
  blocking collectives  43.4 us (11%)
  between operations  14.3 us (4%)
  local copies, waits for them, and re-layouts  13.7 us (3%)
  starting transfers between devices  10.3 us (3%)
    ppermute x5, waiting for transfers between devices, swap_dp(): return lax.ppermute(value, 'dp', perm=[(0, 1), (1, 0)])  137 us
    all_gather x1, waiting for transfers between devices, local(): other_rows = lax.all_gather(other_piece, 'tensor', axis=1, tiled=True)  59.1 us
    all_to_all x1, blocking collectives, local(): lax.all_to_all(outgoing, 'expert', split_axis=0, concat_axis=0, tiled=True)  24.2 us
    convert_element_type x1, other arithmetic, local(): (rounded_own.astype(jnp.float32) + rounded_other.astype(jnp.float32)).ast...  19.6 us
    dot_general x1, matrix products, local(): lax.dot_general(hidden_other, scaled_other, contract_rows, preferred_elem...  17.5 us
    broadcast_in_dim x1, other arithmetic, local(): return (gate_grad[None], up_grad[None], down_grad[None], router_grad)  17.3 us
    dot_general x1, matrix products, local(): lax.dot_general(own_rows, local_weight, contract_cols, preferred_element_...  15.8 us
    dot_general x1, matrix products, local(): lax.dot_general(other_rows, local_weight[moved:], contract_cols, preferre...  15.4 us
  transfers between devices with their start and end apart: 8, of which 4 were waited for; matrix products, arithmetic and copies ran while one was open for 29% of the time, Pallas kernels for 0%

profile of v8, /device:TPU:0, one launch (start us, length us, event | category | flops | bytes accessed | tf_op | source)
XLA Modules:
  0.0 406.6 jit_solution(17571677970908781674)
XLA Ops:
  7.2 0.0 copy-start
  7.2 0.0 all-gather.5.cloned.1.call-start
  7.2 0.9 copy.32
  8.1 0.1 eq.59
  8.2 0.1 eq.55
  8.4 1.2 reduce-window.6
  9.6 0.2 slice_reduce_fusion
  9.8 0.2 reduce-window.9
  10.0 0.1 add_bitcast_fusion
  10.1 0.1 reduce_sum.57
  10.3 0.1 copy.34
  10.3 0.7 multiply_add_fusion
  11.1 0.8 slice_convert_fusion.1
  11.8 0.2 select_reduce_fusion.2
  12.0 0.1 convert_element_type.95
  12.1 0.0 copy-done
  12.1 0.8 convolution_convert_fusion.2
  12.9 8.9 %fusion.2 = bf16[768,3584]{1,0:T(8,128)(2,1)} fusion(bf16[1,768,3584]{2,1,0:T(8,128)(2,1)} %param.10, bf16[1,768,3584]{2,1,0:T(8,128)(2,1)} %param.9), kind=kLoop, calls=%fused_computation.12 | loop fusion | flops 22020096 | bytes 16515072 | tf_op jit(solution)/shard_map/convert_element_type | solution.py:49
  21.7 24.2 %all_to_all.23 = bf16[4,192,1024]{2,1,0:T(8,128)(2,1)} all-to-all(bf16[4,192,1024]{2,1,0:T(8,128)(2,1)S(1)} %bitcast.71), channel_id=1, replica_groups=mesh['dp'=2,'expert'=4,'tensor'=4] {'expert'}, dimensions={0} | all-to-all | bytes 3145728 | tf_op jit(solution)/shard_map/all_to_all | solution.py:60
  46.0 0.0 all-gather.5.cloned.1.call-update
  46.0 0.0 all-gather.7.cloned.1.call-start
  46.0 2.1 collective-permute-start
  48.1 6.1 %all_to_all.24 = bf16[4,1,192]{2,1,0:T(2,128)(2,1)S(1)} all-to-all(bf16[4,1,192]{2,1,0:T(2,128)(2,1)S(1)} %copy.35), channel_id=1, replica_groups=mesh['dp'=2,'expert'=4,'tensor'=4] {'expert'}, dimensions={0} | all-to-all | bytes 3072 | tf_op jit(solution)/shard_map/all_to_all | solution.py:59
  54.3 0.1 reshape.64
  54.4 0.0 collective-permute-start.1
  54.4 112.4 %collective-permute-done.1 = bf16[768]{0:T(1024)(128)(2,1)S(1)} collective-permute-done((bf16[768]{0:T(1024)(128)(2,1)S(1)}, bf16[768]{0:T(1024)(128)(2,1)S(1)}, u32[]{:S(2)}, u32[]{:S(2)}) %collective-permute-start.1) | collective-permute-done | bytes 1568 | tf_op jit(solution)/shard_map/ppermute | solution.py:15
  166.8 0.0 collective-permute-done
  166.8 1.2 constant_dynamic-slice_fusion.1
  168.0 1.8 collective-permute-start.2
  169.8 4.4 %slice_bitcast_fusion = bf16[896,2048]{1,0:T(8,128)(2,1)} fusion(bf16[1,3584,2048]{2,1,0:T(8,128)(2,1)} %param.11), kind=kLoop, calls=%fused_computation.34 | loop fusion | bytes 7340032 | tf_op jit(solution)/shard_map/slice | solution.py:79
  174.1 12.2 %collective-permute-done.2 = bf16[768,512]{1,0:T(8,128)(2,1)S(1)} collective-permute-done((bf16[768,512]{1,0:T(8,128)(2,1)S(1)}, bf16[768,512]{1,0:T(8,128)(2,1)S(1)}, u32[]{:S(2)}, u32[]{:S(2)}) %collective-permute-start.2) | collective-permute-done | bytes 786464 | tf_op jit(solution)/shard_map/ppermute | solution.py:15
  186.4 0.9 copy-done.6
  187.2 0.0 all-gather.7.cloned.1.call-update
  187.3 1.5 collective-permute-start.3
  188.8 3.9 constant_dynamic-slice_fusion
  192.7 59.1 %all-gather.7.cloned.1.call-done = bf16[768,2048]{1,0:T(8,128)(2,1)} async-done(((bf16[768,512]{1,0:T(8,128)(2,1)}), bf16[768,2048]{1,0:T(8,128)(2,1)}) %all-gather.7.cloned.1.call-update) | async-done | bytes 3145744 | tf_op jit(solution)/shard_map/all_gather | solution.py:81
  251.8 15.4 %fusion.20 = bf16[768,2688]{1,0:T(8,128)(2,1)} fusion(bf16[768,2048]{1,0:T(8,128)(2,1)} %all-gather.7.cloned.1.call-done, bf16[1,3584,2048]{2,1,0:T(8,128)(2,1)} %param.11), kind=kOutput, calls=%fused_computation.33 | convolution fusion | flops 8457781248 | bytes 18284544 | tf_op jit(solution)/shard_map/dot_general | solution.py:85
  267.2 0.0 collective-permute-done.3
  267.2 1.5 collective-permute-start.4
  268.8 0.0 copy-done.7
  268.8 17.5 %convolution_convert_fusion = bf16[3584,2048]{1,0:T(8,128)(2,1)} fusion(bf16[768,3584]{1,0:T(8,128)(2,1)} %collective-permute-done, bf16[768,2048]{1,0:T(8,128)(2,1)S(1)} %copy-done.7, f32[768]{0:T(1024)S(1)} %convert_element_type.103), kind=kOutput, calls=%fused_computation.4 | convolution fusion | flops 11286347776 | bytes 23333888 | tf_op jit(solution)/shard_map/dot_general | solution.py:101
  286.3 0.0 slice-done
  286.3 0.0 slice-done.1
  286.3 0.0 copy-done.5
  286.3 14.4 %convolution_convert_fusion.1 = bf16[3584,2048]{1,0:T(8,128)(2,1)} fusion(bf16[768,3584]{1,0:T(8,128)(2,1)S(1)} %bitcast.66, bf16[768,2048]{1,0:T(8,128)(2,1)S(1)} %copy-done.5, f32[768]{0:T(1024)S(1)} %convert_element_type.96), kind=kOutput, calls=%fused_computation.5 | convolution fusion | flops 11286347776 | bytes 23333888 | tf_op jit(solution)/shard_map/dot_general | solution.py:100
  300.7 15.8 %fusion = f32[768,3584]{1,0:T(8,128)S(1)} fusion(bf16[768,2048]{1,0:T(8,128)(2,1)} %constant_dynamic-slice_fusion, bf16[1,3584,2048]{2,1,0:T(8,128)(2,1)} %param.11), kind=kOutput, calls=%fused_computation.6 | convolution fusion | flops 11274289152 | bytes 28835840 | tf_op jit(solution)/shard_map/dot_general | solution.py:92
  316.5 0.0 copy-start.3
  316.5 0.0 slice-start.2
  316.5 10.4 %fusion.25 = f32[768,896]{1,0:T(8,128)S(1)} fusion(bf16[896,2048]{1,0:T(8,128)(2,1)} %collective-permute-done.3, bf16[768,4096]{1,0:T(8,128)(2,1)} %all-gather.5.cloned.1.call-done, s32[]{:T(128)S(6)} %select_n.36), kind=kOutput, calls=%fused_computation.37 | convolution fusion | flops 2818572288 | bytes 9568260 | tf_op jit(solution)/shard_map/dot_general | solution.py:96
  326.9 0.0 slice-start.3
  326.9 19.6 %add_convert_fusion = bf16[3584,2048]{1,0:T(8,128)(2,1)} fusion(bf16[3584,2048]{1,0:T(8,128)(2,1)} %convolution_convert_fusion, bf16[3584,2048]{1,0:T(8,128)(2,1)} %convolution_convert_fusion.1), kind=kLoop, calls=%fused_computation | loop fusion | flops 29360128 | bytes 44040192 | tf_op jit(solution)/shard_map/convert_element_type | solution.py:106
  346.6 11.9 %collective-permute-done.4 = bf16[768,2688]{1,0:T(8,128)(2,1)} collective-permute-done((bf16[768,2688]{1,0:T(8,128)(2,1)}, bf16[768,2688]{1,0:T(8,128)(2,1)}, u32[]{:S(2)}, u32[]{:S(2)}) %collective-permute-start.4) | collective-permute-done | bytes 4128800 | tf_op jit(solution)/shard_map/ppermute | solution.py:15
  358.5 2.7 convert_element_type.98
  361.3 2.4 fusion.9
  363.7 0.8 copy-done.2
  364.4 13.0 %all-gather.1 = f32[4,1,768]{2,1,0:T(1,128)S(1)} all-gather(f32[1,1,768]{2,1,0:T(1,128)S(1)} %reshape.71), channel_id=2, replica_groups=mesh['dp'=2,'expert'=4,'tensor'=4] {'tensor'}, dimensions={0}, use_global_device_ids=true | all-gather | bytes 15360 | tf_op jit(solution)/shard_map/all_gather | solution.py:115
  377.5 0.7 all_to_all.18
  378.2 3.2 all-to-all-start.2
  381.4 0.0 copy-start.1
  381.4 17.3 %fusion.18 = (bf16[1,768,3584]{2,1,0:T(8,128)(2,1)}, bf16[1,768,3584]{2,1,0:T(8,128)(2,1)}) fusion(bf16[1,768,3584]{2,1,0:T(8,128)(2,1)} %param.9, f32[768,3584]{1,0:T(8,128)} %copy-done.3, f32[768,2688]{1,0:T(8,128)} %copy-done.2, f32[768,896]{1,0:T(8,128)} %copy-done.4, f32[768]{0:T(1024)S(1)} %convert_element_type.96, bf16[1,768,3584]{2,1,0:T(8,128)(2,1)} %param.10), kind=kLoop, calls=%fused_computation.31 | loop fusion | flops 49545216 | bytes 44043264 | tf_op jit(solution)/shard_map/broadcast_in_dim | solution.py:136
  398.7 0.0 all-to-all-done.2
  398.7 0.1 broadcast_in_dim.76
  398.8 0.3 select_reduce_fusion.1
  399.2 0.6 pad_maximum_fusion.2
  (25 shorter events, 0.1 us)
Async XLA Ops:
  7.2 5.0 %copy-start = (bf16[256,1024]{1,0:T(8,128)(2,1)S(1)}, bf16[256,1024]{1,0:T(8,128)(2,1)}, u32[]{:S(2)}) copy-start(bf16[256,1024]{1,0:T(8,128)(2,1)} %param.6) | copy-start | bytes 1572868
  7.2 159.6 %all-gather.5.cloned.1.call-start = ((), (), s32[]{:S(2)}) async-start(), calls=%async_computation.3 | async-start | bytes 7864320 | tf_op jit(solution)/shard_map/all_gather | solution.py:66
  46.0 205.8 %all-gather.7.cloned.1.call-start = ((), (), s32[]{:S(2)}) async-start(), calls=%async_computation.4 | async-start | bytes 3932160 | tf_op jit(solution)/shard_map/all_gather | solution.py:81
  46.0 120.7 %collective-permute-start = (bf16[768,3584]{1,0:T(8,128)(2,1)}, bf16[768,3584]{1,0:T(8,128)(2,1)}, u32[]{:S(2)}, u32[]{:S(2)}) collective-permute-start(bf16[768,3584]{1,0:T(8,128)(2,1)} %fusion.2), channel_id=1, source_target_pairs={{0,16},{16,0},{1,17},{17,1},{2,18},{18,2},{3,19},{19,3},{4,20},{20... | collective-permute-start | bytes 16515080 | tf_op jit(solution)/shard_map/ppermute | solution.py:15
  54.4 112.4 %collective-permute-start.1 = (bf16[768]{0:T(1024)(128)(2,1)S(1)}, bf16[768]{0:T(1024)(128)(2,1)S(1)}, u32[]{:S(2)}, u32[]{:S(2)}) collective-permute-start(bf16[768]{0:T(1024)(128)(2,1)S(1)} %reshape.64), channel_id=1, source_target_pairs={{0,16},{16,0},{1,17},{17,1},{2,18},{18,2},{3,19},{19,3},{4,20},{20... | collective-permute-start | bytes 4616 | tf_op jit(solution)/shard_map/ppermute | solution.py:15
  168.0 18.4 %collective-permute-start.2 = (bf16[768,512]{1,0:T(8,128)(2,1)S(1)}, bf16[768,512]{1,0:T(8,128)(2,1)S(1)}, u32[]{:S(2)}, u32[]{:S(2)}) collective-permute-start(bf16[768,512]{1,0:T(8,128)(2,1)S(1)} %constant_dynamic-slice_fusion.1), channel_id=1, source_target_pairs={{0,16},{16,0},{1,17},{17,1},{2,18},{18,2},{3,19},{19,3},{4,20},{20... | collective-permute-start | bytes 2359304 | tf_op jit(solution)/shard_map/ppermute | solution.py:15
  186.4 0.9 copy-start.6
  187.3 80.0 %collective-permute-start.3 = (bf16[896,2048]{1,0:T(8,128)(2,1)}, bf16[896,2048]{1,0:T(8,128)(2,1)}, u32[]{:S(2)}, u32[]{:S(2)}) collective-permute-start(bf16[896,2048]{1,0:T(8,128)(2,1)} %slice_bitcast_fusion), channel_id=1, source_target_pairs={{0,16},{16,0},{1,17},{17,1},{2,18},{18,2},{3,19},{19,3},{4,20},{20... | collective-permute-start | bytes 11010056 | tf_op jit(solution)/shard_map/ppermute | solution.py:15
  251.8 17.0 %copy-start.7 = (bf16[768,2048]{1,0:T(8,128)(2,1)S(1)}, bf16[768,2048]{1,0:T(8,128)(2,1)}, u32[]{:S(2)}) copy-start(bf16[768,2048]{1,0:T(8,128)(2,1)} %all-gather.7.cloned.1.call-done) | copy-start | bytes 9437188
  251.8 34.5 %slice-start = ((s8[5505024]{0:T(1024)(128)(4,1)}), s8[1310720]{0:T(1024)(128)(4,1)S(1)}, s32[]{:S(2)}) async-start(s8[5505024]{0:T(1024)(128)(4,1)} %bitcast.65), calls=%async_computation.5 | async-start | bytes 2621440
  267.2 19.1 %slice-start.1 = ((s8[5505024]{0:T(1024)(128)(4,1)}), s8[4194304]{0:T(1024)(128)(4,1)S(1)}, s32[]{:S(2)}) async-start(s8[5505024]{0:T(1024)(128)(4,1)} %bitcast.65), calls=%async_computation.6 | async-start | bytes 8388608
  267.2 19.1 %copy-start.5 = (bf16[768,2048]{1,0:T(8,128)(2,1)S(1)}, bf16[768,2048]{1,0:T(8,128)(2,1)}, u32[]{:S(2)}) copy-start(bf16[768,2048]{1,0:T(8,128)(2,1)} %constant_dynamic-slice_fusion) | copy-start | bytes 9437188
  267.2 91.3 %collective-permute-start.4 = (bf16[768,2688]{1,0:T(8,128)(2,1)}, bf16[768,2688]{1,0:T(8,128)(2,1)}, u32[]{:S(2)}, u32[]{:S(2)}) collective-permute-start(bf16[768,2688]{1,0:T(8,128)(2,1)} %fusion.20), channel_id=1, source_target_pairs={{0,16},{16,0},{1,17},{17,1},{2,18},{18,2},{3,19},{19,3},{4,20},{20... | collective-permute-start | bytes 12386312 | tf_op jit(solution)/shard_map/ppermute | solution.py:15
  316.5 44.8 %copy-start.3 = (f32[768,3584]{1,0:T(8,128)}, f32[768,3584]{1,0:T(8,128)S(1)}, u32[]{:S(2)}) copy-start(f32[768,3584]{1,0:T(8,128)S(1)} %fusion) | copy-start | bytes 33030148
  316.5 44.8 %slice-start.2 = ((s8[5505024]{0:T(1024)(128)(4,1)}), s8[4194304]{0:T(1024)(128)(4,1)S(1)}, s32[]{:S(2)}) async-start(s8[5505024]{0:T(1024)(128)(4,1)} %bitcast.67), calls=%async_computation.7 | async-start | bytes 8388608
  326.9 34.3 %copy-start.4 = (f32[768,896]{1,0:T(8,128)}, f32[768,896]{1,0:T(8,128)S(1)}, u32[]{:S(2)}) copy-start(f32[768,896]{1,0:T(8,128)S(1)} %fusion.25) | copy-start | bytes 8257540
  326.9 34.3 %slice-start.3 = ((s8[5505024]{0:T(1024)(128)(4,1)}), s8[1310720]{0:T(1024)(128)(4,1)S(1)}, s32[]{:S(2)}) async-start(s8[5505024]{0:T(1024)(128)(4,1)} %bitcast.67), calls=%async_computation.8 | async-start | bytes 2621440
  361.3 3.2 copy-start.2
  378.2 20.6 %all-to-all-start.2 = ((f32[4,1,192]{2,1,0:T(1,128)}), f32[4,1,192]{2,1,0:T(1,128)S(1)}, u32[]{:S(2)}, u32[]{:S(2)}) async-start(f32[4,1,192]{2,1,0:T(1,128)} %all_to_all.18), calls=%async_computation.2 | async-start | bytes 8192 | tf_op jit(solution)/shard_map/all_to_all | solution.py:121
  381.4 18.4 %copy-start.1 = (bf16[256,1024]{1,0:T(8,128)(2,1)S(1)}, bf16[256,1024]{1,0:T(8,128)(2,1)}, u32[]{:S(2)}) copy-start(bf16[256,1024]{1,0:T(8,128)(2,1)} %param.6) | copy-start | bytes 1572868
Sparse Core Ops, SparseCore 0:
  46.1 116.1 all-gather.4
  187.4 64.3 all-gather.6

commit v9 on v2

--- a/solution.py
+++ b/solution.py
@@ -39,6 +39,8 @@
         )
     gate_send = jnp.sum(gate_table, axis=0).astype(jnp.bfloat16).reshape(expert_count, capacity)
 
+    local_weight = down_weight[0]
+
     gate_float = gate_preact[0].astype(jnp.float32)
     up_float = up_preact[0].astype(jnp.float32)
     active, slope = silu_parts(gate_float)
@@ -51,7 +53,6 @@
     )
     outgoing = outgoing.astype(jnp.bfloat16).reshape(expert_count, capacity, -1)
     hidden, outgoing, gate_send = lax.optimization_barrier((hidden, outgoing, gate_send))
-    hidden_other = swap_dp(hidden)
     gate_slots = lax.all_to_all(gate_send, "expert", split_axis=0, concat_axis=0, tiled=True)
     received = lax.all_to_all(outgoing, "expert", split_axis=0, concat_axis=0, tiled=True)
     slots = expert_count * capacity
@@ -59,27 +60,37 @@
     gate_bf16 = gate_slots.reshape(-1)
     gate_column = gate_bf16.astype(jnp.float32)[:, None]
     other_gates = swap_dp(gate_bf16)
-    fragment = lax.all_gather(narrow_rows, "tensor", axis=1, tiled=True)
-
-    width = fragment.shape[1]
+    narrow = narrow_rows.shape[1]
+    width = narrow * tensor_count
     half = width // 2
-    piece = half // tensor_count
+    quarters = tensor_count // 2
+    chunk = narrow // tensor_count
+    mixed = lax.all_to_all(narrow_rows, "tensor", split_axis=1, concat_axis=1, tiled=True)
+    send_rows = lax.dynamic_slice_in_dim(mixed, (1 - replica) * (narrow // 2), narrow // 2, axis=1)
+    other_piece = swap_dp(send_rows)
+    hidden_send, other_piece, other_gates = lax.optimization_barrier(
+        (hidden, other_piece, other_gates)
+    )
+    hidden_other = swap_dp(hidden_send)
+    gathered = lax.all_gather(other_piece, "tensor", axis=1, tiled=True)
+    rows_for_gather, gathered = lax.optimization_barrier((narrow_rows, gathered))
+    fragment = lax.all_gather(rows_for_gather, "tensor", axis=1, tiled=True)
+    gathered, hidden_other = lax.optimization_barrier((gathered, hidden_other))
+    blocks = []
+    for quarter in range(quarters):
+        for source in range(tensor_count):
+            begin = source * (narrow // 2) + quarter * chunk
+            blocks.append(gathered[:, begin : begin + chunk])
+    other_rows = jnp.concatenate(blocks, axis=1)
     own_rows = lax.dynamic_slice_in_dim(fragment, replica * half, half, axis=1)
-    send_rows = lax.dynamic_slice_in_dim(
-        fragment, (1 - replica) * half + part * piece, piece, axis=1
-    )
-    other_piece = swap_dp(send_rows)
-    other_rows = lax.all_gather(other_piece, "tensor", axis=1, tiled=True)
-    hidden_other, other_rows, other_gates = lax.optimization_barrier(
-        (hidden_other, other_rows, other_gates)
-    )
     other_gates = other_gates.astype(jnp.float32)[:, None]
 
-    local_weight = down_weight[0]
     partial_other = lax.dot_general(
         other_rows, local_weight, contract_cols, preferred_element_type=jnp.float32
     )
-    partial_back = swap_dp(partial_other.astype(PARTIAL_DTYPE)).astype(jnp.float32)
+    units = local_weight.shape[0]
+    first_units = units // 2 // 128 * 128
+    partial_first = swap_dp(partial_other[:, :first_units].astype(PARTIAL_DTYPE))
     partial_own = lax.dot_general(
         own_rows, local_weight, contract_cols, preferred_element_type=jnp.float32
     )
@@ -91,13 +102,18 @@
         hidden_other, scaled_other, contract_rows, preferred_element_type=jnp.float32
     )
     rounded_own = lax.optimization_barrier(grad_own.astype(jnp.bfloat16))
+    partial_rest, partial_own, rounded_own = lax.optimization_barrier(
+        (partial_other[:, first_units:].astype(PARTIAL_DTYPE), partial_own, rounded_own)
+    )
+    partial_second = swap_dp(partial_rest)
     rounded_other = lax.optimization_barrier(grad_other.astype(jnp.bfloat16))
     down_grad = (rounded_own.astype(jnp.float32) + rounded_other.astype(jnp.float32)).astype(
         jnp.bfloat16
     )
-    partial_back, partial_own, down_grad = lax.optimization_barrier(
-        (partial_back, partial_own, down_grad)
+    partial_first, partial_second, partial_own, down_grad = lax.optimization_barrier(
+        (partial_first, partial_second, partial_own, down_grad)
     )
+    partial_back = jnp.concatenate((partial_first, partial_second), axis=1).astype(jnp.float32)
     upstream = partial_own + partial_back
 
     score = jnp.sum(hidden.astype(jnp.float32) * upstream, axis=1)

time: 433 us -> 431 us (level)
  waiting for transfers between devices: 240 us -> 219 us
  local copies, waits for them, and re-layouts: 4.71 us -> 22 us
  blocking collectives: 40.1 us -> 45.4 us
    all_gather x2, waiting for transfers between devices: 134 us -> 74.7 us  [the longest x1 60 us: local(): gathered = lax.all_gather(other_piece, 'tensor', axis=1, tiled=True)]
    all_to_all x1, waiting for transfers between devices: 3.75 us -> 36.7 us  [local(): lax.all_to_all(narrow_rows, 'tensor', split_axis=1, concat_axis=1, tiled=...]
    all_to_all x0 -> x3, local copies, waits for them, and re-layouts: none -> 7.81 us  [local(): lax.all_to_all(narrow_rows, 'tensor', split_axis=1, concat_axis=1, tiled=...]
    unnamed x17 -> x32, local copies, waits for them, and re-layouts: 1.77 us -> 8.98 us
    all_to_all x0 -> x1, blocking collectives: none -> 6.11 us  [local(): lax.all_to_all(gate_send, 'expert', split_axis=0, concat_axis=0, tiled=True)]
    ppermute x4 -> x5, waiting for transfers between devices: 102 us -> 108 us  [swap_dp(): return lax.ppermute(value, 'dp', perm=[(0, 1), (1, 0)])]
    dot_general x1, matrix products: 19.4 us -> 15 us  [local(): lax.dot_general(other_rows, local_weight, contract_cols, preferred_elemen...]
  transfers between devices with their start and end apart: 7 -> 8, of which waited for: 5 -> 6; matrix products, arithmetic and copies ran while one was open for 17% -> 23% of each run, Pallas kernels for 0% -> 0%
where the time goes in v9:
time: 431 us; the launch traced here: 430 us
  waiting for transfers between devices  219 us (51%)
  matrix products  69.2 us (16%)
  other arithmetic  48 us (11%)
  blocking collectives  45.4 us (11%)
  local copies, waits for them, and re-layouts  22 us (5%)
  between operations  14.2 us (3%)
  starting transfers between devices  11.8 us (3%)
    ppermute x5, waiting for transfers between devices, swap_dp(): return lax.ppermute(value, 'dp', perm=[(0, 1), (1, 0)])  108 us
    all_gather x1, waiting for transfers between devices, local(): gathered = lax.all_gather(other_piece, 'tensor', axis=1, tiled=True)  60 us
    all_to_all x1, waiting for transfers between devices, local(): lax.all_to_all(narrow_rows, 'tensor', split_axis=1, concat_axis=1, tiled=...  36.7 us
    all_to_all x1, blocking collectives, local(): lax.all_to_all(outgoing, 'expert', split_axis=0, concat_axis=0, tiled=True)  24.1 us
    convert_element_type x1, other arithmetic, local(): (rounded_own.astype(jnp.float32) + rounded_other.astype(jnp.float32)).ast...  20.3 us
    dot_general x1, matrix products, local(): lax.dot_general(hidden, scaled_own, contract_rows, preferred_element_type...  18.2 us
    dot_general x1, matrix products, local(): lax.dot_general(own_rows, local_weight, contract_cols, preferred_element_...  17.3 us
    dot_general x1, matrix products, local(): lax.dot_general(hidden_other, scaled_other, contract_rows, preferred_elem...  16.8 us
  transfers between devices with their start and end apart: 8, of which 6 were waited for; matrix products, arithmetic and copies ran while one was open for 23% of the time, Pallas kernels for 0%

profile of v9, /device:TPU:0, one launch (start us, length us, event | category | flops | bytes accessed | tf_op | source)
XLA Modules:
  0.0 429.7 jit_solution(12144033170993894400)
XLA Ops:
  7.2 0.0 copy-start
  7.2 0.9 copy.36
  8.1 0.1 eq.59
  8.2 0.1 eq.55
  8.4 1.2 reduce-window.6
  9.6 0.2 slice_reduce_fusion
  9.8 0.2 reduce-window.9
  10.0 0.1 add_bitcast_fusion
  10.1 0.1 reduce_sum.48
  10.2 0.1 copy.38
  10.3 0.7 multiply_add_fusion
  11.0 0.8 slice_convert_fusion.1
  11.8 1.9 convolution_convert_fusion.2
  13.7 0.2 select_reduce_fusion.2
  13.9 0.1 convert_element_type.94
  14.0 9.0 %fusion.4 = bf16[768,3584]{1,0:T(8,128)(2,1)} fusion(bf16[1,768,3584]{2,1,0:T(8,128)(2,1)} %param.10, bf16[1,768,3584]{2,1,0:T(8,128)(2,1)} %param.9), kind=kLoop, calls=%fused_computation.12 | loop fusion | flops 22020096 | bytes 16515072 | tf_op jit(solution)/shard_map/convert_element_type | solution.py:47
  23.0 24.1 %all_to_all.35 = bf16[4,192,1024]{2,1,0:T(8,128)(2,1)S(1)} all-to-all(bf16[4,192,1024]{2,1,0:T(8,128)(2,1)S(1)} %bitcast.70), channel_id=1, replica_groups=mesh['dp'=2,'expert'=4,'tensor'=4] {'expert'}, dimensions={0} | all-to-all | bytes 3145728 | tf_op jit(solution)/shard_map/all_to_all | solution.py:57
  47.1 2.5 all_to_all.26
  49.6 2.8 copy.40
  52.3 4.9 %all-to-all-start.2 = ((bf16[768,4,256]{2,0,1:T(8,128)(2,1)}), bf16[768,4,256]{2,0,1:T(8,128)(2,1)}, u32[]{:S(2)}, u32[]{:S(2)}) async-start(bf16[768,4,256]{2,0,1:T(8,128)(2,1)} %copy.40), calls=%async_computation.2 | async-start | bytes 3145728 | tf_op jit(solution)/shard_map/all_to_all | solution.py:68
  57.2 36.7 %all-to-all-done.2 = bf16[768,4,256]{2,0,1:T(8,128)(2,1)} async-done(((bf16[768,4,256]{2,0,1:T(8,128)(2,1)}), bf16[768,4,256]{2,0,1:T(8,128)(2,1)}, u32[]{:S(2)}, u32[]{:S(2)}) %all-to-all-start.2) | async-done | bytes 1572896 | tf_op jit(solution)/shard_map/all_to_all | solution.py:68
  93.9 2.6 copy.41
  96.5 1.2 constant_dynamic-slice_fusion
  97.6 1.6 collective-permute-start
  99.2 6.1 %all_to_all.36 = bf16[4,1,192]{2,1,0:T(2,128)(2,1)S(1)} all-to-all(bf16[4,1,192]{2,1,0:T(2,128)(2,1)S(1)} %copy.39), channel_id=1, replica_groups=mesh['dp'=2,'expert'=4,'tensor'=4] {'expert'}, dimensions={0} | all-to-all | bytes 3072 | tf_op jit(solution)/shard_map/all_to_all | solution.py:56
  105.3 0.1 reshape.65
  105.4 0.5 collective-permute-start.1
  106.0 10.3 %collective-permute-done.1 = bf16[768]{0:T(1024)(128)(2,1)S(1)} collective-permute-done((bf16[768]{0:T(1024)(128)(2,1)S(1)}, bf16[768]{0:T(1024)(128)(2,1)S(1)}, u32[]{:S(2)}, u32[]{:S(2)}) %collective-permute-start.1) | collective-permute-done | bytes 1568 | tf_op jit(solution)/shard_map/ppermute | solution.py:15
  116.3 0.9 copy-done.4
  117.1 0.0 all-gather.3.cloned.1.call-update
  117.2 0.2 all-gather.5.cloned.1.call-start
  117.4 1.6 collective-permute-start.2
  119.0 60.0 %all-gather.3.cloned.1.call-done = bf16[768,2048]{0,1:T(8,128)(2,1)} async-done(((bf16[768,512]{0,1:T(8,128)(2,1)}), bf16[768,2048]{0,1:T(8,128)(2,1)}) %all-gather.3.cloned.1.call-update) | async-done | bytes 3145744 | tf_op jit(solution)/shard_map/all_gather | solution.py:75
  178.9 0.0 all-gather.5.cloned.1.call-update
  179.0 57.5 %collective-permute-done.2 = bf16[768,3584]{1,0:T(8,128)(2,1)} collective-permute-done((bf16[768,3584]{1,0:T(8,128)(2,1)}, bf16[768,3584]{1,0:T(8,128)(2,1)}, u32[]{:S(2)}, u32[]{:S(2)}) %collective-permute-start.2) | collective-permute-done | bytes 5505056 | tf_op jit(solution)/shard_map/ppermute | solution.py:15
  236.5 1.0 slice_dynamic-update-slice_fusion.7
  237.5 1.0 slice_dynamic-update-slice_fusion.6
  238.5 1.0 slice_dynamic-update-slice_fusion.5
  239.6 1.0 slice_dynamic-update-slice_fusion.4
  240.6 1.0 slice_dynamic-update-slice_fusion.3
  241.6 1.0 slice_dynamic-update-slice_fusion.2
  242.6 1.0 slice_dynamic-update-slice_fusion.1
  243.7 1.0 slice_dynamic-update-slice_fusion
  244.7 15.0 %fusion.12 = bf16[768,3584]{1,0:T(8,128)(2,1)S(1)} fusion(bf16[768,2048]{0,1:T(8,128)(2,1)S(1)} %slice_dynamic-update-slice_fusion, bf16[1,3584,2048]{2,1,0:T(8,128)(2,1)} %param.11), kind=kOutput, calls=%fused_computation.23 | convolution fusion | flops 11277041664 | bytes 23330816 | tf_op jit(solution)/shard_map/dot_general | solution.py:88
  259.7 1.9 fusion.37
  261.6 1.5 collective-permute-start.3
  263.1 16.8 %convolution_convert_fusion = bf16[3584,2048]{1,0:T(8,128)(2,1)} fusion(bf16[768,3584]{1,0:T(8,128)(2,1)} %collective-permute-done.2, bf16[768,2048]{0,1:T(8,128)(2,1)S(1)} %slice_dynamic-update-slice_fusion, f32[768]{0:T(1024)S(1)} %convert_element_type.100), kind=kOutput, calls=%fused_computation.4 | convolution fusion | flops 11286347776 | bytes 23333888 | tf_op jit(solution)/shard_map/dot_general | solution.py:101
  279.8 14.7 %all-gather.5.cloned.1.call-done = bf16[768,4096]{1,0:T(8,128)(2,1)} async-done(((bf16[768,1024]{1,0:T(8,128)(2,1)}), bf16[768,4096]{1,0:T(8,128)(2,1)}) %all-gather.5.cloned.1.call-update) | async-done | bytes 6291472 | tf_op jit(solution)/shard_map/all_gather | solution.py:77
  294.5 18.2 %convolution_convert_fusion.1 = bf16[3584,2048]{1,0:T(8,128)(2,1)} fusion(bf16[768,3584]{1,0:T(8,128)(2,1)} %fusion.4, f32[768]{0:T(1024)S(1)} %convert_element_type.95, bf16[768,4096]{1,0:T(8,128)(2,1)} %all-gather.5.cloned.1.call-done, s32[]{:T(128)S(6)} %select_n.32), kind=kOutput, calls=%fused_computation.5 | convolution fusion | flops 11286347776 | bytes 23333892 | tf_op jit(solution)/shard_map/dot_general | solution.py:100
  312.8 17.3 %fusion = f32[768,3584]{1,0:T(8,128)} fusion(bf16[1,3584,2048]{2,1,0:T(8,128)(2,1)} %param.11, bf16[768,4096]{1,0:T(8,128)(2,1)S(1)} %copy-done.5, s32[]{:T(128)S(6)} %select_n.32), kind=kOutput, calls=%fused_computation.6 | convolution fusion | flops 11274289152 | bytes 28835844 | tf_op jit(solution)/shard_map/dot_general | solution.py:94
  330.1 0.0 slice-start.3
  330.1 0.0 slice-start.5
  330.1 1.5 collective-permute-start.4
  331.7 20.3 %add_convert_fusion = bf16[3584,2048]{1,0:T(8,128)(2,1)} fusion(bf16[3584,2048]{1,0:T(8,128)(2,1)} %convolution_convert_fusion, bf16[3584,2048]{1,0:T(8,128)(2,1)} %convolution_convert_fusion.1), kind=kLoop, calls=%fused_computation | loop fusion | flops 29360128 | bytes 44040192 | tf_op jit(solution)/shard_map/convert_element_type | solution.py:110
  352.0 0.0 collective-permute-done.3
  352.0 40.0 %collective-permute-done.4 = bf16[768,1792]{1,0:T(8,128)(2,1)} collective-permute-done((bf16[768,1792]{1,0:T(8,128)(2,1)S(1)}, bf16[768,1792]{1,0:T(8,128)(2,1)}, u32[]{:S(2)}, u32[]{:S(2)}) %collective-permute-start.4) | collective-permute-done | bytes 2752544 | tf_op jit(solution)/shard_map/ppermute | solution.py:15
  392.0 0.0 copy-start.1
  392.0 14.6 %fusion.15 = (bf16[1,768,3584]{2,1,0:T(8,128)(2,1)}, bf16[1,768,3584]{2,1,0:T(8,128)(2,1)}, f32[768]{0:T(1024)S(1)}) fusion(f32[768]{0:T(1024)S(1)} %convert_element_type.95, bf16[1,768,3584]{2,1,0:T(8,128)(2,1)S(1)} %bitcast.62, f32[768,3584]{1,0:T(8,128)} %fusion, bf16[768,1792]{1,0:T(8,128)(2,1)} %collective-permute-done.4, ...), kind=kLoop, calls=%fused_computation.26 | loop fusion | flops 66059520 | bytes 44046336 | tf_op jit(solution)/shard_map/broadcast_in_dim | solution.py:139
  406.6 0.1 all_to_all.29
  406.7 8.6 %psum.7 = f32[4,1,192]{2,1,0:T(1,128)S(1)} all-reduce(f32[4,1,192]{2,1,0:T(1,128)S(1)} %all_to_all.29), channel_id=1, replica_groups=mesh['dp'=2,'expert'=4,'tensor'=4] {'tensor'}, use_global_device_ids=true, to_apply=%region_5.6 | all-reduce | flops 768 | bytes 6144 | tf_op jit(solution)/shard_map/psum | solution.py:123
  415.3 6.6 %all_to_all.37 = f32[4,1,192]{2,1,0:T(1,128)S(1)} all-to-all(f32[4,1,192]{2,1,0:T(1,128)S(1)} %psum.7), channel_id=1, replica_groups=mesh['dp'=2,'expert'=4,'tensor'=4] {'expert'}, dimensions={0} | all-to-all | bytes 6144 | tf_op jit(solution)/shard_map/all_to_all | solution.py:124
  421.9 0.1 broadcast_in_dim.76
  421.9 0.3 select_reduce_fusion.1
  422.3 0.6 pad_maximum_fusion
  (32 shorter events, 0.1 us)
Async XLA Ops:
  7.2 4.6 %copy-start = (bf16[256,1024]{1,0:T(8,128)(2,1)S(1)}, bf16[256,1024]{1,0:T(8,128)(2,1)}, u32[]{:S(2)}) copy-start(bf16[256,1024]{1,0:T(8,128)(2,1)} %param.6) | copy-start | bytes 1572868
  14.0 9.0 %copy-start.3 = (bf16[768,1024]{1,0:T(8,128)(2,1)S(1)}, bf16[768,1024]{1,0:T(8,128)(2,1)}, u32[]{:S(2)}) copy-start(bf16[768,1024]{1,0:T(8,128)(2,1)} %convolution_convert_fusion.2) | copy-start | bytes 4718596
  47.1 49.4 %copy-start.2 = (bf16[4,192,1024]{2,1,0:T(8,128)(2,1)}, bf16[4,192,1024]{2,1,0:T(8,128)(2,1)S(1)}, u32[]{:S(2)}) copy-start(bf16[4,192,1024]{2,1,0:T(8,128)(2,1)S(1)} %all_to_all.35) | copy-start | bytes 4718596
  52.3 41.6 %all-to-all-start.2 = ((bf16[768,4,256]{2,0,1:T(8,128)(2,1)}), bf16[768,4,256]{2,0,1:T(8,128)(2,1)}, u32[]{:S(2)}, u32[]{:S(2)}) async-start(bf16[768,4,256]{2,0,1:T(8,128)(2,1)} %copy.40), calls=%async_computation.2 | async-start | bytes 3145728 | tf_op jit(solution)/shard_map/all_to_all | solution.py:68
  57.2 121.8 %all-gather.3.cloned.1.call-start = ((), (), s32[]{:S(2)}) async-start(), calls=%async_computation.4 | async-start | bytes 3932160 | tf_op jit(solution)/shard_map/all_gather | solution.py:75
  97.6 18.6 %collective-permute-start = (bf16[768,512]{0,1:T(8,128)(2,1)S(1)}, bf16[768,512]{0,1:T(8,128)(2,1)S(1)}, u32[]{:S(2)}, u32[]{:S(2)}) collective-permute-start(bf16[768,512]{0,1:T(8,128)(2,1)S(1)} %constant_dynamic-slice_fusion), channel_id=1, source_target_pairs={{0,16},{16,0},{1,17},{17,1},{2,18},{18,2},{3,19},{19,3},{4,20},{20... | collective-permute-start | bytes 2359304 | tf_op jit(solution)/shard_map/ppermute | solution.py:15
  105.4 10.8 %collective-permute-start.1 = (bf16[768]{0:T(1024)(128)(2,1)S(1)}, bf16[768]{0:T(1024)(128)(2,1)S(1)}, u32[]{:S(2)}, u32[]{:S(2)}) collective-permute-start(bf16[768]{0:T(1024)(128)(2,1)S(1)} %reshape.65), channel_id=1, source_target_pairs={{0,16},{16,0},{1,17},{17,1},{2,18},{18,2},{3,19},{19,3},{4,20},{20... | collective-permute-start | bytes 4616 | tf_op jit(solution)/shard_map/ppermute | solution.py:15
  116.3 0.9 copy-start.4
  117.2 177.4 %all-gather.5.cloned.1.call-start = ((), (), s32[]{:S(2)}) async-start(), calls=%async_computation.5 | async-start | bytes 7864320 | tf_op jit(solution)/shard_map/all_gather | solution.py:77
  117.4 119.1 %collective-permute-start.2 = (bf16[768,3584]{1,0:T(8,128)(2,1)}, bf16[768,3584]{1,0:T(8,128)(2,1)}, u32[]{:S(2)}, u32[]{:S(2)}) collective-permute-start(bf16[768,3584]{1,0:T(8,128)(2,1)} %fusion.4), channel_id=1, source_target_pairs={{0,16},{16,0},{1,17},{17,1},{2,18},{18,2},{3,19},{19,3},{4,20},{20... | collective-permute-start | bytes 16515080 | tf_op jit(solution)/shard_map/ppermute | solution.py:15
  261.6 90.4 %collective-permute-start.3 = (bf16[768,1792]{1,0:T(8,128)(2,1)}, bf16[768,1792]{1,0:T(8,128)(2,1)}, u32[]{:S(2)}, u32[]{:S(2)}) collective-permute-start(bf16[768,1792]{1,0:T(8,128)(2,1)} %get-tuple-element.44), channel_id=1, source_target_pairs={{0,16},{16,0},{1,17},{17,1},{2,18},{18,2},{3,19},{19,3},{4,20},{20... | collective-permute-start | bytes 8257544 | tf_op jit(solution)/shard_map/ppermute | solution.py:15
  294.5 18.3 %copy-start.5 = (bf16[768,4096]{1,0:T(8,128)(2,1)S(1)}, bf16[768,4096]{1,0:T(8,128)(2,1)}, u32[]{:S(2)}) copy-start(bf16[768,4096]{1,0:T(8,128)(2,1)} %all-gather.5.cloned.1.call-done) | copy-start | bytes 18874372
  330.1 61.8 %slice-start = ((s8[5505024]{0:T(1024)(128)(4,1)}), s8[4194304]{0:T(1024)(128)(4,1)S(1)}, s32[]{:S(2)}) async-start(s8[5505024]{0:T(1024)(128)(4,1)} %bitcast.61), calls=%async_computation.6 | async-start | bytes 8388608
  330.1 61.8 %slice-start.2 = ((s8[5505024]{0:T(1024)(128)(4,1)}), s8[4194304]{0:T(1024)(128)(4,1)S(1)}, s32[]{:S(2)}) async-start(s8[5505024]{0:T(1024)(128)(4,1)} %bitcast.63), calls=%async_computation.8 | async-start | bytes 8388608
  330.1 61.8 %slice-start.4 = ((s8[5505024]{0:T(1024)(128)(4,1)}), s8[4194304]{0:T(1024)(128)(4,1)S(1)}, s32[]{:S(2)}) async-start(s8[5505024]{0:T(1024)(128)(4,1)} %bitcast.65), calls=%async_computation.10 | async-start | bytes 8388608
  330.1 61.9 %slice-start.1 = ((s8[5505024]{0:T(1024)(128)(4,1)}), s8[1310720]{0:T(1024)(128)(4,1)S(1)}, s32[]{:S(2)}) async-start(s8[5505024]{0:T(1024)(128)(4,1)} %bitcast.61), calls=%async_computation.7 | async-start | bytes 2621440
  330.1 61.9 %slice-start.3 = ((s8[5505024]{0:T(1024)(128)(4,1)}), s8[1310720]{0:T(1024)(128)(4,1)S(1)}, s32[]{:S(2)}) async-start(s8[5505024]{0:T(1024)(128)(4,1)} %bitcast.63), calls=%async_computation.9 | async-start | bytes 2621440
  330.1 61.9 %slice-start.5 = ((s8[5505024]{0:T(1024)(128)(4,1)}), s8[1310720]{0:T(1024)(128)(4,1)S(1)}, s32[]{:S(2)}) async-start(s8[5505024]{0:T(1024)(128)(4,1)} %bitcast.65), calls=%async_computation.11 | async-start | bytes 2621440
  330.1 61.8 %collective-permute-start.4 = (bf16[768,1792]{1,0:T(8,128)(2,1)S(1)}, bf16[768,1792]{1,0:T(8,128)(2,1)}, u32[]{:S(2)}, u32[]{:S(2)}) collective-permute-start(bf16[768,1792]{1,0:T(8,128)(2,1)S(1)} %get-tuple-element.29), channel_id=1, source_target_pairs={{0,16},{16,0},{1,17},{17,1},{2,18},{18,2},{3,19},{19,3},{4,20},{20... | collective-permute-start | bytes 8257544 | tf_op jit(solution)/shard_map/ppermute | solution.py:15
  392.0 30.9 %copy-start.1 = (bf16[256,1024]{1,0:T(8,128)(2,1)S(1)}, bf16[256,1024]{1,0:T(8,128)(2,1)}, u32[]{:S(2)}) copy-start(bf16[256,1024]{1,0:T(8,128)(2,1)} %param.6) | copy-start | bytes 1572868
Sparse Core Ops, SparseCore 0:
  117.3 61.6 all-gather.2
  180.5 113.9 all-gather.4

commit v10 on v5

--- a/solution.py
+++ b/solution.py
@@ -41,7 +41,7 @@
 
     local_weight = down_weight[0]
     units = local_weight.shape[0]
-    moved = units // 4 // 16 * 16
+    moved = units * 2 // 7 // 128 * 128
 
     gate_float = gate_preact[0].astype(jnp.float32)
     up_float = up_preact[0].astype(jnp.float32)

time: 402 us -> 407 us (1.012)
  transfers between devices with their start and end apart: 7 -> 7, of which waited for: 4 -> 5; matrix products, arithmetic and copies ran while one was open for 24% -> 24% of each run, Pallas kernels for 0% -> 0%
where the time goes in v10:
time: 407 us; the launch traced here: 406 us
  waiting for transfers between devices  205 us (50%)
  matrix products  72.3 us (18%)
  blocking collectives  48.6 us (12%)
  other arithmetic  46.6 us (11%)
  between operations  14.2 us (3%)
  local copies, waits for them, and re-layouts  12.8 us (3%)
  starting transfers between devices  6.91 us (2%)
    ppermute x5, waiting for transfers between devices, swap_dp(): return lax.ppermute(value, 'dp', perm=[(0, 1), (1, 0)])  146 us
    all_gather x1, waiting for transfers between devices, local(): other_rows = lax.all_gather(other_piece, 'tensor', axis=1, tiled=True)  59 us
    all_to_all x1, blocking collectives, local(): lax.all_to_all(outgoing, 'expert', split_axis=0, concat_axis=0, tiled=True)  24.2 us
    dot_general x1, matrix products, local(): lax.dot_general(hidden_other, scaled_other, contract_rows, preferred_elem...  17.8 us
    dot_general x1, matrix products, local(): lax.dot_general(own_rows, local_weight, contract_cols, preferred_element_...  17.3 us
    broadcast_in_dim x1, other arithmetic, local(): return (gate_grad[None], up_grad[None], down_grad[None], router_grad)  16.9 us
    convert_element_type x1, other arithmetic, local(): (rounded_own.astype(jnp.float32) + rounded_other.astype(jnp.float32)).ast...  15.6 us
    dot_general x1, matrix products, local(): lax.dot_general(hidden, scaled_own, contract_rows, preferred_element_type...  14.6 us
  transfers between devices with their start and end apart: 7, of which 5 were waited for; matrix products, arithmetic and copies ran while one was open for 24% of the time, Pallas kernels for 0%

profile of v10, /device:TPU:0, one launch (start us, length us, event | category | flops | bytes accessed | tf_op | source)
XLA Modules:
  0.0 406.4 jit_solution(2660223754882530097)
XLA Ops:
  7.2 0.0 copy-start
  7.2 0.0 all-gather.3.cloned.1.call-start
  7.2 0.9 copy.32
  8.1 0.1 eq.59
  8.2 0.1 eq.55
  8.4 1.2 reduce-window.6
  9.6 0.2 slice_reduce_fusion
  9.8 0.2 reduce-window.9
  10.0 0.1 add_bitcast_fusion
  10.1 0.1 reduce_sum.48
  10.3 0.1 copy.34
  10.3 0.7 multiply_add_fusion
  11.1 0.8 slice_convert_fusion.1
  11.8 0.2 select_reduce_fusion.2
  12.0 0.1 convert_element_type.95
  12.1 0.0 copy-done
  12.1 0.8 convolution_convert_fusion.2
  12.9 8.9 %fusion.2 = bf16[768,3584]{1,0:T(8,128)(2,1)} fusion(bf16[1,768,3584]{2,1,0:T(8,128)(2,1)} %param.10, bf16[1,768,3584]{2,1,0:T(8,128)(2,1)} %param.9), kind=kLoop, calls=%fused_computation.10 | loop fusion | flops 22020096 | bytes 16515072 | tf_op jit(solution)/shard_map/convert_element_type | solution.py:49
  21.7 24.2 %all_to_all.23 = bf16[4,192,1024]{2,1,0:T(8,128)(2,1)} all-to-all(bf16[4,192,1024]{2,1,0:T(8,128)(2,1)S(1)} %bitcast.71), channel_id=1, replica_groups=mesh['dp'=2,'expert'=4,'tensor'=4] {'expert'}, dimensions={0} | all-to-all | bytes 3145728 | tf_op jit(solution)/shard_map/all_to_all | solution.py:60
  46.0 0.0 all-gather.3.cloned.1.call-update
  46.0 0.0 all-gather.5.cloned.1.call-start
  46.0 2.1 collective-permute-start
  48.1 6.1 %all_to_all.24 = bf16[4,1,192]{2,1,0:T(2,128)(2,1)S(1)} all-to-all(bf16[4,1,192]{2,1,0:T(2,128)(2,1)S(1)} %copy.35), channel_id=1, replica_groups=mesh['dp'=2,'expert'=4,'tensor'=4] {'expert'}, dimensions={0} | all-to-all | bytes 3072 | tf_op jit(solution)/shard_map/all_to_all | solution.py:59
  54.3 0.1 reshape.64
  54.3 0.0 collective-permute-start.1
  54.4 112.4 %collective-permute-done.1 = bf16[768]{0:T(1024)(128)(2,1)S(1)} collective-permute-done((bf16[768]{0:T(1024)(128)(2,1)S(1)}, bf16[768]{0:T(1024)(128)(2,1)S(1)}, u32[]{:S(2)}, u32[]{:S(2)}) %collective-permute-start.1) | collective-permute-done | bytes 1568 | tf_op jit(solution)/shard_map/ppermute | solution.py:15
  166.7 0.0 collective-permute-done
  166.7 0.0 all-gather.3.cloned.1.call-done
  166.7 1.2 constant_dynamic-slice_fusion.1
  167.9 1.8 collective-permute-start.2
  169.7 4.8 %slice_bitcast_fusion = bf16[1024,2048]{1,0:T(8,128)(2,1)} fusion(bf16[1,3584,2048]{2,1,0:T(8,128)(2,1)} %param.11), kind=kLoop, calls=%fused_computation.29 | loop fusion | bytes 8388608 | tf_op jit(solution)/shard_map/slice | solution.py:79
  174.5 11.8 %collective-permute-done.2 = bf16[768,512]{1,0:T(8,128)(2,1)S(1)} collective-permute-done((bf16[768,512]{1,0:T(8,128)(2,1)S(1)}, bf16[768,512]{1,0:T(8,128)(2,1)S(1)}, u32[]{:S(2)}, u32[]{:S(2)}) %collective-permute-start.2) | collective-permute-done | bytes 786464 | tf_op jit(solution)/shard_map/ppermute | solution.py:15
  186.3 0.9 copy-done.4
  187.2 0.0 all-gather.5.cloned.1.call-update
  187.2 1.5 collective-permute-start.3
  188.7 4.0 constant_dynamic-slice_fusion
  192.8 59.0 %all-gather.5.cloned.1.call-done = bf16[768,2048]{1,0:T(8,128)(2,1)} async-done(((bf16[768,512]{1,0:T(8,128)(2,1)}), bf16[768,2048]{1,0:T(8,128)(2,1)}) %all-gather.5.cloned.1.call-update) | async-done | bytes 3145744 | tf_op jit(solution)/shard_map/all_gather | solution.py:81
  251.8 0.0 slice-start.2
  251.8 13.4 %fusion.15 = bf16[768,2560]{1,0:T(8,128)(2,1)} fusion(bf16[768,2048]{1,0:T(8,128)(2,1)} %all-gather.5.cloned.1.call-done, bf16[1,3584,2048]{2,1,0:T(8,128)(2,1)} %param.11), kind=kOutput, calls=%fused_computation.28 | convolution fusion | flops 8055029760 | bytes 17563648 | tf_op jit(solution)/shard_map/dot_general | solution.py:85
  265.2 0.0 slice-start.3
  265.2 12.8 %collective-permute-done.3 = bf16[1024,2048]{1,0:T(8,128)(2,1)} collective-permute-done((bf16[1024,2048]{1,0:T(8,128)(2,1)}, bf16[1024,2048]{1,0:T(8,128)(2,1)}, u32[]{:S(2)}, u32[]{:S(2)}) %collective-permute-start.3) | collective-permute-done | bytes 4194336 | tf_op jit(solution)/shard_map/ppermute | solution.py:15
  278.0 1.4 collective-permute-start.4
  279.5 17.8 %convolution_convert_fusion = bf16[3584,2048]{1,0:T(8,128)(2,1)} fusion(bf16[768,3584]{1,0:T(8,128)(2,1)} %collective-permute-done, bf16[768,2048]{1,0:T(8,128)(2,1)} %all-gather.5.cloned.1.call-done, f32[768]{0:T(1024)S(1)} %convert_element_type.103), kind=kOutput, calls=%fused_computation.4 | convolution fusion | flops 11286347776 | bytes 23333888 | tf_op jit(solution)/shard_map/dot_general | solution.py:101
  297.3 0.0 slice-done.2
  297.3 0.0 slice-done.3
  297.3 0.0 copy-done.3
  297.3 14.6 %convolution_convert_fusion.1 = bf16[3584,2048]{1,0:T(8,128)(2,1)} fusion(bf16[768,3584]{1,0:T(8,128)(2,1)S(1)} %bitcast.68, bf16[768,2048]{1,0:T(8,128)(2,1)S(1)} %copy-done.3, f32[768]{0:T(1024)S(1)} %convert_element_type.96), kind=kOutput, calls=%fused_computation.5 | convolution fusion | flops 11286347776 | bytes 23333888 | tf_op jit(solution)/shard_map/dot_general | solution.py:100
  311.9 17.3 %fusion = f32[768,3584]{1,0:T(8,128)} fusion(bf16[768,2048]{1,0:T(8,128)(2,1)S(1)} %copy-done.3, bf16[1,3584,2048]{2,1,0:T(8,128)(2,1)} %param.11), kind=kOutput, calls=%fused_computation.6 | convolution fusion | flops 11274289152 | bytes 28835840 | tf_op jit(solution)/shard_map/dot_general | solution.py:92
  329.2 8.4 %fusion.20 = f32[768,1024]{1,0:T(8,128)} fusion(bf16[1024,2048]{1,0:T(8,128)(2,1)} %collective-permute-done.3, bf16[768,4096]{1,0:T(8,128)(2,1)} %all-gather.3.cloned.1.call-done, s32[]{:T(128)S(6)} %select_n.36), kind=kOutput, calls=%fused_computation.32 | convolution fusion | flops 3221225472 | bytes 10485764 | tf_op jit(solution)/shard_map/dot_general | solution.py:96
  337.6 0.0 copy-done.2
  337.6 15.6 %add_convert_fusion = bf16[3584,2048]{1,0:T(8,128)(2,1)} fusion(bf16[3584,2048]{1,0:T(8,128)(2,1)S(1)} %copy-done.2, bf16[3584,2048]{1,0:T(8,128)(2,1)} %convolution_convert_fusion.1), kind=kLoop, calls=%fused_computation | loop fusion | flops 29360128 | bytes 44040192 | tf_op jit(solution)/shard_map/convert_element_type | solution.py:106
  353.2 9.0 %collective-permute-done.4 = bf16[768,2560]{1,0:T(8,128)(2,1)S(1)} collective-permute-done((bf16[768,2560]{1,0:T(8,128)(2,1)}, bf16[768,2560]{1,0:T(8,128)(2,1)S(1)}, u32[]{:S(2)}, u32[]{:S(2)}) %collective-permute-start.4) | collective-permute-done | bytes 3932192 | tf_op jit(solution)/shard_map/ppermute | solution.py:15
  362.2 1.1 convert_element_type.98
  363.3 0.0 slice-done
  363.3 0.0 slice-done.1
  363.3 0.0 copy-start.1
  363.3 16.9 %fusion.13 = (bf16[1,768,3584]{2,1,0:T(8,128)(2,1)}, bf16[1,768,3584]{2,1,0:T(8,128)(2,1)}, f32[768]{0:T(1024)S(1)}) fusion(f32[768]{0:T(1024)S(1)} %convert_element_type.96, bf16[1,768,3584]{2,1,0:T(8,128)(2,1)S(1)} %bitcast.66, f32[768,3584]{1,0:T(8,128)} %fusion, f32[768,2560]{1,0:T(8,128)S(1)} %convert_element_type.98, f32[768,1024]{1,0:T(8,128)} %fusion.20, ...), kind=kLoop, calls=%fused_computation.26 | loop fusion | flops 57801984 | bytes 49551360 | tf_op jit(solution)/shard_map/broadcast_in_dim | solution.py:134
  380.2 0.1 all_to_all.18
  380.3 11.6 %psum.7 = f32[4,1,192]{2,1,0:T(1,128)S(1)} all-reduce(f32[4,1,192]{2,1,0:T(1,128)S(1)} %all_to_all.18), channel_id=1, replica_groups=mesh['dp'=2,'expert'=4,'tensor'=4] {'tensor'}, use_global_device_ids=true, to_apply=%region_5.6 | all-reduce | flops 768 | bytes 6144 | tf_op jit(solution)/shard_map/psum | solution.py:118
  391.8 6.7 %all_to_all.25 = f32[4,1,192]{2,1,0:T(1,128)S(1)} all-to-all(f32[4,1,192]{2,1,0:T(1,128)S(1)} %psum.7), channel_id=1, replica_groups=mesh['dp'=2,'expert'=4,'tensor'=4] {'expert'}, dimensions={0} | all-to-all | bytes 6144 | tf_op jit(solution)/shard_map/all_to_all | solution.py:119
  398.6 0.1 broadcast_in_dim.76
  398.7 0.3 select_reduce_fusion.1
  399.0 0.6 pad_maximum_fusion
  399.6 0.0 copy-done.1
  (15 shorter events, 0.1 us)
Async XLA Ops:
  7.2 5.0 %copy-start = (bf16[256,1024]{1,0:T(8,128)(2,1)S(1)}, bf16[256,1024]{1,0:T(8,128)(2,1)}, u32[]{:S(2)}) copy-start(bf16[256,1024]{1,0:T(8,128)(2,1)} %param.6) | copy-start | bytes 1572868
  7.2 159.6 %all-gather.3.cloned.1.call-start = ((), (), s32[]{:S(2)}) async-start(), calls=%async_computation.3 | async-start | bytes 7864320 | tf_op jit(solution)/shard_map/all_gather | solution.py:66
  46.0 205.8 %all-gather.5.cloned.1.call-start = ((), (), s32[]{:S(2)}) async-start(), calls=%async_computation.4 | async-start | bytes 3932160 | tf_op jit(solution)/shard_map/all_gather | solution.py:81
  46.0 120.7 %collective-permute-start = (bf16[768,3584]{1,0:T(8,128)(2,1)}, bf16[768,3584]{1,0:T(8,128)(2,1)}, u32[]{:S(2)}, u32[]{:S(2)}) collective-permute-start(bf16[768,3584]{1,0:T(8,128)(2,1)} %fusion.2), channel_id=1, source_target_pairs={{0,16},{16,0},{1,17},{17,1},{2,18},{18,2},{3,19},{19,3},{4,20},{20... | collective-permute-start | bytes 16515080 | tf_op jit(solution)/shard_map/ppermute | solution.py:15
  54.3 112.4 %collective-permute-start.1 = (bf16[768]{0:T(1024)(128)(2,1)S(1)}, bf16[768]{0:T(1024)(128)(2,1)S(1)}, u32[]{:S(2)}, u32[]{:S(2)}) collective-permute-start(bf16[768]{0:T(1024)(128)(2,1)S(1)} %reshape.64), channel_id=1, source_target_pairs={{0,16},{16,0},{1,17},{17,1},{2,18},{18,2},{3,19},{19,3},{4,20},{20... | collective-permute-start | bytes 4616 | tf_op jit(solution)/shard_map/ppermute | solution.py:15
  167.9 18.4 %collective-permute-start.2 = (bf16[768,512]{1,0:T(8,128)(2,1)S(1)}, bf16[768,512]{1,0:T(8,128)(2,1)S(1)}, u32[]{:S(2)}, u32[]{:S(2)}) collective-permute-start(bf16[768,512]{1,0:T(8,128)(2,1)S(1)} %constant_dynamic-slice_fusion.1), channel_id=1, source_target_pairs={{0,16},{16,0},{1,17},{17,1},{2,18},{18,2},{3,19},{19,3},{4,20},{20... | collective-permute-start | bytes 2359304 | tf_op jit(solution)/shard_map/ppermute | solution.py:15
  186.3 0.9 copy-start.4
  187.2 90.8 %collective-permute-start.3 = (bf16[1024,2048]{1,0:T(8,128)(2,1)}, bf16[1024,2048]{1,0:T(8,128)(2,1)}, u32[]{:S(2)}, u32[]{:S(2)}) collective-permute-start(bf16[1024,2048]{1,0:T(8,128)(2,1)} %slice_bitcast_fusion), channel_id=1, source_target_pairs={{0,16},{16,0},{1,17},{17,1},{2,18},{18,2},{3,19},{19,3},{4,20},{20... | collective-permute-start | bytes 12582920 | tf_op jit(solution)/shard_map/ppermute | solution.py:15
  251.8 45.5 %slice-start.2 = ((s8[5505024]{0:T(1024)(128)(4,1)}), s8[4194304]{0:T(1024)(128)(4,1)S(1)}, s32[]{:S(2)}) async-start(s8[5505024]{0:T(1024)(128)(4,1)} %bitcast.67), calls=%async_computation.7 | async-start | bytes 8388608
  265.2 32.1 %slice-start.3 = ((s8[5505024]{0:T(1024)(128)(4,1)}), s8[1310720]{0:T(1024)(128)(4,1)S(1)}, s32[]{:S(2)}) async-start(s8[5505024]{0:T(1024)(128)(4,1)} %bitcast.67), calls=%async_computation.8 | async-start | bytes 2621440
  265.2 32.1 %copy-start.3 = (bf16[768,2048]{1,0:T(8,128)(2,1)S(1)}, bf16[768,2048]{1,0:T(8,128)(2,1)}, u32[]{:S(2)}) copy-start(bf16[768,2048]{1,0:T(8,128)(2,1)} %constant_dynamic-slice_fusion) | copy-start | bytes 9437188
  278.0 84.2 %collective-permute-start.4 = (bf16[768,2560]{1,0:T(8,128)(2,1)}, bf16[768,2560]{1,0:T(8,128)(2,1)S(1)}, u32[]{:S(2)}, u32[]{:S(2)}) collective-permute-start(bf16[768,2560]{1,0:T(8,128)(2,1)} %fusion.15), channel_id=1, source_target_pairs={{0,16},{16,0},{1,17},{17,1},{2,18},{18,2},{3,19},{19,3},{4,20},{20... | collective-permute-start | bytes 11796488 | tf_op jit(solution)/shard_map/ppermute | solution.py:15
  329.2 8.4 %copy-start.2 = (bf16[3584,2048]{1,0:T(8,128)(2,1)S(1)}, bf16[3584,2048]{1,0:T(8,128)(2,1)}, u32[]{:S(2)}) copy-start(bf16[3584,2048]{1,0:T(8,128)(2,1)} %convolution_convert_fusion) | copy-start | bytes 44040196
  329.2 34.1 %slice-start = ((s8[5505024]{0:T(1024)(128)(4,1)}), s8[4194304]{0:T(1024)(128)(4,1)S(1)}, s32[]{:S(2)}) async-start(s8[5505024]{0:T(1024)(128)(4,1)} %bitcast.65), calls=%async_computation.5 | async-start | bytes 8388608
  337.6 25.7 %slice-start.1 = ((s8[5505024]{0:T(1024)(128)(4,1)}), s8[1310720]{0:T(1024)(128)(4,1)S(1)}, s32[]{:S(2)}) async-start(s8[5505024]{0:T(1024)(128)(4,1)} %bitcast.65), calls=%async_computation.6 | async-start | bytes 2621440
  363.3 36.3 %copy-start.1 = (bf16[256,1024]{1,0:T(8,128)(2,1)S(1)}, bf16[256,1024]{1,0:T(8,128)(2,1)}, u32[]{:S(2)}) copy-start(bf16[256,1024]{1,0:T(8,128)(2,1)} %param.6) | copy-start | bytes 1572868
Sparse Core Ops, SparseCore 0:
  46.1 116.1 all-gather.2
  187.3 64.3 all-gather.4
